TPU v7x, 128 devices: a whole 4x4x4 slice. The times are simulated.
128 devices in a mesh: group: 8 (over y, z_hi), blk: 16 (over x, z_lo, core).
Axes of the slice: x: 4, y: 4, z: 4 (z_hi: 2, z_lo: 2; z = z_hi * 2 + z_lo), core: 2. Of those that a mesh axis runs over, the one named last changes fastest.
Arguments:
- embeddings: float32 [73728, 1024], P(('group', 'blk')), may hold values from -100 to 100
- cluster: int32 [73728], P(('group', 'blk')), may hold values from 0 to 63, as said below
- global_index: int32 [73728], P(('group', 'blk')), may hold values from 0 to 73727, each once
- send_counts: int32 [128, 8], P(('group', 'blk')), may hold values from 1 to 108, as said below
Outputs:
- best_cosine: float32 [73728], P(('group', 'blk'))
Inputs may be any that keep to these rules, and one draw needn't show every extreme that they name: The row's cluster group is given by send_counts; of the rows that one device sends to one cluster group, at most 7 have a cluster number in any one block c // 4 of consecutive cluster numbers, and every device has exactly 7 in some block. `global_index`: each number once over all devices. The 8 counts of a device sum to 576; its rows stand in order of cluster group, send_counts[d,g] of them for group g; every device has a count of exactly 108.
All inputs are finite; a program needn't handle non-finite values.
Results may differ from a plain program's by a relative error of at most 0.0003.
Values may be sent and summed in bfloat16 or wider, within the bound.
No kernel may reach another device: no remote copies, remote signals or barrier semaphores. Data moves between devices by JAX's collectives and lax.ppermute only.
A program may use at most 128 MiB of HBM per device.

v0:
```python
import jax
import jax.numpy as jnp
from jax import lax
from jax.sharding import PartitionSpec as P


def passed_along(x, axis, by):
    count = lax.axis_size(axis)
    return lax.ppermute(x, axis, [(i, (i + by) % count) for i in range(count)])


def compare(best_now, q_rows, q_label, q_ids, key_rows, key_label, key_ids):
    cosine = lax.dot_general(
        q_rows, key_rows, (((1,), (1,)), ((), ())), preferred_element_type=jnp.float32
    )
    usable = (q_label[:, None] == key_label[None, :]) & (key_ids[None, :] < q_ids[:, None])
    return jnp.maximum(best_now, jnp.max(jnp.where(usable, cosine, jnp.float32(-1.0)), axis=1))


def on_device(embeddings, cluster, global_index, send_counts):
    row_count = embeddings.shape[0]
    feat_width = embeddings.shape[1]
    groups = lax.axis_size("group")
    blocks = lax.axis_size("blk")
    capacity = 3 * row_count // (2 * groups)
    slots = groups * capacity
    counts = send_counts[0]
    cum_ends = jnp.cumsum(counts)
    starts = cum_ends - counts
    squares = jnp.sum(embeddings * embeddings, axis=1, keepdims=True)
    unit_rows = (embeddings * lax.rsqrt(squares + 1e-06)).astype(jnp.bfloat16)
    slot_index = jnp.arange(capacity, dtype=jnp.int32)
    source = jnp.clip(starts[:, None] + slot_index[None, :], 0, row_count - 1)
    is_valid = slot_index[None, :] < counts[:, None]
    send_rows = jnp.take(unit_rows, source.reshape(-1), axis=0).reshape(
        groups, capacity, feat_width
    )
    send_label = jnp.where(is_valid, cluster[source], -1)
    send_ids = global_index[source]
    got_rows, got_label, got_ids = (
        lax.all_to_all(send_rows, "group", split_axis=0, concat_axis=0, tiled=True),
        lax.all_to_all(send_label, "group", split_axis=0, concat_axis=0, tiled=True),
        lax.all_to_all(send_ids, "group", split_axis=0, concat_axis=0, tiled=True),
    )
    q_rows = got_rows.reshape(slots, feat_width)
    q_label = got_label.reshape(slots)
    q_ids = got_ids.reshape(slots)
    best_cos = jnp.full((slots,), -1.0, jnp.float32)
    best_cos = compare(best_cos, q_rows, q_label, q_ids, q_rows, q_label, q_ids)

    def turn_cycle(turn_index, state_now):
        moving, best_now = state_now
        moving = passed_along((moving[0], moving[1], moving[2]), "blk", 1)
        return (moving, compare(best_now, q_rows, q_label, q_ids, moving[0], moving[1], moving[2]))

    moving, best_cos = lax.fori_loop(
        0, blocks - 1, turn_cycle, ((q_rows, q_label, q_ids), best_cos)
    )
    returned = lax.all_to_all(
        best_cos.reshape(groups, capacity), "group", split_axis=0, concat_axis=0, tiled=True
    )
    position = jnp.arange(row_count, dtype=jnp.int32)
    owner_group = jnp.sum((position[:, None] >= cum_ends[None, :]).astype(jnp.int32), axis=1)
    flat_index = owner_group * capacity + position - starts[owner_group]
    return returned.reshape(-1)[flat_index]


def solution(mesh):
    placed = (
        P(("group", "blk"), None),
        P(("group", "blk")),
        P(("group", "blk")),
        P(("group", "blk"), None),
    )
    return jax.shard_map(
        on_device, mesh=mesh, in_specs=placed, out_specs=P(("group", "blk")), check_vma=False
    )
```

profile of v0, /device:TPU:0, one launch (start us, length us, event | category | flops | bytes accessed | tf_op | source)
XLA Modules:
  0.0 536.1 jit_solution(7701567560229174602)
XLA Ops:
  2.2 3.7 gather_fusion.1
  6.6 7.9 %all-to-all-start.1 = ((s32[8,1,108]{2,1,0:T(1,128)}), s32[8,1,108]{2,1,0:T(1,128)S(1)}, u32[]{:S(2)}, u32[]{:S(2)}) async-start(s32[8,1,108]{2,1,0:T(1,128)} %compare_select_fusion.1), calls=%async_computation.1 | async-start | bytes 8192 | tf_op jit(solution)/shard_map/all_to_all | solution.py:42
  15.8 4.2 gather_fusion
  21.7 3.7 gather_fusion.2
  26.0 7.2 %all-to-all-start.2 = ((s32[8,1,108]{2,1,0:T(1,128)}), s32[8,1,108]{2,1,0:T(1,128)S(1)}, u32[]{:S(2)}, u32[]{:S(2)}) async-start(s32[8,1,108]{2,1,0:T(1,128)} %all_to_all.25), calls=%async_computation.2 | async-start | bytes 8192 | tf_op jit(solution)/shard_map/all_to_all | solution.py:43
  34.7 6.2 %all-to-all-done.2 = s32[8,1,108]{2,1,0:T(1,128)S(1)} async-done(((s32[8,1,108]{2,1,0:T(1,128)}), s32[8,1,108]{2,1,0:T(1,128)S(1)}, u32[]{:S(2)}, u32[]{:S(2)}) %all-to-all-start.2) | async-done | bytes 3488 | tf_op jit(solution)/shard_map/all_to_all | solution.py:43
  40.9 3.6 all-to-all-start
  45.3 4.4 fusion.1
  55.5 13.3 %all-to-all-done = bf16[8,108,1024]{2,1,0:T(8,128)(2,1)S(1)} async-done(((bf16[8,108,1024]{2,1,0:T(8,128)(2,1)}), bf16[8,108,1024]{2,1,0:T(8,128)(2,1)S(1)}, u32[]{:S(2)}, u32[]{:S(2)}) %all-to-all-start) | async-done | bytes 1769504 | tf_op jit(solution)/shard_map/all_to_all | solution.py:41
  70.2 3.0 copy.6
  73.1 2.9 select_reduce_fusion.1
  76.0 443.0 %while.17 = (s32[]{:T(128)}, bf16[864,1024]{1,0:T(8,128)(2,1)}, s32[864]{0:T(1024)}, s32[864]{0:T(1024)}, f32[864]{0:T(1024)S(1)}, /*index=5*/s32[8,108]{1,0:T(8...) while((s32[]{:T(128)}, bf16[864,1024]{1,0:T(8,128)(2,1)}, ...), condition=%wide.wide.region_5.6_spmd, body=%wide.wide.region_3.5_spmd.sunk | while | flops 1532556288 | bytes 14225125 | solution.py:56
  77.3 23.1 %collective-permute-done.1 = s32[864]{0:T(1024)S(1)} collective-permute-done((s32[864]{0:T(1024)}, s32[864]{0:T(1024)S(1)}, u32[]{:S(2)}, u32[]{:S(2)}) %collective-permute-start.1) | collective-permute-done | bytes 3488 | tf_op jit(solution)/shard_map/while/body/eval_jaxpr/ppermute | solution.py:9
  105.6 24.3 %collective-permute-done.1 = s32[864]{0:T(1024)S(1)} collective-permute-done((s32[864]{0:T(1024)}, s32[864]{0:T(1024)S(1)}, u32[]{:S(2)}, u32[]{:S(2)}) %collective-permute-start.1) | collective-permute-done | bytes 3488 | tf_op jit(solution)/shard_map/while/body/eval_jaxpr/ppermute | solution.py:9
  135.2 24.3 %collective-permute-done.1 = s32[864]{0:T(1024)S(1)} collective-permute-done((s32[864]{0:T(1024)}, s32[864]{0:T(1024)S(1)}, u32[]{:S(2)}, u32[]{:S(2)}) %collective-permute-start.1) | collective-permute-done | bytes 3488 | tf_op jit(solution)/shard_map/while/body/eval_jaxpr/ppermute | solution.py:9
  164.7 24.3 %collective-permute-done.1 = s32[864]{0:T(1024)S(1)} collective-permute-done((s32[864]{0:T(1024)}, s32[864]{0:T(1024)S(1)}, u32[]{:S(2)}, u32[]{:S(2)}) %collective-permute-start.1) | collective-permute-done | bytes 3488 | tf_op jit(solution)/shard_map/while/body/eval_jaxpr/ppermute | solution.py:9
  194.2 24.3 %collective-permute-done.1 = s32[864]{0:T(1024)S(1)} collective-permute-done((s32[864]{0:T(1024)}, s32[864]{0:T(1024)S(1)}, u32[]{:S(2)}, u32[]{:S(2)}) %collective-permute-start.1) | collective-permute-done | bytes 3488 | tf_op jit(solution)/shard_map/while/body/eval_jaxpr/ppermute | solution.py:9
  219.7 2.8 select_reduce_fusion.4
  223.7 24.3 %collective-permute-done.1 = s32[864]{0:T(1024)S(1)} collective-permute-done((s32[864]{0:T(1024)}, s32[864]{0:T(1024)S(1)}, u32[]{:S(2)}, u32[]{:S(2)}) %collective-permute-start.1) | collective-permute-done | bytes 3488 | tf_op jit(solution)/shard_map/while/body/eval_jaxpr/ppermute | solution.py:9
  253.3 24.3 %collective-permute-done.1 = s32[864]{0:T(1024)S(1)} collective-permute-done((s32[864]{0:T(1024)}, s32[864]{0:T(1024)S(1)}, u32[]{:S(2)}, u32[]{:S(2)}) %collective-permute-start.1) | collective-permute-done | bytes 3488 | tf_op jit(solution)/shard_map/while/body/eval_jaxpr/ppermute | solution.py:9
  282.8 24.3 %collective-permute-done.1 = s32[864]{0:T(1024)S(1)} collective-permute-done((s32[864]{0:T(1024)}, s32[864]{0:T(1024)S(1)}, u32[]{:S(2)}, u32[]{:S(2)}) %collective-permute-start.1) | collective-permute-done | bytes 3488 | tf_op jit(solution)/shard_map/while/body/eval_jaxpr/ppermute | solution.py:9
  312.3 24.3 %collective-permute-done.1 = s32[864]{0:T(1024)S(1)} collective-permute-done((s32[864]{0:T(1024)}, s32[864]{0:T(1024)S(1)}, u32[]{:S(2)}, u32[]{:S(2)}) %collective-permute-start.1) | collective-permute-done | bytes 3488 | tf_op jit(solution)/shard_map/while/body/eval_jaxpr/ppermute | solution.py:9
  341.8 24.3 %collective-permute-done.1 = s32[864]{0:T(1024)S(1)} collective-permute-done((s32[864]{0:T(1024)}, s32[864]{0:T(1024)S(1)}, u32[]{:S(2)}, u32[]{:S(2)}) %collective-permute-start.1) | collective-permute-done | bytes 3488 | tf_op jit(solution)/shard_map/while/body/eval_jaxpr/ppermute | solution.py:9
  371.4 24.3 %collective-permute-done.1 = s32[864]{0:T(1024)S(1)} collective-permute-done((s32[864]{0:T(1024)}, s32[864]{0:T(1024)S(1)}, u32[]{:S(2)}, u32[]{:S(2)}) %collective-permute-start.1) | collective-permute-done | bytes 3488 | tf_op jit(solution)/shard_map/while/body/eval_jaxpr/ppermute | solution.py:9
  396.9 2.8 select_reduce_fusion.4
  400.9 24.3 %collective-permute-done.1 = s32[864]{0:T(1024)S(1)} collective-permute-done((s32[864]{0:T(1024)}, s32[864]{0:T(1024)S(1)}, u32[]{:S(2)}, u32[]{:S(2)}) %collective-permute-start.1) | collective-permute-done | bytes 3488 | tf_op jit(solution)/shard_map/while/body/eval_jaxpr/ppermute | solution.py:9
  430.4 24.3 %collective-permute-done.1 = s32[864]{0:T(1024)S(1)} collective-permute-done((s32[864]{0:T(1024)}, s32[864]{0:T(1024)S(1)}, u32[]{:S(2)}, u32[]{:S(2)}) %collective-permute-start.1) | collective-permute-done | bytes 3488 | tf_op jit(solution)/shard_map/while/body/eval_jaxpr/ppermute | solution.py:9
  459.9 24.3 %collective-permute-done.1 = s32[864]{0:T(1024)S(1)} collective-permute-done((s32[864]{0:T(1024)}, s32[864]{0:T(1024)S(1)}, u32[]{:S(2)}, u32[]{:S(2)}) %collective-permute-start.1) | collective-permute-done | bytes 3488 | tf_op jit(solution)/shard_map/while/body/eval_jaxpr/ppermute | solution.py:9
  489.5 24.3 %collective-permute-done.1 = s32[864]{0:T(1024)S(1)} collective-permute-done((s32[864]{0:T(1024)}, s32[864]{0:T(1024)S(1)}, u32[]{:S(2)}, u32[]{:S(2)}) %collective-permute-start.1) | collective-permute-done | bytes 3488 | tf_op jit(solution)/shard_map/while/body/eval_jaxpr/ppermute | solution.py:9
  519.7 3.3 all-to-all-start.3
  523.7 6.9 %all-to-all-done.3 = f32[8,1,108]{2,1,0:T(1,128)S(1)} async-done(((f32[8,1,108]{2,1,0:T(1,128)}), f32[8,1,108]{2,1,0:T(1,128)S(1)}, u32[]{:S(2)}, u32[]{:S(2)}) %all-to-all-start.3) | async-done | bytes 3488 | tf_op jit(solution)/shard_map/all_to_all | solution.py:59
  531.8 4.3 gather_fusion.3
  (206 shorter events, 92.3 us)
Async XLA Ops:
  40.9 27.9 %all-to-all-start = ((bf16[8,108,1024]{2,1,0:T(8,128)(2,1)}), bf16[8,108,1024]{2,1,0:T(8,128)(2,1)S(1)}, u32[]{:S(2)}, u32[]{:S(2)}) async-start(bf16[8,108,1024]{2,1,0:T(8,128)(2,1)} %broadcast_select_fusion), calls=%async_computation | async-start | bytes 3670016 | tf_op jit(solution)/shard_map/all_to_all | solution.py:41
  76.0 25.6 %collective-permute-start = (bf16[864,1024]{1,0:T(8,128)(2,1)}, bf16[864,1024]{1,0:T(8,128)(2,1)S(1)}, u32[]{:S(2)}, u32[]{:S(2)}) collective-permute-start(bf16[864,1024]{1,0:T(8,128)(2,1)} %get-tuple-element.176), channel_id=1, source_target_pairs={{0,1},{1,2},{2,3},{3,4},{4,5},{5,6},{6,7},{7,8},{8,9},{9,10},{10,1... | collective-permute-start | bytes 5308424 | tf_op jit(solution)/shard_map/while/body/eval_jaxpr/ppermute | solution.py:9
  105.6 25.5 %collective-permute-start = (bf16[864,1024]{1,0:T(8,128)(2,1)}, bf16[864,1024]{1,0:T(8,128)(2,1)S(1)}, u32[]{:S(2)}, u32[]{:S(2)}) collective-permute-start(bf16[864,1024]{1,0:T(8,128)(2,1)} %get-tuple-element.176), channel_id=1, source_target_pairs={{0,1},{1,2},{2,3},{3,4},{4,5},{5,6},{6,7},{7,8},{8,9},{9,10},{10,1... | collective-permute-start | bytes 5308424 | tf_op jit(solution)/shard_map/while/body/eval_jaxpr/ppermute | solution.py:9
  105.6 24.3 %collective-permute-start.1 = (s32[864]{0:T(1024)}, s32[864]{0:T(1024)S(1)}, u32[]{:S(2)}, u32[]{:S(2)}) collective-permute-start(s32[864]{0:T(1024)} %get-tuple-element.177), channel_id=1, source_target_pairs={{0,1},{1,2},{2,3},{3,4},{4,5},{5,6},{6,7},{7,8},{8,9},{9,10},{10,1... | collective-permute-start | bytes 10376 | tf_op jit(solution)/shard_map/while/body/eval_jaxpr/ppermute | solution.py:9
  105.6 24.9 %collective-permute-start.2 = (s32[864]{0:T(1024)}, s32[864]{0:T(1024)S(1)}, u32[]{:S(2)}, u32[]{:S(2)}) collective-permute-start(s32[864]{0:T(1024)} %get-tuple-element.178), channel_id=1, source_target_pairs={{0,1},{1,2},{2,3},{3,4},{4,5},{5,6},{6,7},{7,8},{8,9},{9,10},{10,1... | collective-permute-start | bytes 10376 | tf_op jit(solution)/shard_map/while/body/eval_jaxpr/ppermute | solution.py:9
  135.1 25.5 %collective-permute-start = (bf16[864,1024]{1,0:T(8,128)(2,1)}, bf16[864,1024]{1,0:T(8,128)(2,1)S(1)}, u32[]{:S(2)}, u32[]{:S(2)}) collective-permute-start(bf16[864,1024]{1,0:T(8,128)(2,1)} %get-tuple-element.176), channel_id=1, source_target_pairs={{0,1},{1,2},{2,3},{3,4},{4,5},{5,6},{6,7},{7,8},{8,9},{9,10},{10,1... | collective-permute-start | bytes 5308424 | tf_op jit(solution)/shard_map/while/body/eval_jaxpr/ppermute | solution.py:9
  135.1 24.9 %collective-permute-start.2 = (s32[864]{0:T(1024)}, s32[864]{0:T(1024)S(1)}, u32[]{:S(2)}, u32[]{:S(2)}) collective-permute-start(s32[864]{0:T(1024)} %get-tuple-element.178), channel_id=1, source_target_pairs={{0,1},{1,2},{2,3},{3,4},{4,5},{5,6},{6,7},{7,8},{8,9},{9,10},{10,1... | collective-permute-start | bytes 10376 | tf_op jit(solution)/shard_map/while/body/eval_jaxpr/ppermute | solution.py:9
  164.7 25.5 %collective-permute-start = (bf16[864,1024]{1,0:T(8,128)(2,1)}, bf16[864,1024]{1,0:T(8,128)(2,1)S(1)}, u32[]{:S(2)}, u32[]{:S(2)}) collective-permute-start(bf16[864,1024]{1,0:T(8,128)(2,1)} %get-tuple-element.176), channel_id=1, source_target_pairs={{0,1},{1,2},{2,3},{3,4},{4,5},{5,6},{6,7},{7,8},{8,9},{9,10},{10,1... | collective-permute-start | bytes 5308424 | tf_op jit(solution)/shard_map/while/body/eval_jaxpr/ppermute | solution.py:9
  164.7 24.9 %collective-permute-start.2 = (s32[864]{0:T(1024)}, s32[864]{0:T(1024)S(1)}, u32[]{:S(2)}, u32[]{:S(2)}) collective-permute-start(s32[864]{0:T(1024)} %get-tuple-element.178), channel_id=1, source_target_pairs={{0,1},{1,2},{2,3},{3,4},{4,5},{5,6},{6,7},{7,8},{8,9},{9,10},{10,1... | collective-permute-start | bytes 10376 | tf_op jit(solution)/shard_map/while/body/eval_jaxpr/ppermute | solution.py:9
  194.2 25.5 %collective-permute-start = (bf16[864,1024]{1,0:T(8,128)(2,1)}, bf16[864,1024]{1,0:T(8,128)(2,1)S(1)}, u32[]{:S(2)}, u32[]{:S(2)}) collective-permute-start(bf16[864,1024]{1,0:T(8,128)(2,1)} %get-tuple-element.176), channel_id=1, source_target_pairs={{0,1},{1,2},{2,3},{3,4},{4,5},{5,6},{6,7},{7,8},{8,9},{9,10},{10,1... | collective-permute-start | bytes 5308424 | tf_op jit(solution)/shard_map/while/body/eval_jaxpr/ppermute | solution.py:9
  194.2 24.9 %collective-permute-start.2 = (s32[864]{0:T(1024)}, s32[864]{0:T(1024)S(1)}, u32[]{:S(2)}, u32[]{:S(2)}) collective-permute-start(s32[864]{0:T(1024)} %get-tuple-element.178), channel_id=1, source_target_pairs={{0,1},{1,2},{2,3},{3,4},{4,5},{5,6},{6,7},{7,8},{8,9},{9,10},{10,1... | collective-permute-start | bytes 10376 | tf_op jit(solution)/shard_map/while/body/eval_jaxpr/ppermute | solution.py:9
  223.7 25.5 %collective-permute-start = (bf16[864,1024]{1,0:T(8,128)(2,1)}, bf16[864,1024]{1,0:T(8,128)(2,1)S(1)}, u32[]{:S(2)}, u32[]{:S(2)}) collective-permute-start(bf16[864,1024]{1,0:T(8,128)(2,1)} %get-tuple-element.176), channel_id=1, source_target_pairs={{0,1},{1,2},{2,3},{3,4},{4,5},{5,6},{6,7},{7,8},{8,9},{9,10},{10,1... | collective-permute-start | bytes 5308424 | tf_op jit(solution)/shard_map/while/body/eval_jaxpr/ppermute | solution.py:9
  223.7 24.9 %collective-permute-start.2 = (s32[864]{0:T(1024)}, s32[864]{0:T(1024)S(1)}, u32[]{:S(2)}, u32[]{:S(2)}) collective-permute-start(s32[864]{0:T(1024)} %get-tuple-element.178), channel_id=1, source_target_pairs={{0,1},{1,2},{2,3},{3,4},{4,5},{5,6},{6,7},{7,8},{8,9},{9,10},{10,1... | collective-permute-start | bytes 10376 | tf_op jit(solution)/shard_map/while/body/eval_jaxpr/ppermute | solution.py:9
  253.2 25.5 %collective-permute-start = (bf16[864,1024]{1,0:T(8,128)(2,1)}, bf16[864,1024]{1,0:T(8,128)(2,1)S(1)}, u32[]{:S(2)}, u32[]{:S(2)}) collective-permute-start(bf16[864,1024]{1,0:T(8,128)(2,1)} %get-tuple-element.176), channel_id=1, source_target_pairs={{0,1},{1,2},{2,3},{3,4},{4,5},{5,6},{6,7},{7,8},{8,9},{9,10},{10,1... | collective-permute-start | bytes 5308424 | tf_op jit(solution)/shard_map/while/body/eval_jaxpr/ppermute | solution.py:9
  253.3 24.9 %collective-permute-start.2 = (s32[864]{0:T(1024)}, s32[864]{0:T(1024)S(1)}, u32[]{:S(2)}, u32[]{:S(2)}) collective-permute-start(s32[864]{0:T(1024)} %get-tuple-element.178), channel_id=1, source_target_pairs={{0,1},{1,2},{2,3},{3,4},{4,5},{5,6},{6,7},{7,8},{8,9},{9,10},{10,1... | collective-permute-start | bytes 10376 | tf_op jit(solution)/shard_map/while/body/eval_jaxpr/ppermute | solution.py:9
  282.8 25.5 %collective-permute-start = (bf16[864,1024]{1,0:T(8,128)(2,1)}, bf16[864,1024]{1,0:T(8,128)(2,1)S(1)}, u32[]{:S(2)}, u32[]{:S(2)}) collective-permute-start(bf16[864,1024]{1,0:T(8,128)(2,1)} %get-tuple-element.176), channel_id=1, source_target_pairs={{0,1},{1,2},{2,3},{3,4},{4,5},{5,6},{6,7},{7,8},{8,9},{9,10},{10,1... | collective-permute-start | bytes 5308424 | tf_op jit(solution)/shard_map/while/body/eval_jaxpr/ppermute | solution.py:9
  282.8 24.9 %collective-permute-start.2 = (s32[864]{0:T(1024)}, s32[864]{0:T(1024)S(1)}, u32[]{:S(2)}, u32[]{:S(2)}) collective-permute-start(s32[864]{0:T(1024)} %get-tuple-element.178), channel_id=1, source_target_pairs={{0,1},{1,2},{2,3},{3,4},{4,5},{5,6},{6,7},{7,8},{8,9},{9,10},{10,1... | collective-permute-start | bytes 10376 | tf_op jit(solution)/shard_map/while/body/eval_jaxpr/ppermute | solution.py:9
  312.3 25.5 %collective-permute-start = (bf16[864,1024]{1,0:T(8,128)(2,1)}, bf16[864,1024]{1,0:T(8,128)(2,1)S(1)}, u32[]{:S(2)}, u32[]{:S(2)}) collective-permute-start(bf16[864,1024]{1,0:T(8,128)(2,1)} %get-tuple-element.176), channel_id=1, source_target_pairs={{0,1},{1,2},{2,3},{3,4},{4,5},{5,6},{6,7},{7,8},{8,9},{9,10},{10,1... | collective-permute-start | bytes 5308424 | tf_op jit(solution)/shard_map/while/body/eval_jaxpr/ppermute | solution.py:9
  312.3 24.9 %collective-permute-start.2 = (s32[864]{0:T(1024)}, s32[864]{0:T(1024)S(1)}, u32[]{:S(2)}, u32[]{:S(2)}) collective-permute-start(s32[864]{0:T(1024)} %get-tuple-element.178), channel_id=1, source_target_pairs={{0,1},{1,2},{2,3},{3,4},{4,5},{5,6},{6,7},{7,8},{8,9},{9,10},{10,1... | collective-permute-start | bytes 10376 | tf_op jit(solution)/shard_map/while/body/eval_jaxpr/ppermute | solution.py:9
  341.8 25.5 %collective-permute-start = (bf16[864,1024]{1,0:T(8,128)(2,1)}, bf16[864,1024]{1,0:T(8,128)(2,1)S(1)}, u32[]{:S(2)}, u32[]{:S(2)}) collective-permute-start(bf16[864,1024]{1,0:T(8,128)(2,1)} %get-tuple-element.176), channel_id=1, source_target_pairs={{0,1},{1,2},{2,3},{3,4},{4,5},{5,6},{6,7},{7,8},{8,9},{9,10},{10,1... | collective-permute-start | bytes 5308424 | tf_op jit(solution)/shard_map/while/body/eval_jaxpr/ppermute | solution.py:9
  341.8 24.9 %collective-permute-start.2 = (s32[864]{0:T(1024)}, s32[864]{0:T(1024)S(1)}, u32[]{:S(2)}, u32[]{:S(2)}) collective-permute-start(s32[864]{0:T(1024)} %get-tuple-element.178), channel_id=1, source_target_pairs={{0,1},{1,2},{2,3},{3,4},{4,5},{5,6},{6,7},{7,8},{8,9},{9,10},{10,1... | collective-permute-start | bytes 10376 | tf_op jit(solution)/shard_map/while/body/eval_jaxpr/ppermute | solution.py:9
  371.4 25.5 %collective-permute-start = (bf16[864,1024]{1,0:T(8,128)(2,1)}, bf16[864,1024]{1,0:T(8,128)(2,1)S(1)}, u32[]{:S(2)}, u32[]{:S(2)}) collective-permute-start(bf16[864,1024]{1,0:T(8,128)(2,1)} %get-tuple-element.176), channel_id=1, source_target_pairs={{0,1},{1,2},{2,3},{3,4},{4,5},{5,6},{6,7},{7,8},{8,9},{9,10},{10,1... | collective-permute-start | bytes 5308424 | tf_op jit(solution)/shard_map/while/body/eval_jaxpr/ppermute | solution.py:9
  371.4 24.9 %collective-permute-start.2 = (s32[864]{0:T(1024)}, s32[864]{0:T(1024)S(1)}, u32[]{:S(2)}, u32[]{:S(2)}) collective-permute-start(s32[864]{0:T(1024)} %get-tuple-element.178), channel_id=1, source_target_pairs={{0,1},{1,2},{2,3},{3,4},{4,5},{5,6},{6,7},{7,8},{8,9},{9,10},{10,1... | collective-permute-start | bytes 10376 | tf_op jit(solution)/shard_map/while/body/eval_jaxpr/ppermute | solution.py:9
  400.9 25.5 %collective-permute-start = (bf16[864,1024]{1,0:T(8,128)(2,1)}, bf16[864,1024]{1,0:T(8,128)(2,1)S(1)}, u32[]{:S(2)}, u32[]{:S(2)}) collective-permute-start(bf16[864,1024]{1,0:T(8,128)(2,1)} %get-tuple-element.176), channel_id=1, source_target_pairs={{0,1},{1,2},{2,3},{3,4},{4,5},{5,6},{6,7},{7,8},{8,9},{9,10},{10,1... | collective-permute-start | bytes 5308424 | tf_op jit(solution)/shard_map/while/body/eval_jaxpr/ppermute | solution.py:9
  400.9 24.9 %collective-permute-start.2 = (s32[864]{0:T(1024)}, s32[864]{0:T(1024)S(1)}, u32[]{:S(2)}, u32[]{:S(2)}) collective-permute-start(s32[864]{0:T(1024)} %get-tuple-element.178), channel_id=1, source_target_pairs={{0,1},{1,2},{2,3},{3,4},{4,5},{5,6},{6,7},{7,8},{8,9},{9,10},{10,1... | collective-permute-start | bytes 10376 | tf_op jit(solution)/shard_map/while/body/eval_jaxpr/ppermute | solution.py:9
  430.4 25.5 %collective-permute-start = (bf16[864,1024]{1,0:T(8,128)(2,1)}, bf16[864,1024]{1,0:T(8,128)(2,1)S(1)}, u32[]{:S(2)}, u32[]{:S(2)}) collective-permute-start(bf16[864,1024]{1,0:T(8,128)(2,1)} %get-tuple-element.176), channel_id=1, source_target_pairs={{0,1},{1,2},{2,3},{3,4},{4,5},{5,6},{6,7},{7,8},{8,9},{9,10},{10,1... | collective-permute-start | bytes 5308424 | tf_op jit(solution)/shard_map/while/body/eval_jaxpr/ppermute | solution.py:9
  430.4 24.9 %collective-permute-start.2 = (s32[864]{0:T(1024)}, s32[864]{0:T(1024)S(1)}, u32[]{:S(2)}, u32[]{:S(2)}) collective-permute-start(s32[864]{0:T(1024)} %get-tuple-element.178), channel_id=1, source_target_pairs={{0,1},{1,2},{2,3},{3,4},{4,5},{5,6},{6,7},{7,8},{8,9},{9,10},{10,1... | collective-permute-start | bytes 10376 | tf_op jit(solution)/shard_map/while/body/eval_jaxpr/ppermute | solution.py:9
  459.9 25.5 %collective-permute-start = (bf16[864,1024]{1,0:T(8,128)(2,1)}, bf16[864,1024]{1,0:T(8,128)(2,1)S(1)}, u32[]{:S(2)}, u32[]{:S(2)}) collective-permute-start(bf16[864,1024]{1,0:T(8,128)(2,1)} %get-tuple-element.176), channel_id=1, source_target_pairs={{0,1},{1,2},{2,3},{3,4},{4,5},{5,6},{6,7},{7,8},{8,9},{9,10},{10,1... | collective-permute-start | bytes 5308424 | tf_op jit(solution)/shard_map/while/body/eval_jaxpr/ppermute | solution.py:9
  459.9 24.9 %collective-permute-start.2 = (s32[864]{0:T(1024)}, s32[864]{0:T(1024)S(1)}, u32[]{:S(2)}, u32[]{:S(2)}) collective-permute-start(s32[864]{0:T(1024)} %get-tuple-element.178), channel_id=1, source_target_pairs={{0,1},{1,2},{2,3},{3,4},{4,5},{5,6},{6,7},{7,8},{8,9},{9,10},{10,1... | collective-permute-start | bytes 10376 | tf_op jit(solution)/shard_map/while/body/eval_jaxpr/ppermute | solution.py:9
  489.5 25.5 %collective-permute-start = (bf16[864,1024]{1,0:T(8,128)(2,1)}, bf16[864,1024]{1,0:T(8,128)(2,1)S(1)}, u32[]{:S(2)}, u32[]{:S(2)}) collective-permute-start(bf16[864,1024]{1,0:T(8,128)(2,1)} %get-tuple-element.176), channel_id=1, source_target_pairs={{0,1},{1,2},{2,3},{3,4},{4,5},{5,6},{6,7},{7,8},{8,9},{9,10},{10,1... | collective-permute-start | bytes 5308424 | tf_op jit(solution)/shard_map/while/body/eval_jaxpr/ppermute | solution.py:9
  489.5 24.4 %collective-permute-start.1 = (s32[864]{0:T(1024)}, s32[864]{0:T(1024)S(1)}, u32[]{:S(2)}, u32[]{:S(2)}) collective-permute-start(s32[864]{0:T(1024)} %get-tuple-element.177), channel_id=1, source_target_pairs={{0,1},{1,2},{2,3},{3,4},{4,5},{5,6},{6,7},{7,8},{8,9},{9,10},{10,1... | collective-permute-start | bytes 10376 | tf_op jit(solution)/shard_map/while/body/eval_jaxpr/ppermute | solution.py:9
  489.5 24.9 %collective-permute-start.2 = (s32[864]{0:T(1024)}, s32[864]{0:T(1024)S(1)}, u32[]{:S(2)}, u32[]{:S(2)}) collective-permute-start(s32[864]{0:T(1024)} %get-tuple-element.178), channel_id=1, source_target_pairs={{0,1},{1,2},{2,3},{3,4},{4,5},{5,6},{6,7},{7,8},{8,9},{9,10},{10,1... | collective-permute-start | bytes 10376 | tf_op jit(solution)/shard_map/while/body/eval_jaxpr/ppermute | solution.py:9
  (27 other events, 472.5 us)
where the time goes:
time: 537 us; the launch traced here: 536 us
  waiting for transfers between devices  390 us (73%)
  local copies, waits for them, and re-layouts  64.4 us (12%)
  matrix products  44.7 us (8%)
  starting transfers between devices  23.4 us (4%)
  other arithmetic  13.4 us (2%)
    ppermute x45, waiting for transfers between devices, passed_along(): return lax.ppermute(x, axis, [(i, (i + by) % count) for i in range(count)])  363 us
    dot_general x16, matrix products, compare(): lax.dot_general(q_rows, key_rows, (((1,), (1,)), ((), ())), preferred_ele...  44.7 us
    while x45, local copies, waits for them, and re-layouts  36.1 us
    all_to_all x1, waiting for transfers between devices, on_device(): lax.all_to_all(send_rows, 'group', split_axis=0, concat_axis=0, tiled=True)  13.3 us
  transfers between devices with their start and end apart: 49, of which 18 were waited for; matrix products, arithmetic and copies ran while one was open for 8% of the time, Pallas kernels for 0%

commit v1 on v0

v1 whole, which is shorter than its diff:
```python
import jax
import jax.numpy as jnp
from jax import lax
from jax.sharding import PartitionSpec as P

BLOCK_WIDTH = 4
BLOCK_CAP = 7
AXES = ("group", "blk")


def on_device(embeddings, cluster, global_index, send_counts):
    row_count = embeddings.shape[0]
    blocks = lax.axis_size("blk")
    devices = lax.axis_size("group") * blocks
    slots = devices * BLOCK_CAP
    counts = send_counts[0]
    cum_ends = jnp.cumsum(counts)
    squares = jnp.sum(embeddings * embeddings, axis=1, keepdims=True)
    unit_rows = (embeddings * lax.rsqrt(squares + 1e-06)).astype(jnp.bfloat16)

    position = jnp.arange(row_count, dtype=jnp.int32)
    owner_group = jnp.sum((position[:, None] >= cum_ends[None, :]).astype(jnp.int32), axis=1)
    dest = owner_group * blocks + cluster // BLOCK_WIDTH
    earlier = (dest[:, None] == dest[None, :]) & (position[None, :] < position[:, None])
    rank = jnp.sum(earlier.astype(jnp.int32), axis=1)
    slot = dest * BLOCK_CAP + rank

    slot_ids = jnp.arange(slots, dtype=jnp.int32)
    picks = slot_ids[:, None] == slot[None, :]
    send_rows = jnp.dot(
        picks.astype(jnp.bfloat16), unit_rows, preferred_element_type=jnp.float32
    ).astype(jnp.bfloat16)
    meta = global_index * BLOCK_WIDTH + cluster % BLOCK_WIDTH
    send_meta = jnp.max(jnp.where(picks, meta[None, :], -1), axis=1)

    got_rows = lax.all_to_all(
        send_rows.reshape(devices, BLOCK_CAP, -1), AXES, 0, 0, tiled=True
    ).reshape(slots, -1)
    got_meta = lax.all_to_all(
        send_meta.reshape(devices, BLOCK_CAP), AXES, 0, 0, tiled=True
    ).reshape(slots)

    cosine = lax.dot_general(
        got_rows, got_rows, (((1,), (1,)), ((), ())), preferred_element_type=jnp.float32
    )
    got_ids = got_meta // BLOCK_WIDTH
    got_sub = got_meta % BLOCK_WIDTH
    usable = (
        (got_meta[None, :] >= 0)
        & (got_sub[:, None] == got_sub[None, :])
        & (got_ids[None, :] < got_ids[:, None])
    )
    best = jnp.max(jnp.where(usable, cosine, jnp.float32(-1.0)), axis=1)

    returned = lax.all_to_all(best.reshape(devices, BLOCK_CAP), AXES, 0, 0, tiled=True)
    return returned.reshape(slots)[slot]


def solution(mesh):
    placed = (
        P(AXES, None),
        P(AXES),
        P(AXES),
        P(AXES, None),
    )
    return jax.shard_map(
        on_device, mesh=mesh, in_specs=placed, out_specs=P(AXES), check_vma=False
    )
```

time: 537 us -> 90.8 us (0.17)
  waiting for transfers between devices: 390 us -> 38.4 us
  local copies, waits for them, and re-layouts: 64.4 us -> 12.8 us
  matrix products: 44.7 us -> 7.41 us
  other arithmetic: 13.4 us -> 5.97 us
    ppermute x45 -> x0, waiting for transfers between devices: 363 us -> none  [passed_along(): return lax.ppermute(x, axis, [(i, (i + by) % count) for i in range(count)])]
    dot_general x16 -> x2, matrix products: 44.7 us -> 7.41 us  [the longest x1 4.43 us: on_device(): lax.dot_general(got_rows, got_rows, (((1,), (1,)), ((), ())), preferred_e...]
    while x45 -> x0, local copies, waits for them, and re-layouts: 36.1 us -> none
    gather x7 -> x1, local copies, waits for them, and re-layouts: 18.2 us -> 4.27 us  [on_device(): return returned.reshape(slots)[slot]]
    all_to_all x4 -> x3, waiting for transfers between devices: 26.4 us -> 38.4 us  [the longest x1 28.4 us: on_device(): lax.all_to_all(send_rows.reshape(devices, BLOCK_CAP, -1), AXES, 0, 0, til...]
    gather x6 -> x1, other arithmetic: 5.75 us -> 0.01 us  [on_device(): return returned.reshape(slots)[slot]]
    all_to_all x4 -> x3, starting transfers between devices: 22 us -> 24.9 us  [the longest x1 11.2 us: on_device(): lax.all_to_all(send_meta.reshape(devices, BLOCK_CAP), AXES, 0, 0, tiled=T...]
  transfers between devices with their start and end apart: 49 -> 3, of which waited for: 18 -> 3; matrix products, arithmetic and copies ran while one was open for 8% -> 12% of each run, Pallas kernels for 0% -> 0%
where the time goes in v1:
time: 90.8 us; the launch traced here: 89.6 us
  waiting for transfers between devices  38.4 us (42%)
  starting transfers between devices  24.9 us (27%)
  local copies, waits for them, and re-layouts  12.8 us (14%)
  matrix products  7.41 us (8%)
  other arithmetic  5.97 us (7%)
    all_to_all x1, waiting for transfers between devices, on_device(): lax.all_to_all(send_rows.reshape(devices, BLOCK_CAP, -1), AXES, 0, 0, til...  28.4 us
    all_to_all x1, starting transfers between devices, on_device(): lax.all_to_all(send_meta.reshape(devices, BLOCK_CAP), AXES, 0, 0, tiled=T...  11.2 us
    all_to_all x1, waiting for transfers between devices, on_device(): lax.all_to_all(best.reshape(devices, BLOCK_CAP), AXES, 0, 0, tiled=True)  9.38 us
    all_to_all x1, starting transfers between devices, on_device(): lax.all_to_all(send_rows.reshape(devices, BLOCK_CAP, -1), AXES, 0, 0, til...  9.14 us
    all_to_all x1, starting transfers between devices, on_device(): lax.all_to_all(best.reshape(devices, BLOCK_CAP), AXES, 0, 0, tiled=True)  4.61 us
    dot_general x1, matrix products, on_device(): lax.dot_general(got_rows, got_rows, (((1,), (1,)), ((), ())), preferred_e...  4.43 us
    gather x1, local copies, waits for them, and re-layouts, on_device(): return returned.reshape(slots)[slot]  4.27 us
    reshape x1, local copies, waits for them, and re-layouts, on_device(): send_rows.reshape(devices, BLOCK_CAP, -1)  3.88 us
  transfers between devices with their start and end apart: 3, of which 3 were waited for; matrix products, arithmetic and copies ran while one was open for 12% of the time, Pallas kernels for 0%

profile of v1, /device:TPU:0, one launch (start us, length us, event | category | flops | bytes accessed | tf_op | source)
XLA Modules:
  0.0 89.6 jit_solution(13697133538695838627)
XLA Ops:
  0.0 0.0 copy-start
  0.0 1.0 %reduce-window.8 = s32[8,1]{0,1:T(1,128)S(1)} reduce-window(s32[8,1]{0,1:T(1,128)} %bitcast.7, s32[]{:T(128)} %constant.57.clone.1), window={size=8x1 pad=7_0x0_0}, to_apply=%region_0.0 | reduce-window | flops 56 | bytes 68 | tf_op jit(solution)/shard_map/reduce-window.3
  1.0 0.1 convert_reduce_fusion.1
  1.1 0.7 fusion.6
  1.8 0.3 convert_reduce_fusion
  2.1 0.4 select_reduce_fusion.1
  2.4 0.8 all_to_all.15
  3.3 11.2 %all-to-all-start = ((s32[128,1,7]{2,1,0:T(1,128)}), s32[128,1,7]{2,1,0:T(1,128)S(1)}, u32[]{:S(2)}, u32[]{:S(2)}) async-start(s32[128,1,7]{2,1,0:T(1,128)} %bitcast.2), calls=%async_computation | async-start | bytes 131072 | tf_op jit(solution)/shard_map/all_to_all | solution.py:39
  14.4 1.9 %multiply_reduce_fusion = f32[576]{0:T(1024)S(1)} fusion(f32[576,1024]{1,0:T(8,128)} %param.4), kind=kLoop, calls=%fused_computation.3 | loop fusion | flops 1179072 | bytes 2361600 | tf_op jit(solution)/shard_map/reduce_sum | solution.py:18
  16.4 0.0 copy-done
  16.4 3.0 %fusion.1 = bf16[896,1024]{1,0:T(8,128)(2,1)} fusion(f32[576,1024]{1,0:T(8,128)S(1)} %copy-done, f32[576]{0:T(1024)S(1)} %add_rsqrt_fusion, s32[576]{0:T(1024)S(1)} %get-tuple-element.6), kind=kOutput, calls=%fused_computation.7 | convolution fusion | flops 1059577856 | bytes 4198912 | tf_op jit(solution)/shard_map/dot_general | solution.py:30
  19.3 3.9 %reshape.165 = bf16[128,7,1024]{2,1,0:T(8,128)(2,1)} reshape(bf16[896,1024]{1,0:T(8,128)(2,1)} %fusion.1) | data formatting | bytes 3670016 | tf_op jit(solution)/shard_map/reshape | solution.py:37
  23.2 0.6 all-to-all-done
  23.8 9.1 %all-to-all-start.1 = ((bf16[128,7,1024]{2,1,0:T(8,128)(2,1)}), bf16[128,7,1024]{2,1,0:T(8,128)(2,1)S(1)}, u32[]{:S(2)}, u32[]{:S(2)}) async-start(bf16[128,7,1024]{2,1,0:T(8,128)(2,1)} %reshape.165), calls=%async_computation.1 | async-start | bytes 4194304 | tf_op jit(solution)/shard_map/all_to_all | solution.py:36
  33.0 0.5 broadcast.138
  33.5 0.8 reduce.6
  34.3 0.2 broadcast_in_dim_reshape.3
  34.6 28.4 %all-to-all-done.1 = bf16[128,7,1024]{2,1,0:T(8,128)(2,1)S(1)} async-done(((bf16[128,7,1024]{2,1,0:T(8,128)(2,1)}), bf16[128,7,1024]{2,1,0:T(8,128)(2,1)S(1)}, u32[]{:S(2)}, u32[]{:S(2)}) %all-to-all-start.1) | async-done | bytes 1835040 | tf_op jit(solution)/shard_map/all_to_all | solution.py:36
  62.9 1.6 %reshape.166 = bf16[896,1024]{1,0:T(8,128)(2,1)} reshape(bf16[128,7,1024]{2,1,0:T(8,128)(2,1)S(1)} %all-to-all-done.1) | data formatting | bytes 3670016 | tf_op jit(solution)/shard_map/reshape | solution.py:38
  64.5 4.4 %select_reduce_fusion = f32[896]{0:T(1024)S(1)} fusion(bf16[896,1024]{1,0:T(8,128)(2,1)} %reshape.166, s32[896]{0:T(1024)S(1)} %get-tuple-element.8, s32[896]{0:T(1024)S(1)} %get-tuple-element.7, pred[896]{0:T(1024)(128)(4,1)S(1)} %broadcast_compare_fusion), kind=kOutput, calls=%fused_computation.1 | convolution fusion | flops 1648983168 | bytes 1846656 | tf_op jit(solution)/shard_map/dot_general | solution.py:43
  69.0 0.8 all_to_all.18
  69.8 4.6 %all-to-all-start.2 = ((f32[128,1,7]{2,1,0:T(1,128)}), f32[128,1,7]{2,1,0:T(1,128)S(1)}, u32[]{:S(2)}, u32[]{:S(2)}) async-start(f32[128,1,7]{2,1,0:T(1,128)} %bitcast.3), calls=%async_computation.2 | async-start | bytes 131072 | tf_op jit(solution)/shard_map/all_to_all | solution.py:55
  74.4 9.4 %all-to-all-done.2 = f32[128,1,7]{2,1,0:T(1,128)S(1)} async-done(((f32[128,1,7]{2,1,0:T(1,128)}), f32[128,1,7]{2,1,0:T(1,128)S(1)}, u32[]{:S(2)}, u32[]{:S(2)}) %all-to-all-start.2) | async-done | bytes 3616 | tf_op jit(solution)/shard_map/all_to_all | solution.py:55
  83.8 0.5 broadcast.139
  84.3 0.8 reduce.7
  85.1 0.2 reshape.167
  85.3 4.3 %gather_fusion = f32[576]{0:T(1024)} fusion(f32[896]{0:T(1024)S(1)} %reshape.167, s32[1024]{0:T(1024)S(1)} %pad_clamp_fusion), kind=kCustom, calls=%fused_computation | custom fusion | bytes 6912 | tf_op jit(solution)/shard_map/gather | solution.py:56
  (5 shorter events, 0.0 us)
Async XLA Ops:
  0.0 16.4 %copy-start = (f32[576,1024]{1,0:T(8,128)S(1)}, f32[576,1024]{1,0:T(8,128)}, u32[]{:S(2)}) copy-start(f32[576,1024]{1,0:T(8,128)} %param.4) | copy-start | bytes 7077892
  3.3 20.6 %all-to-all-start = ((s32[128,1,7]{2,1,0:T(1,128)}), s32[128,1,7]{2,1,0:T(1,128)S(1)}, u32[]{:S(2)}, u32[]{:S(2)}) async-start(s32[128,1,7]{2,1,0:T(1,128)} %bitcast.2), calls=%async_computation | async-start | bytes 131072 | tf_op jit(solution)/shard_map/all_to_all | solution.py:39
  23.8 39.1 %all-to-all-start.1 = ((bf16[128,7,1024]{2,1,0:T(8,128)(2,1)}), bf16[128,7,1024]{2,1,0:T(8,128)(2,1)S(1)}, u32[]{:S(2)}, u32[]{:S(2)}) async-start(bf16[128,7,1024]{2,1,0:T(8,128)(2,1)} %reshape.165), calls=%async_computation.1 | async-start | bytes 4194304 | tf_op jit(solution)/shard_map/all_to_all | solution.py:36
  69.8 14.0 %all-to-all-start.2 = ((f32[128,1,7]{2,1,0:T(1,128)}), f32[128,1,7]{2,1,0:T(1,128)S(1)}, u32[]{:S(2)}, u32[]{:S(2)}) async-start(f32[128,1,7]{2,1,0:T(1,128)} %bitcast.3), calls=%async_computation.2 | async-start | bytes 131072 | tf_op jit(solution)/shard_map/all_to_all | solution.py:55

commit v2 on v1

v2 whole, which is shorter than its diff:
```python
import jax
import jax.numpy as jnp
from jax import lax
from jax.sharding import PartitionSpec as P

BLOCK_WIDTH = 4
BLOCK_CAP = 7
CHUNK = 8
META_W = 8
AXES = ("group", "blk")


def meta_digits(cluster, global_index):
    return (
        jnp.ones_like(cluster),
        cluster % BLOCK_WIDTH,
        global_index // 4096,
        (global_index // 64) % 64,
        global_index % 64,
    )


def on_device(embeddings, cluster, global_index, send_counts):
    row_count, feat_width = embeddings.shape
    blocks = lax.axis_size("blk")
    devices = lax.axis_size("group") * blocks
    slots = devices * CHUNK
    counts = send_counts[0]
    cum_ends = jnp.cumsum(counts)
    squares = jnp.sum(embeddings * embeddings, axis=1, keepdims=True)
    unit_rows = (embeddings * lax.rsqrt(squares + 1e-06)).astype(jnp.bfloat16)

    position = jnp.arange(row_count, dtype=jnp.int32)
    owner_group = jnp.sum((position[:, None] >= cum_ends[None, :]).astype(jnp.int32), axis=1)
    dest = owner_group * blocks + cluster // BLOCK_WIDTH
    earlier = (dest[:, None] == dest[None, :]) & (position[None, :] < position[:, None])
    rank = jnp.sum(earlier.astype(jnp.int32), axis=1)
    slot = dest * CHUNK + rank

    slot_ids = jnp.arange(slots, dtype=jnp.int32)
    picks = slot_ids[:, None] == slot[None, :]
    send_rows = jnp.dot(
        picks.astype(jnp.bfloat16), unit_rows, preferred_element_type=jnp.float32
    ).astype(jnp.bfloat16)

    offset = jnp.arange(feat_width, dtype=jnp.int32)[None, :] - rank[:, None] * META_W
    spread = jnp.zeros((row_count, feat_width), jnp.int32)
    for t, digit in enumerate(meta_digits(cluster, global_index)):
        spread = jnp.where(offset == t, digit[:, None], spread)
    to_dest = dest[:, None] == jnp.arange(devices, dtype=jnp.int32)[None, :]
    meta_rows = lax.dot_general(
        to_dest.astype(jnp.bfloat16),
        spread.astype(jnp.bfloat16),
        (((0,), (0,)), ((), ())),
        preferred_element_type=jnp.float32,
    ).astype(jnp.bfloat16)
    is_meta = jnp.arange(CHUNK) == CHUNK - 1
    send = jnp.where(
        is_meta[None, :, None],
        meta_rows[:, None, :],
        send_rows.reshape(devices, CHUNK, feat_width),
    )

    got = lax.all_to_all(send, AXES, 0, 0, tiled=True)
    got_rows = got.reshape(slots, feat_width)
    coded = got[:, CHUNK - 1, : BLOCK_CAP * META_W].astype(jnp.int32)
    coded = coded.reshape(devices, BLOCK_CAP, META_W)
    pad = ((0, 0), (0, CHUNK - BLOCK_CAP))
    got_valid = jnp.pad(coded[:, :, 0], pad).reshape(slots) > 0
    got_sub = jnp.pad(coded[:, :, 1], pad).reshape(slots)
    got_ids = jnp.pad(
        coded[:, :, 2] * 4096 + coded[:, :, 3] * 64 + coded[:, :, 4], pad
    ).reshape(slots)

    cosine = lax.dot_general(
        got_rows, got_rows, (((1,), (1,)), ((), ())), preferred_element_type=jnp.float32
    )
    usable = (
        got_valid[None, :]
        & (got_sub[:, None] == got_sub[None, :])
        & (got_ids[None, :] < got_ids[:, None])
    )
    best = jnp.max(jnp.where(usable, cosine, jnp.float32(-1.0)), axis=1)

    returned = lax.all_to_all(best.reshape(devices, CHUNK), AXES, 0, 0, tiled=True)
    return jnp.sum(jnp.where(picks, returned.reshape(slots, 1), jnp.float32(0.0)), axis=0)


def solution(mesh):
    placed = (
        P(AXES, None),
        P(AXES),
        P(AXES),
        P(AXES, None),
    )
    return jax.shard_map(
        on_device, mesh=mesh, in_specs=placed, out_specs=P(AXES), check_vma=False
    )
```

time: 90.8 us -> 69.5 us (0.77)
  blocking collectives: 0 us -> 54.4 us
  waiting for transfers between devices: 38.4 us -> 0 us
  starting transfers between devices: 24.9 us -> 0 us
  local copies, waits for them, and re-layouts: 12.8 us -> 1.76 us
  matrix products: 7.41 us -> 6.49 us
    all_to_all x0 -> x2, blocking collectives: none -> 54.4 us  [the longest x1 40.9 us: on_device(): got = lax.all_to_all(send, AXES, 0, 0, tiled=True)]
    all_to_all x3 -> x0, waiting for transfers between devices: 38.4 us -> none  [the longest x1 28.4 us: on_device(): lax.all_to_all(send_rows.reshape(devices, BLOCK_CAP, -1), AXES, 0, 0, til...]
    all_to_all x3 -> x0, starting transfers between devices: 24.9 us -> none  [the longest x1 11.2 us: on_device(): lax.all_to_all(send_meta.reshape(devices, BLOCK_CAP), AXES, 0, 0, tiled=T...]
    reshape x3 -> x0, local copies, waits for them, and re-layouts: 5.67 us -> none  [the longest x1 3.88 us: on_device(): send_rows.reshape(devices, BLOCK_CAP, -1)]
    gather x1 -> x0, local copies, waits for them, and re-layouts: 4.27 us -> none  [on_device(): return returned.reshape(slots)[slot]]
    all_to_all x4 -> x2, local copies, waits for them, and re-layouts: 2.66 us -> 0.59 us  [on_device(): lax.all_to_all(best.reshape(devices, CHUNK), AXES, 0, 0, tiled=True)]
    dot_general x0 -> x1, matrix products: none -> 1.4 us  [on_device(): lax.dot_general(to_dest.astype(jnp.bfloat16), spread.astype(jnp.bfloat16)...]
    dot_general x1, matrix products: 4.43 us -> 3.11 us  [on_device(): lax.dot_general(got_rows, got_rows, (((1,), (1,)), ((), ())), preferred_e...]
  transfers between devices with their start and end apart: 3 -> 0, of which waited for: 3 -> 0; matrix products, arithmetic and copies ran while one was open for 12% -> 0% of each run, Pallas kernels for 0% -> 0%
where the time goes in v2:
time: 69.5 us; the launch traced here: 68.5 us
  blocking collectives  54.4 us (78%)
  matrix products  6.49 us (9%)
  other arithmetic  5.68 us (8%)
  local copies, waits for them, and re-layouts  1.76 us (3%)
    all_to_all x1, blocking collectives, on_device(): got = lax.all_to_all(send, AXES, 0, 0, tiled=True)  40.9 us
    all_to_all x1, blocking collectives, on_device(): lax.all_to_all(best.reshape(devices, CHUNK), AXES, 0, 0, tiled=True)  13.5 us
    dot_general x1, matrix products, on_device(): lax.dot_general(got_rows, got_rows, (((1,), (1,)), ((), ())), preferred_e...  3.11 us
    dot_general x1, matrix products, on_device(): jnp.dot(picks.astype(jnp.bfloat16), unit_rows, preferred_element_type=jnp...  1.98 us
    reduce_sum x1, other arithmetic, on_device(): squares = jnp.sum(embeddings * embeddings, axis=1, keepdims=True)  1.91 us
    dot_general x1, matrix products, on_device(): lax.dot_general(to_dest.astype(jnp.bfloat16), spread.astype(jnp.bfloat16)...  1.4 us

profile of v2, /device:TPU:0, one launch (start us, length us, event | category | flops | bytes accessed | tf_op | source)
XLA Modules:
  0.0 68.5 jit_solution(7080596029416827919)
XLA Ops:
  0.0 0.8 %reduce-window.8 = s32[8,1]{0,1:T(1,128)S(1)} reduce-window(s32[8,1]{0,1:T(1,128)} %bitcast.25, s32[]{:T(128)} %constant.74.clone.1), window={size=8x1 pad=7_0x0_0}, to_apply=%region_0.0 | reduce-window | flops 56 | bytes 68 | tf_op jit(solution)/shard_map/reduce-window.3
  0.8 0.1 convert_reduce_fusion.1
  0.9 0.7 %add_select_fusion = (s32[576]{0:T(1024)S(1)}, s32[576]{0:T(1024)S(1)}, s32[576]{0:T(1024)S(1)}, s32[576]{0:T(1024)S(1)}, s32[576]{0:T(1024)S(1)}) fusion(s32[576]{0:T(1024)} %param.5, s32[576]{0:T(1024)S(1)} %convert_reduce_fusion.1, s32[576]{0:T(1024)} %param.6), kind=kLoop, calls=%fused_computation.36 | loop fusion | flops 35136 | bytes 18432 | tf_op jit(solution)/shard_map/jit(remainder)/select_n | solution.py:16
  1.6 0.3 convert_reduce_fusion
  1.9 1.9 %multiply_reduce_fusion = f32[576]{0:T(1024)S(1)} fusion(f32[576,1024]{1,0:T(8,128)} %param.4), kind=kLoop, calls=%fused_computation.3 | loop fusion | flops 1179072 | bytes 2361600 | tf_op jit(solution)/shard_map/reduce_sum | solution.py:30
  3.9 0.0 copy-start
  3.9 1.4 %convolution_convert_fusion = bf16[128,1024]{1,0:T(8,128)(2,1)S(1)} fusion(s32[576]{0:T(1024)S(1)} %get-tuple-element.13, s32[576]{0:T(1024)S(1)} %get-tuple-element.15, s32[576]{0:T(1024)S(1)} %get-tuple-element.16, s32[576]{0:T(1024)S(1)} %get-tuple-element.17, s32[576]{0:T(1024)S(1)} %get-tuple-element.8, s32[576]{0:T(1024)S(1)} %get-tuple-element.14), kind=kOutput, calls=%fused_computation.19 | convolution fusion | flops 158277632 | bytes 275968 | tf_op jit(solution)/shard_map/dot_general | solution.py:51
  5.3 0.3 copy-done
  5.5 2.0 %bitcast_select_fusion = bf16[128,8,1024]{2,1,0:T(8,128)(2,1)S(1)} fusion(pred[8]{0:T(512)(128)(4,1)S(1)} %iota_compare_fusion.8, f32[576,1024]{1,0:T(8,128)S(1)} %copy-done, f32[576]{0:T(1024)S(1)} %add_rsqrt_fusion, s32[576]{0:T(1024)S(1)} %get-tuple-element.9, bf16[128,1024]{1,0:T(8,128)(2,1)S(1)} %convolution_convert_fusion), kind=kOutput, calls=%fused_computation.15 | convolution fusion | flops 1211826176 | bytes 4723208 | tf_op jit(solution)/shard_map/dot_general | solution.py:42
  7.5 40.9 %all_to_all.14 = bf16[128,8,1024]{2,1,0:T(8,128)(2,1)S(1)} all-to-all(bf16[128,8,1024]{2,1,0:T(8,128)(2,1)S(1)} %bitcast_select_fusion), channel_id=1, replica_groups=mesh['group'=8,'blk'=16] {'group','blk'}, dimensions={0} | all-to-all | bytes 4194304 | tf_op jit(solution)/shard_map/all_to_all | solution.py:64
  48.4 0.1 slice.24
  48.5 0.1 copy.29
  48.6 0.1 copy.32
  48.8 0.1 eq.111
  48.8 0.1 copy.33
  49.0 0.1 lt.48
  49.1 0.1 copy.22
  49.2 0.1 gt.15
  49.3 3.1 %select_reduce_fusion = f32[1024]{0:T(1024)S(1)} fusion(bf16[128,8,1024]{2,1,0:T(8,128)(2,1)S(1)} %all_to_all.14, s32[1024]{0:T(1024)S(1)} %lt.48, s32[1024]{0:T(1024)S(1)} %eq.111, pred[1024]{0:T(1024)(128)(4,1)S(1)} %gt.15), kind=kOutput, calls=%fused_computation | convolution fusion | flops 2153774080 | bytes 2110464 | tf_op jit(solution)/shard_map/dot_general | solution.py:75
  52.4 0.1 all_to_all.10
  52.5 13.5 %all_to_all.15 = f32[128,1,8]{2,1,0:T(1,128)S(1)} all-to-all(f32[128,1,8]{2,1,0:T(1,128)S(1)} %bitcast.22), channel_id=1, replica_groups=mesh['group'=8,'blk'=16] {'group','blk'}, dimensions={0} | all-to-all | bytes 8192 | tf_op jit(solution)/shard_map/all_to_all | solution.py:85
  66.1 0.5 broadcast.94
  66.6 0.8 %reduce.3 = f32[128,8]{1,0:T(8,128)S(1)} reduce(f32[128,1,8]{2,1,0:T(1,128)S(1)} %all_to_all.15, f32[]{:T(128)} %broadcast.94), dimensions={1}, to_apply=%all_to_all.11.reduce_sub_computation.3 | reduce | bytes 8196 | tf_op jit(solution)/shard_map/all_to_all | solution.py:85
  67.4 0.1 broadcast_in_dim.87
  67.5 1.0 %select_reduce_fusion.1 = f32[576]{0:T(1024)} fusion(f32[1024]{0:T(1024)S(1)} %broadcast_in_dim.87, s32[576]{0:T(1024)S(1)} %get-tuple-element.9), kind=kLoop, calls=%fused_computation.1 | loop fusion | flops 1768896 | bytes 8704 | tf_op jit(solution)/shard_map/reduce_sum | solution.py:86
  (9 shorter events, 0.1 us)
Async XLA Ops:
  3.9 1.7 %copy-start = (f32[576,1024]{1,0:T(8,128)S(1)}, f32[576,1024]{1,0:T(8,128)}, u32[]{:S(2)}) copy-start(f32[576,1024]{1,0:T(8,128)} %param.4) | copy-start | bytes 7077892

commit v3 on v2

--- a/solution.py
+++ b/solution.py
@@ -26,7 +26,9 @@
     devices = lax.axis_size("group") * blocks
     slots = devices * CHUNK
     counts = send_counts[0]
-    cum_ends = jnp.cumsum(counts)
+    groups = counts.shape[0]
+    upto = jnp.arange(groups)[:, None] >= jnp.arange(groups)[None, :]
+    cum_ends = jnp.sum(jnp.where(upto, counts[None, :], 0), axis=1)
     squares = jnp.sum(embeddings * embeddings, axis=1, keepdims=True)
     unit_rows = (embeddings * lax.rsqrt(squares + 1e-06)).astype(jnp.bfloat16)
 
@@ -37,29 +39,18 @@
     rank = jnp.sum(earlier.astype(jnp.int32), axis=1)
     slot = dest * CHUNK + rank
 
-    slot_ids = jnp.arange(slots, dtype=jnp.int32)
-    picks = slot_ids[:, None] == slot[None, :]
-    send_rows = jnp.dot(
-        picks.astype(jnp.bfloat16), unit_rows, preferred_element_type=jnp.float32
-    ).astype(jnp.bfloat16)
-
     offset = jnp.arange(feat_width, dtype=jnp.int32)[None, :] - rank[:, None] * META_W
     spread = jnp.zeros((row_count, feat_width), jnp.int32)
     for t, digit in enumerate(meta_digits(cluster, global_index)):
         spread = jnp.where(offset == t, digit[:, None], spread)
-    to_dest = dest[:, None] == jnp.arange(devices, dtype=jnp.int32)[None, :]
-    meta_rows = lax.dot_general(
-        to_dest.astype(jnp.bfloat16),
-        spread.astype(jnp.bfloat16),
-        (((0,), (0,)), ((), ())),
+    slot_ids = jnp.arange(slots, dtype=jnp.int32)
+    picks = slot_ids[:, None] == slot[None, :]
+    meta_picks = slot_ids[:, None] == (dest * CHUNK + CHUNK - 1)[None, :]
+    send = jnp.dot(
+        jnp.concatenate([picks, meta_picks], axis=1).astype(jnp.bfloat16),
+        jnp.concatenate([unit_rows, spread.astype(jnp.bfloat16)], axis=0),
         preferred_element_type=jnp.float32,
-    ).astype(jnp.bfloat16)
-    is_meta = jnp.arange(CHUNK) == CHUNK - 1
-    send = jnp.where(
-        is_meta[None, :, None],
-        meta_rows[:, None, :],
-        send_rows.reshape(devices, CHUNK, feat_width),
-    )
+    ).astype(jnp.bfloat16).reshape(devices, CHUNK, feat_width)
 
     got = lax.all_to_all(send, AXES, 0, 0, tiled=True)
     got_rows = got.reshape(slots, feat_width)
@@ -82,7 +73,9 @@
     )
     best = jnp.max(jnp.where(usable, cosine, jnp.float32(-1.0)), axis=1)
 
-    returned = lax.all_to_all(best.reshape(devices, CHUNK), AXES, 0, 0, tiled=True)
+    lanes = 128
+    wide = jnp.pad(best.reshape(devices, CHUNK), ((0, 0), (0, lanes - CHUNK)))
+    returned = lax.all_to_all(wide, AXES, 0, 0, tiled=True)[:, :CHUNK]
     return jnp.sum(jnp.where(picks, returned.reshape(slots, 1), jnp.float32(0.0)), axis=0)
 
 

time: 69.5 us -> 69.4 us (level)
  other arithmetic: 5.68 us -> 6.55 us
  local copies, waits for them, and re-layouts: 1.76 us -> 1.01 us
    convert_element_type x0 -> x2, other arithmetic: none -> 1.51 us  [the longest x1 1.32 us: on_device(): spread.astype(jnp.bfloat16)]
    reduce_sum x0 -> x1, other arithmetic: none -> 0.92 us  [on_device(): cum_ends = jnp.sum(jnp.where(upto, counts[None, :], 0), axis=1)]
    another operation x1 -> x0, other arithmetic: 0.83 us -> none
    all_to_all x1 -> x0, other arithmetic: 0.81 us -> none  [on_device(): lax.all_to_all(best.reshape(devices, CHUNK), AXES, 0, 0, tiled=True)]
    eq x1 -> x2, other arithmetic: 0.01 us -> 0.79 us  [the longest x1 0.4 us: on_device(): picks = slot_ids[:, None] == slot[None, :]]
    select_n x1, other arithmetic: 0.73 us -> 0.02 us  [meta_digits(): global_index % 64]
    dot_general x2 -> x1, matrix products: 3.37 us -> 3.16 us  [on_device(): jnp.dot(jnp.concatenate([picks, meta_picks], axis=1).astype(jnp.bfloat16)...]
where the time goes in v3:
time: 69.4 us; the launch traced here: 68.4 us
  blocking collectives  54.4 us (78%)
  other arithmetic  6.55 us (9%)
  matrix products  6.28 us (9%)
  local copies, waits for them, and re-layouts  1.01 us (1%)
    all_to_all x1, blocking collectives, on_device(): got = lax.all_to_all(send, AXES, 0, 0, tiled=True)  40.9 us
    all_to_all x1, blocking collectives, on_device(): returned = lax.all_to_all(wide, AXES, 0, 0, tiled=True)[:, :CHUNK]  13.5 us
    dot_general x1, matrix products, on_device(): jnp.dot(jnp.concatenate([picks, meta_picks], axis=1).astype(jnp.bfloat16)...  3.16 us
    dot_general x1, matrix products, on_device(): lax.dot_general(got_rows, got_rows, (((1,), (1,)), ((), ())), preferred_e...  3.12 us
    reduce_sum x1, other arithmetic, on_device(): squares = jnp.sum(embeddings * embeddings, axis=1, keepdims=True)  1.91 us

profile of v3, /device:TPU:0, one launch (start us, length us, event | category | flops | bytes accessed | tf_op | source)
XLA Modules:
  0.0 68.4 jit_solution(3302300043056648547)
XLA Ops:
  0.0 0.0 copy-start
  0.0 0.0 copy-start.1
  0.0 0.0 copy-start.2
  0.0 0.9 %select_reduce_fusion.2 = s32[8]{0:T(128)S(1)} fusion(s32[8]{0:T(128)} %bitcast.28), kind=kLoop, calls=%fused_computation.53 | loop fusion | flops 184 | bytes 64 | tf_op jit(solution)/shard_map/reduce_sum | solution.py:31
  0.9 0.1 convert_reduce_fusion.1
  1.0 1.9 %multiply_reduce_fusion = f32[576]{0:T(1024)S(1)} fusion(f32[576,1024]{1,0:T(8,128)} %param.4), kind=kLoop, calls=%fused_computation.17 | loop fusion | flops 1179072 | bytes 2361600 | tf_op jit(solution)/shard_map/reduce_sum | solution.py:32
  2.9 0.0 copy-done.1
  2.9 0.0 copy-done.2
  3.0 0.3 convert_reduce_fusion
  3.3 0.4 iota_compare_fusion.1
  3.7 0.4 iota_compare_fusion
  4.1 0.0 copy-done
  4.1 0.2 multiply_convert_fusion
  4.3 1.3 %select_convert_fusion = bf16[576,1024]{1,0:T(8,128)(2,1)S(1)} fusion(s32[576]{0:T(1024)S(1)} %get-tuple-element.16, s32[576]{0:T(1024)S(1)} %get-tuple-element.15, s32[576]{0:T(1024)S(1)} %get-tuple-element.14, s32[576]{0:T(1024)S(1)} %get-tuple-element.13, s32[576]{0:T(1024)S(1)} %get-tuple-element.11), kind=kLoop, calls=%fused_computation.9 | loop fusion | flops 7077888 | bytes 1191168 | tf_op jit(solution)/shard_map/convert_element_type | solution.py:51
  5.6 3.2 %convert_bitcast_fusion = bf16[128,8,1024]{2,1,0:T(8,128)(2,1)S(1)} fusion(bf16[576,1024]{1,0:T(8,128)(2,1)S(1)} %select_convert_fusion, bf16[576,1024]{1,0:T(8,128)(2,1)S(1)} %multiply_convert_fusion, pred[1024,576]{0,1:T(32,128)(4,1)S(1)} %iota_compare_fusion, pred[1024,576]{0,1:T(32,128)(4,1)S(1)} %iota_compare_fusion.1), kind=kOutput, calls=%fused_computation.22 | convolution fusion | flops 2422865920 | bytes 5636096 | tf_op jit(solution)/shard_map/dot_general | solution.py:49
  8.8 40.9 %all_to_all.17 = bf16[128,8,1024]{2,1,0:T(8,128)(2,1)S(1)} all-to-all(bf16[128,8,1024]{2,1,0:T(8,128)(2,1)S(1)} %convert_bitcast_fusion), channel_id=1, replica_groups=mesh['group'=8,'blk'=16] {'group','blk'}, dimensions={0} | all-to-all | bytes 4194304 | tf_op jit(solution)/shard_map/all_to_all | solution.py:55
  49.7 0.1 slice.28
  49.8 0.1 copy.27
  49.9 0.1 copy.20
  50.1 0.1 gt.15
  50.2 0.1 copy.31
  50.3 0.1 lt.48
  50.4 0.1 copy.30
  50.5 0.1 eq.103
  50.6 3.1 %select_reduce_fusion = f32[1024]{0:T(1024)S(1)} fusion(bf16[128,8,1024]{2,1,0:T(8,128)(2,1)S(1)} %all_to_all.17, s32[1024]{0:T(1024)S(1)} %lt.48, s32[1024]{0:T(1024)S(1)} %eq.103, pred[1024]{0:T(1024)(128)(4,1)S(1)} %gt.15), kind=kOutput, calls=%fused_computation.4 | convolution fusion | flops 2153774080 | bytes 2110464 | tf_op jit(solution)/shard_map/dot_general | solution.py:66
  53.7 0.1 reshape.56
  53.8 13.5 %all_to_all.18 = f32[128,1,128]{2,1,0:T(1,128)S(1)} all-to-all(f32[128,1,128]{2,1,0:T(1,128)S(1)} %bitcast.24), channel_id=1, replica_groups=mesh['group'=8,'blk'=16] {'group','blk'}, dimensions={0} | all-to-all | bytes 131072 | tf_op jit(solution)/shard_map/all_to_all | solution.py:78
  67.3 0.1 broadcast_in_dim.86
  67.4 1.0 %select_reduce_fusion.1 = f32[576]{0:T(1024)} fusion(f32[1024]{0:T(1024)S(1)} %broadcast_in_dim.86, s32[576]{0:T(1024)S(1)} %get-tuple-element.10), kind=kLoop, calls=%fused_computation.8 | loop fusion | flops 1768896 | bytes 8704 | tf_op jit(solution)/shard_map/reduce_sum | solution.py:79
  (10 shorter events, 0.1 us)
Async XLA Ops:
  0.0 4.1 %copy-start = (f32[576,1024]{1,0:T(8,128)S(1)}, f32[576,1024]{1,0:T(8,128)}, u32[]{:S(2)}) copy-start(f32[576,1024]{1,0:T(8,128)} %param.4) | copy-start | bytes 7077892
  0.0 2.9 %copy-start.1 = (s32[576]{0:T(1024)S(1)}, s32[576]{0:T(1024)}, u32[]{:S(2)}) copy-start(s32[576]{0:T(1024)} %param.6) | copy-start | bytes 6916
  0.0 2.9 %copy-start.2 = (s32[576]{0:T(1024)S(1)}, s32[576]{0:T(1024)}, u32[]{:S(2)}) copy-start(s32[576]{0:T(1024)} %param.5) | copy-start | bytes 6916

commit v4 on v2

--- a/solution.py
+++ b/solution.py
@@ -6,7 +6,7 @@
 BLOCK_WIDTH = 4
 BLOCK_CAP = 7
 CHUNK = 8
-META_W = 8
+META_DIGITS = 5
 AXES = ("group", "blk")
 
 
@@ -26,7 +26,9 @@
     devices = lax.axis_size("group") * blocks
     slots = devices * CHUNK
     counts = send_counts[0]
-    cum_ends = jnp.cumsum(counts)
+    groups = counts.shape[0]
+    upto = jnp.arange(groups)[:, None] >= jnp.arange(groups)[None, :]
+    cum_ends = jnp.sum(jnp.where(upto, counts[None, :], 0), axis=1)
     squares = jnp.sum(embeddings * embeddings, axis=1, keepdims=True)
     unit_rows = (embeddings * lax.rsqrt(squares + 1e-06)).astype(jnp.bfloat16)
 
@@ -43,10 +45,11 @@
         picks.astype(jnp.bfloat16), unit_rows, preferred_element_type=jnp.float32
     ).astype(jnp.bfloat16)
 
-    offset = jnp.arange(feat_width, dtype=jnp.int32)[None, :] - rank[:, None] * META_W
-    spread = jnp.zeros((row_count, feat_width), jnp.int32)
+    lanes = 128
+    column = jnp.arange(lanes, dtype=jnp.int32)[None, :]
+    spread = jnp.zeros((row_count, lanes), jnp.int32)
     for t, digit in enumerate(meta_digits(cluster, global_index)):
-        spread = jnp.where(offset == t, digit[:, None], spread)
+        spread = jnp.where(column == t * CHUNK + rank[:, None], digit[:, None], spread)
     to_dest = dest[:, None] == jnp.arange(devices, dtype=jnp.int32)[None, :]
     meta_rows = lax.dot_general(
         to_dest.astype(jnp.bfloat16),
@@ -54,23 +57,22 @@
         (((0,), (0,)), ((), ())),
         preferred_element_type=jnp.float32,
     ).astype(jnp.bfloat16)
-    is_meta = jnp.arange(CHUNK) == CHUNK - 1
-    send = jnp.where(
-        is_meta[None, :, None],
-        meta_rows[:, None, :],
+    send = lax.dynamic_update_slice(
         send_rows.reshape(devices, CHUNK, feat_width),
+        meta_rows.reshape(devices, 1, lanes),
+        (0, CHUNK - 1, 0),
     )
 
     got = lax.all_to_all(send, AXES, 0, 0, tiled=True)
     got_rows = got.reshape(slots, feat_width)
-    coded = got[:, CHUNK - 1, : BLOCK_CAP * META_W].astype(jnp.int32)
-    coded = coded.reshape(devices, BLOCK_CAP, META_W)
-    pad = ((0, 0), (0, CHUNK - BLOCK_CAP))
-    got_valid = jnp.pad(coded[:, :, 0], pad).reshape(slots) > 0
-    got_sub = jnp.pad(coded[:, :, 1], pad).reshape(slots)
-    got_ids = jnp.pad(
-        coded[:, :, 2] * 4096 + coded[:, :, 3] * 64 + coded[:, :, 4], pad
-    ).reshape(slots)
+    coded = got[:, CHUNK - 1, : META_DIGITS * CHUNK].astype(jnp.int32)
+
+    def digit(t):
+        return coded[:, t * CHUNK : (t + 1) * CHUNK].reshape(slots)
+
+    got_valid = digit(0) > 0
+    got_sub = digit(1)
+    got_ids = digit(2) * 4096 + digit(3) * 64 + digit(4)
 
     cosine = lax.dot_general(
         got_rows, got_rows, (((1,), (1,)), ((), ())), preferred_element_type=jnp.float32
@@ -82,7 +84,8 @@
     )
     best = jnp.max(jnp.where(usable, cosine, jnp.float32(-1.0)), axis=1)
 
-    returned = lax.all_to_all(best.reshape(devices, CHUNK), AXES, 0, 0, tiled=True)
+    wide = jnp.pad(best.reshape(devices, CHUNK), ((0, 0), (0, lanes - CHUNK)))
+    returned = lax.all_to_all(wide, AXES, 0, 0, tiled=True)[:, :CHUNK]
     return jnp.sum(jnp.where(picks, returned.reshape(slots, 1), jnp.float32(0.0)), axis=0)
 
 

time: 69.5 us -> 74.3 us (1.069)
  local copies, waits for them, and re-layouts: 1.76 us -> 6.52 us
  other arithmetic: 5.68 us -> 4.48 us
  matrix products: 6.49 us -> 7.56 us
    dynamic_update_slice x0 -> x1, local copies, waits for them, and re-layouts: none -> 5.99 us  [on_device(): lax.dynamic_update_slice(send_rows.reshape(devices, CHUNK, feat_width), m...]
    dot_general x1, matrix products: 1.98 us -> 3.31 us  [on_device(): jnp.dot(picks.astype(jnp.bfloat16), unit_rows, preferred_element_type=jnp...]
    reduce_sum x0 -> x1, other arithmetic: none -> 0.92 us  [on_device(): cum_ends = jnp.sum(jnp.where(upto, counts[None, :], 0), axis=1)]
    another operation x1 -> x0, other arithmetic: 0.83 us -> none
    all_to_all x1 -> x0, other arithmetic: 0.81 us -> none  [on_device(): lax.all_to_all(best.reshape(devices, CHUNK), AXES, 0, 0, tiled=True)]
where the time goes in v4:
time: 74.3 us; the launch traced here: 73.3 us
  blocking collectives  54.6 us (73%)
  matrix products  7.56 us (10%)
  local copies, waits for them, and re-layouts  6.52 us (9%)
  other arithmetic  4.48 us (6%)
    all_to_all x1, blocking collectives, on_device(): got = lax.all_to_all(send, AXES, 0, 0, tiled=True)  41.1 us
    all_to_all x1, blocking collectives, on_device(): returned = lax.all_to_all(wide, AXES, 0, 0, tiled=True)[:, :CHUNK]  13.5 us
    dynamic_update_slice x1, local copies, waits for them, and re-layouts, on_device(): lax.dynamic_update_slice(send_rows.reshape(devices, CHUNK, feat_width), m...  5.99 us
    dot_general x1, matrix products, on_device(): jnp.dot(picks.astype(jnp.bfloat16), unit_rows, preferred_element_type=jnp...  3.31 us
    dot_general x1, matrix products, on_device(): lax.dot_general(got_rows, got_rows, (((1,), (1,)), ((), ())), preferred_e...  3.11 us
    reduce_sum x1, other arithmetic, on_device(): squares = jnp.sum(embeddings * embeddings, axis=1, keepdims=True)  1.91 us

profile of v4, /device:TPU:0, one launch (start us, length us, event | category | flops | bytes accessed | tf_op | source)
XLA Modules:
  0.0 73.3 jit_solution(8254400575616216791)
XLA Ops:
  0.0 0.0 copy-start
  0.0 0.0 copy-start.2
  0.0 0.0 copy-start.1
  0.0 0.9 %select_reduce_fusion.2 = s32[8]{0:T(128)S(1)} fusion(s32[8]{0:T(128)} %bitcast.20), kind=kLoop, calls=%fused_computation.66 | loop fusion | flops 184 | bytes 64 | tf_op jit(solution)/shard_map/reduce_sum | solution.py:31
  0.9 0.1 convert_reduce_fusion.1
  1.0 1.9 %multiply_reduce_fusion = f32[576]{0:T(1024)S(1)} fusion(f32[576,1024]{1,0:T(8,128)} %param.4), kind=kLoop, calls=%fused_computation.3 | loop fusion | flops 1179072 | bytes 2361600 | tf_op jit(solution)/shard_map/reduce_sum | solution.py:32
  2.9 0.0 copy-done.2
  2.9 0.0 copy-done.1
  3.0 0.3 convert_reduce_fusion
  3.3 1.1 %fusion.8 = bf16[128,1,128]{2,0,1:T(8,128)(2,1)S(1)} fusion(s32[576]{0:T(1024)S(1)} %convert_reduce_fusion, s32[576]{0:T(1024)S(1)} %get-tuple-element.15, s32[576]{0:T(1024)S(1)} %get-tuple-element.8, s32[576]{0:T(1024)S(1)} %get-tuple-element.17, s32[576]{0:T(1024)S(1)} %get-tuple-element.9, s32[576]{0:T(1024)S(1)} %get-tuple-element.18, ...), kind=kOutput, calls=%fused_computation.15 | convolution fusion | flops 19775488 | bytes 55808 | tf_op jit(solution)/shard_map/dot_general | solution.py:54
  4.4 0.1 copy.10
  4.5 0.0 copy-done
  4.5 3.3 %convert_bitcast_fusion = bf16[128,8,1024]{2,1,0:T(8,128)(2,1)} fusion(f32[576,1024]{1,0:T(8,128)S(1)} %copy-done, f32[576]{0:T(1024)S(1)} %add_rsqrt_fusion, s32[576]{0:T(1024)S(1)} %get-tuple-element.11), kind=kOutput, calls=%fused_computation.8 | convolution fusion | flops 1210777600 | bytes 4461056 | tf_op jit(solution)/shard_map/dot_general | solution.py:44
  7.8 6.0 %dynamic_update_slice.3 = bf16[128,8,1024]{2,1,0:T(8,128)(2,1)} dynamic-update-slice(bf16[128,8,1024]{2,1,0:T(8,128)(2,1)} %convert_bitcast_fusion, bf16[128,1,128]{2,1,0:T(2,128)(2,1)S(1)} %copy.10, s32[]{:T(128)} %constant.71.clone.1, s32[]{:T(128)} %constant.88.clone.1, s32[]{:T(128)} %constant.71.clone.1) | dynamic-update-slice | bytes 65540 | tf_op jit(solution)/shard_map/dynamic_update_slice | solution.py:60
  13.8 41.1 %all_to_all.17 = bf16[128,8,1024]{2,1,0:T(8,128)(2,1)S(1)} all-to-all(bf16[128,8,1024]{2,1,0:T(8,128)(2,1)} %dynamic_update_slice.3), channel_id=1, replica_groups=mesh['group'=8,'blk'=16] {'group','blk'}, dimensions={0} | all-to-all | bytes 4194304 | tf_op jit(solution)/shard_map/all_to_all | solution.py:66
  54.9 0.1 slice_convert_fusion
  55.0 0.1 fusion.31
  55.2 0.1 gt.15
  55.3 0.1 eq.147
  55.4 0.1 add.117
  55.5 3.1 %select_reduce_fusion = f32[1024]{0:T(1024)S(1)} fusion(bf16[128,8,1024]{2,1,0:T(8,128)(2,1)S(1)} %all_to_all.17, s32[1024]{0:T(1024)S(1)} %add.117, s32[1024]{0:T(1024)S(1)} %eq.147, pred[1024]{0:T(1024)(128)(4,1)S(1)} %gt.15), kind=kOutput, calls=%fused_computation | convolution fusion | flops 2153774080 | bytes 2110464 | tf_op jit(solution)/shard_map/dot_general | solution.py:77
  58.6 0.1 reshape.103
  58.7 13.5 %all_to_all.18 = f32[128,1,128]{2,1,0:T(1,128)S(1)} all-to-all(f32[128,1,128]{2,1,0:T(1,128)S(1)} %bitcast.18), channel_id=1, replica_groups=mesh['group'=8,'blk'=16] {'group','blk'}, dimensions={0} | all-to-all | bytes 131072 | tf_op jit(solution)/shard_map/all_to_all | solution.py:88
  72.2 0.1 broadcast_in_dim.99
  72.3 1.0 %select_reduce_fusion.1 = f32[576]{0:T(1024)} fusion(f32[1024]{0:T(1024)S(1)} %broadcast_in_dim.99, s32[576]{0:T(1024)S(1)} %get-tuple-element.11), kind=kLoop, calls=%fused_computation.1 | loop fusion | flops 1768896 | bytes 8704 | tf_op jit(solution)/shard_map/reduce_sum | solution.py:89
  (5 shorter events, 0.1 us)
Async XLA Ops:
  0.0 4.5 %copy-start = (f32[576,1024]{1,0:T(8,128)S(1)}, f32[576,1024]{1,0:T(8,128)}, u32[]{:S(2)}) copy-start(f32[576,1024]{1,0:T(8,128)} %param.4) | copy-start | bytes 7077892
  0.0 2.9 %copy-start.2 = (s32[576]{0:T(1024)S(1)}, s32[576]{0:T(1024)}, u32[]{:S(2)}) copy-start(s32[576]{0:T(1024)} %param.6) | copy-start | bytes 6916
  0.0 2.9 %copy-start.1 = (s32[576]{0:T(1024)S(1)}, s32[576]{0:T(1024)}, u32[]{:S(2)}) copy-start(s32[576]{0:T(1024)} %param.5) | copy-start | bytes 6916

commit v5 on v4

--- a/solution.py
+++ b/solution.py
@@ -39,12 +39,6 @@
     rank = jnp.sum(earlier.astype(jnp.int32), axis=1)
     slot = dest * CHUNK + rank
 
-    slot_ids = jnp.arange(slots, dtype=jnp.int32)
-    picks = slot_ids[:, None] == slot[None, :]
-    send_rows = jnp.dot(
-        picks.astype(jnp.bfloat16), unit_rows, preferred_element_type=jnp.float32
-    ).astype(jnp.bfloat16)
-
     lanes = 128
     column = jnp.arange(lanes, dtype=jnp.int32)[None, :]
     spread = jnp.zeros((row_count, lanes), jnp.int32)
@@ -57,11 +51,17 @@
         (((0,), (0,)), ((), ())),
         preferred_element_type=jnp.float32,
     ).astype(jnp.bfloat16)
-    send = lax.dynamic_update_slice(
-        send_rows.reshape(devices, CHUNK, feat_width),
-        meta_rows.reshape(devices, 1, lanes),
-        (0, CHUNK - 1, 0),
-    )
+
+    slot_ids = jnp.arange(slots, dtype=jnp.int32)
+    picks = slot_ids[:, None] == slot[None, :]
+    meta_picks = slot_ids[:, None] == (jnp.arange(devices, dtype=jnp.int32) * CHUNK + CHUNK - 1)[None, :]
+    send = jnp.dot(
+        jnp.concatenate([picks, meta_picks], axis=1).astype(jnp.bfloat16),
+        jnp.concatenate(
+            [unit_rows, jnp.pad(meta_rows, ((0, 0), (0, feat_width - lanes)))], axis=0
+        ),
+        preferred_element_type=jnp.float32,
+    ).astype(jnp.bfloat16).reshape(devices, CHUNK, feat_width)
 
     got = lax.all_to_all(send, AXES, 0, 0, tiled=True)
     got_rows = got.reshape(slots, feat_width)

time: 74.3 us -> 67.3 us (0.906)
  local copies, waits for them, and re-layouts: 6.52 us -> 0.48 us
  matrix products: 7.56 us -> 6.09 us
    dynamic_update_slice x1 -> x0, local copies, waits for them, and re-layouts: 5.99 us -> none  [on_device(): lax.dynamic_update_slice(send_rows.reshape(devices, CHUNK, feat_width), m...]
    dot_general x1, matrix products: 3.31 us -> 1.85 us  [on_device(): jnp.dot(jnp.concatenate([picks, meta_picks], axis=1).astype(jnp.bfloat16)...]
where the time goes in v5:
time: 67.3 us; the launch traced here: 66.3 us
  blocking collectives  54.4 us (81%)
  matrix products  6.09 us (9%)
  other arithmetic  5.22 us (8%)
    all_to_all x1, blocking collectives, on_device(): got = lax.all_to_all(send, AXES, 0, 0, tiled=True)  40.9 us
    all_to_all x1, blocking collectives, on_device(): returned = lax.all_to_all(wide, AXES, 0, 0, tiled=True)[:, :CHUNK]  13.5 us
    dot_general x1, matrix products, on_device(): lax.dot_general(got_rows, got_rows, (((1,), (1,)), ((), ())), preferred_e...  3.11 us
    reduce_sum x1, other arithmetic, on_device(): squares = jnp.sum(embeddings * embeddings, axis=1, keepdims=True)  1.91 us
    dot_general x1, matrix products, on_device(): jnp.dot(jnp.concatenate([picks, meta_picks], axis=1).astype(jnp.bfloat16)...  1.85 us

profile of v5, /device:TPU:0, one launch (start us, length us, event | category | flops | bytes accessed | tf_op | source)
XLA Modules:
  0.0 66.3 jit_solution(7581134945280237411)
XLA Ops:
  0.0 0.0 copy-start
  0.0 0.0 copy-start.2
  0.0 0.0 copy-start.1
  0.0 0.9 %select_reduce_fusion.2 = s32[8]{0:T(128)S(1)} fusion(s32[8]{0:T(128)} %bitcast.18), kind=kLoop, calls=%fused_computation.74 | loop fusion | flops 184 | bytes 64 | tf_op jit(solution)/shard_map/reduce_sum | solution.py:31
  0.9 0.1 convert_reduce_fusion.1
  1.0 1.9 %multiply_reduce_fusion = f32[576]{0:T(1024)S(1)} fusion(f32[576,1024]{1,0:T(8,128)} %param.4), kind=kLoop, calls=%fused_computation.9 | loop fusion | flops 1179072 | bytes 2361600 | tf_op jit(solution)/shard_map/reduce_sum | solution.py:32
  2.9 0.0 copy-done.2
  2.9 0.0 copy-done.1
  3.0 0.3 convert_reduce_fusion
  3.3 0.1 iota_compare_fusion.3
  3.4 0.4 iota_compare_fusion.1
  3.8 0.0 copy-done
  3.8 0.2 multiply_convert_fusion
  4.0 1.1 %convolution_convert_fusion = bf16[128,128]{1,0:T(8,128)(2,1)S(1)} fusion(s32[576]{0:T(1024)S(1)} %convert_reduce_fusion, s32[576]{0:T(1024)S(1)} %get-tuple-element.15, s32[576]{0:T(1024)S(1)} %get-tuple-element.8, s32[576]{0:T(1024)S(1)} %get-tuple-element.17, s32[576]{0:T(1024)S(1)} %get-tuple-element.9, s32[576]{0:T(1024)S(1)} %get-tuple-element.18, ...), kind=kOutput, calls=%fused_computation.21 | convolution fusion | flops 19775488 | bytes 55808 | tf_op jit(solution)/shard_map/dot_general | solution.py:48
  5.2 1.9 %convert_bitcast_fusion = bf16[128,8,1024]{2,1,0:T(8,128)(2,1)S(1)} fusion(pred[1024,128]{0,1:T(32,128)(4,1)S(1)} %iota_compare_fusion.3, pred[1024,576]{0,1:T(32,128)(4,1)S(1)} %iota_compare_fusion.1, bf16[128,128]{1,0:T(8,128)(2,1)S(1)} %convolution_convert_fusion, bf16[576,1024]{1,0:T(8,128)(2,1)S(1)} %multiply_convert_fusion), kind=kOutput, calls=%fused_computation.13 | convolution fusion | flops 1482489856 | bytes 4030464 | tf_op jit(solution)/shard_map/dot_general | solution.py:58
  7.0 40.9 %all_to_all.17 = bf16[128,8,1024]{2,1,0:T(8,128)(2,1)S(1)} all-to-all(bf16[128,8,1024]{2,1,0:T(8,128)(2,1)S(1)} %convert_bitcast_fusion), channel_id=1, replica_groups=mesh['group'=8,'blk'=16] {'group','blk'}, dimensions={0} | all-to-all | bytes 4194304 | tf_op jit(solution)/shard_map/all_to_all | solution.py:66
  47.9 0.1 slice_convert_fusion
  48.1 0.1 fusion.44
  48.2 0.1 gt.15
  48.3 0.1 eq.163
  48.4 0.1 add.128
  48.5 3.1 %select_reduce_fusion = f32[1024]{0:T(1024)S(1)} fusion(bf16[128,8,1024]{2,1,0:T(8,128)(2,1)S(1)} %all_to_all.17, s32[1024]{0:T(1024)S(1)} %add.128, s32[1024]{0:T(1024)S(1)} %eq.163, pred[1024]{0:T(1024)(128)(4,1)S(1)} %gt.15), kind=kOutput, calls=%fused_computation | convolution fusion | flops 2153774080 | bytes 2110464 | tf_op jit(solution)/shard_map/dot_general | solution.py:77
  51.6 0.1 reshape.104
  51.7 13.5 %all_to_all.18 = f32[128,1,128]{2,1,0:T(1,128)S(1)} all-to-all(f32[128,1,128]{2,1,0:T(1,128)S(1)} %bitcast.16), channel_id=1, replica_groups=mesh['group'=8,'blk'=16] {'group','blk'}, dimensions={0} | all-to-all | bytes 131072 | tf_op jit(solution)/shard_map/all_to_all | solution.py:88
  65.2 0.1 broadcast_in_dim.101
  65.3 1.0 %select_reduce_fusion.1 = f32[576]{0:T(1024)} fusion(f32[1024]{0:T(1024)S(1)} %broadcast_in_dim.101, s32[576]{0:T(1024)S(1)} %get-tuple-element.11), kind=kLoop, calls=%fused_computation.7 | loop fusion | flops 1768896 | bytes 8704 | tf_op jit(solution)/shard_map/reduce_sum | solution.py:89
  (6 shorter events, 0.1 us)
Async XLA Ops:
  0.0 3.8 %copy-start = (f32[576,1024]{1,0:T(8,128)S(1)}, f32[576,1024]{1,0:T(8,128)}, u32[]{:S(2)}) copy-start(f32[576,1024]{1,0:T(8,128)} %param.4) | copy-start | bytes 7077892
  0.0 2.9 %copy-start.2 = (s32[576]{0:T(1024)S(1)}, s32[576]{0:T(1024)}, u32[]{:S(2)}) copy-start(s32[576]{0:T(1024)} %param.6) | copy-start | bytes 6916
  0.0 2.9 %copy-start.1 = (s32[576]{0:T(1024)S(1)}, s32[576]{0:T(1024)}, u32[]{:S(2)}) copy-start(s32[576]{0:T(1024)} %param.5) | copy-start | bytes 6916

commit v6 on v5

--- a/solution.py
+++ b/solution.py
@@ -1,6 +1,8 @@
 import jax
 import jax.numpy as jnp
 from jax import lax
+from jax.experimental import pallas as pl
+from jax.experimental.pallas import tpu as pltpu
 from jax.sharding import PartitionSpec as P
 
 BLOCK_WIDTH = 4
@@ -20,6 +22,34 @@
     )
 
 
+def pack_kernel(x_ref, slot_ref, meta_ref, out_ref):
+    x = x_ref[...]
+    squares = jnp.sum(x * x, axis=1, keepdims=True)
+    unit = (x * lax.rsqrt(squares + 1e-06)).astype(jnp.bfloat16)
+    slots = out_ref.shape[0]
+    lanes = meta_ref.shape[1]
+    slot_at = lax.broadcasted_iota(jnp.int32, (slots, slot_ref.shape[1]), 0)
+    picks = (slot_at == slot_ref[...]).astype(jnp.bfloat16)
+    rows = jnp.dot(picks, unit, preferred_element_type=jnp.float32)
+    out_ref[...] = rows.astype(jnp.bfloat16)
+    meta_at = lax.broadcasted_iota(jnp.int32, (slots, meta_ref.shape[0]), 0)
+    chunk_of = lax.broadcasted_iota(jnp.int32, (slots, meta_ref.shape[0]), 1)
+    meta_picks = (meta_at == chunk_of * CHUNK + CHUNK - 1).astype(jnp.bfloat16)
+    meta = jnp.dot(meta_picks, meta_ref[...], preferred_element_type=jnp.float32)
+    out_ref[:, :lanes] = (rows[:, :lanes] + meta).astype(jnp.bfloat16)
+
+
+def pack(embeddings, slot, meta_rows, slots):
+    vmem = pltpu.MemorySpace.VMEM
+    return pl.pallas_call(
+        pack_kernel,
+        out_shape=jax.ShapeDtypeStruct((slots, embeddings.shape[1]), jnp.bfloat16),
+        in_specs=[pl.BlockSpec(memory_space=vmem)] * 3,
+        out_specs=pl.BlockSpec(memory_space=vmem),
+        compiler_params=pltpu.CompilerParams(vmem_limit_bytes=48 * 1024 * 1024),
+    )(embeddings, slot.reshape(1, -1), meta_rows)
+
+
 def on_device(embeddings, cluster, global_index, send_counts):
     row_count, feat_width = embeddings.shape
     blocks = lax.axis_size("blk")
@@ -29,8 +59,6 @@
     groups = counts.shape[0]
     upto = jnp.arange(groups)[:, None] >= jnp.arange(groups)[None, :]
     cum_ends = jnp.sum(jnp.where(upto, counts[None, :], 0), axis=1)
-    squares = jnp.sum(embeddings * embeddings, axis=1, keepdims=True)
-    unit_rows = (embeddings * lax.rsqrt(squares + 1e-06)).astype(jnp.bfloat16)
 
     position = jnp.arange(row_count, dtype=jnp.int32)
     owner_group = jnp.sum((position[:, None] >= cum_ends[None, :]).astype(jnp.int32), axis=1)
@@ -52,16 +80,9 @@
         preferred_element_type=jnp.float32,
     ).astype(jnp.bfloat16)
 
+    send = pack(embeddings, slot, meta_rows, slots).reshape(devices, CHUNK, feat_width)
     slot_ids = jnp.arange(slots, dtype=jnp.int32)
     picks = slot_ids[:, None] == slot[None, :]
-    meta_picks = slot_ids[:, None] == (jnp.arange(devices, dtype=jnp.int32) * CHUNK + CHUNK - 1)[None, :]
-    send = jnp.dot(
-        jnp.concatenate([picks, meta_picks], axis=1).astype(jnp.bfloat16),
-        jnp.concatenate(
-            [unit_rows, jnp.pad(meta_rows, ((0, 0), (0, feat_width - lanes)))], axis=0
-        ),
-        preferred_element_type=jnp.float32,
-    ).astype(jnp.bfloat16).reshape(devices, CHUNK, feat_width)
 
     got = lax.all_to_all(send, AXES, 0, 0, tiled=True)
     got_rows = got.reshape(slots, feat_width)

time: 67.3 us -> 67 us (level)
  other arithmetic: 5.22 us -> 3.12 us
  Pallas kernels: 0 us -> 2 us
  matrix products: 6.09 us -> 4.24 us
  local copies, waits for them, and re-layouts: 0.48 us -> 2.13 us
    pallas_call x0 -> x1, Pallas kernels: none -> 2 us  [pack(): pl.pallas_call(pack_kernel, out_shape=jax.ShapeDtypeStruct((slots, embedd...]
    reduce_sum x1 -> x0, other arithmetic: 1.91 us -> none  [on_device(): squares = jnp.sum(embeddings * embeddings, axis=1, keepdims=True)]
    dot_general x1 -> x0, matrix products: 1.85 us -> none  [on_device(): jnp.dot(jnp.concatenate([picks, meta_picks], axis=1).astype(jnp.bfloat16)...]
    unnamed x6 -> x2, local copies, waits for them, and re-layouts: 0.01 us -> 1.66 us
    select_n x1, other arithmetic: 0.02 us -> 0.73 us  [meta_digits(): cluster % BLOCK_WIDTH]
where the time goes in v6:
time: 67 us; the launch traced here: 66 us
  blocking collectives  54.4 us (81%)
  matrix products  4.24 us (6%)
  other arithmetic  3.12 us (5%)
  local copies, waits for them, and re-layouts  2.13 us (3%)
  Pallas kernels  2 us (3%)
    all_to_all x1, blocking collectives, on_device(): got = lax.all_to_all(send, AXES, 0, 0, tiled=True)  40.9 us
    all_to_all x1, blocking collectives, on_device(): returned = lax.all_to_all(wide, AXES, 0, 0, tiled=True)[:, :CHUNK]  13.5 us
    dot_general x1, matrix products, on_device(): lax.dot_general(got_rows, got_rows, (((1,), (1,)), ((), ())), preferred_e...  3.11 us
    pallas_call x1, Pallas kernels, pack(): pl.pallas_call(pack_kernel, out_shape=jax.ShapeDtypeStruct((slots, embedd...  2 us
    unnamed x2, local copies, waits for them, and re-layouts  1.66 us

profile of v6, /device:TPU:0, one launch (start us, length us, event | category | flops | bytes accessed | tf_op | source)
XLA Modules:
  0.0 66.0 jit_solution(5116926796353324331)
XLA Ops:
  0.0 0.8 %select_reduce_fusion.2 = s32[8]{0:T(128)S(1)} fusion(s32[8]{0:T(128)} %bitcast.18), kind=kLoop, calls=%fused_computation.58 | loop fusion | flops 184 | bytes 64 | tf_op jit(solution)/shard_map/reduce_sum | solution.py:61
  0.8 0.1 convert_reduce_fusion.1
  0.9 0.7 %add_select_fusion = (s32[576]{0:T(1024)S(1)}, s32[576]{0:T(1024)S(1)}, s32[576]{0:T(1024)S(1)}, s32[576]{0:T(1024)S(1)}, s32[576]{0:T(1024)S(1)}) fusion(s32[576]{0:T(1024)} %param.5, s32[576]{0:T(1024)S(1)} %convert_reduce_fusion.1, s32[576]{0:T(1024)} %param.6), kind=kLoop, calls=%fused_computation.36 | loop fusion | flops 35136 | bytes 18432 | tf_op jit(solution)/shard_map/jit(remainder)/select_n | solution.py:18
  1.6 0.3 convert_reduce_fusion
  1.9 1.1 %convolution_convert_fusion.meta_ref = bf16[128,128]{1,0:T(8,128)(2,1)S(1)} fusion(s32[576]{0:T(1024)S(1)} %convert_reduce_fusion, s32[576]{0:T(1024)S(1)} %get-tuple-element.15, s32[576]{0:T(1024)S(1)} %get-tuple-element.8, s32[576]{0:T(1024)S(1)} %get-tuple-element.17, s32[576]{0:T(1024)S(1)} %get-tuple-element.9, s32[576]{0:T(1024)S(1)} %get-tuple-element.18, ...), kind=kOutput, calls=%fused_computation.8 | convolution fusion | flops 19775488 | bytes 55808 | tf_op jit(solution)/shard_map/dot_general | solution.py:76
  3.0 0.0 copy-start
  3.0 1.7 %copy-done = f32[576,1024]{1,0:T(8,128)S(1)} copy-done((f32[576,1024]{1,0:T(8,128)S(1)}, f32[576,1024]{1,0:T(8,128)}, u32[]{:S(2)}) %copy-start) | copy-done | bytes 2359320
  4.7 2.0 %shard_map.46 = bf16[1024,1024]{1,0:T(8,128)(2,1)S(1)} custom-call(f32[576,1024]{1,0:T(8,128)S(1)} %copy-done, s32[1,576]{1,0:T(1,128)S(1)} %broadcast_in_dim.93.slot_ref, bf16[128,128]{1,0:T(8,128)(2,1)S(1)} %convolution_convert_fusion.meta_ref), custom_call_target="tpu_custom_call" | custom-call | tf_op jit(solution)/shard_map/pallas_call | solution.py:44
  6.7 40.9 %all_to_all.17 = bf16[128,8,1024]{2,1,0:T(8,128)(2,1)S(1)} all-to-all(bf16[128,8,1024]{2,1,0:T(8,128)(2,1)S(1)} %bitcast.13), channel_id=1, replica_groups=mesh['group'=8,'blk'=16] {'group','blk'}, dimensions={0} | all-to-all | bytes 4194304 | tf_op jit(solution)/shard_map/all_to_all | solution.py:87
  47.6 0.1 slice_convert_fusion
  47.7 0.1 fusion.27
  47.9 0.1 gt.15
  48.0 0.1 eq.147
  48.1 0.1 add.104
  48.2 3.1 %select_reduce_fusion = f32[1024]{0:T(1024)S(1)} fusion(bf16[128,8,1024]{2,1,0:T(8,128)(2,1)S(1)} %all_to_all.17, s32[1024]{0:T(1024)S(1)} %add.104, s32[1024]{0:T(1024)S(1)} %eq.147, pred[1024]{0:T(1024)(128)(4,1)S(1)} %gt.15), kind=kOutput, calls=%fused_computation | convolution fusion | flops 2153774080 | bytes 2110464 | tf_op jit(solution)/shard_map/dot_general | solution.py:98
  51.3 0.1 reshape.94
  51.4 13.5 %all_to_all.18 = f32[128,1,128]{2,1,0:T(1,128)S(1)} all-to-all(f32[128,1,128]{2,1,0:T(1,128)S(1)} %bitcast.16), channel_id=1, replica_groups=mesh['group'=8,'blk'=16] {'group','blk'}, dimensions={0} | all-to-all | bytes 131072 | tf_op jit(solution)/shard_map/all_to_all | solution.py:109
  64.9 0.1 broadcast_in_dim.101
  65.0 1.0 %select_reduce_fusion.1 = f32[576]{0:T(1024)} fusion(f32[1024]{0:T(1024)S(1)} %broadcast_in_dim.101, s32[576]{0:T(1024)S(1)} %get-tuple-element.11), kind=kLoop, calls=%fused_computation.1 | loop fusion | flops 1768896 | bytes 8704 | tf_op jit(solution)/shard_map/reduce_sum | solution.py:110
  (4 shorter events, 0.0 us)
Async XLA Ops:
  3.0 1.7 %copy-start = (f32[576,1024]{1,0:T(8,128)S(1)}, f32[576,1024]{1,0:T(8,128)}, u32[]{:S(2)}) copy-start(f32[576,1024]{1,0:T(8,128)} %x_ref.1) | copy-start | bytes 7077892

commit v7 on v6

v7 whole, which is shorter than its diff:
```python
import jax
import jax.numpy as jnp
from jax import lax
from jax.experimental import pallas as pl
from jax.experimental.pallas import tpu as pltpu
from jax.sharding import PartitionSpec as P

BLOCK_WIDTH = 4
BLOCK_CAP = 7
CHUNK = 8
META_DIGITS = 5
AXES = ("group", "blk")
LANES = 128


def meta_digits(cluster, global_index):
    return (
        jnp.ones_like(cluster),
        cluster % BLOCK_WIDTH,
        global_index // 4096,
        (global_index // 64) % 64,
        global_index % 64,
    )


def pack_kernel(x_hbm, idx_ref, cols_ref, out_ref, x_buf, unit_buf, sems):
    pieces = sems.shape[0]
    piece = x_buf.shape[0] // pieces
    copies = [
        pltpu.make_async_copy(
            x_hbm.at[pl.ds(j * piece, piece)], x_buf.at[pl.ds(j * piece, piece)], sems.at[j]
        )
        for j in range(pieces)
    ]
    for copy in copies:
        copy.start()
    for j, copy in enumerate(copies):
        copy.wait()
        x = x_buf[pl.ds(j * piece, piece), :]
        squares = jnp.sum(x * x, axis=1, keepdims=True)
        unit_buf[pl.ds(j * piece, piece), :] = (x * lax.rsqrt(squares + 1e-06)).astype(jnp.bfloat16)

    row_count = x_buf.shape[0]
    slots = out_ref.shape[0]
    devices = slots // CHUNK
    lanes = 128
    slot_at = lax.broadcasted_iota(jnp.int32, (slots, row_count), 0)
    picks = (slot_at == idx_ref[0:1, :]).astype(jnp.bfloat16)
    rows = jnp.dot(picks, unit_buf[...], preferred_element_type=jnp.float32)

    dest_at = lax.broadcasted_iota(jnp.int32, (devices, row_count), 0)
    to_dest = (dest_at == idx_ref[1:2, :]).astype(jnp.bfloat16)
    cols = cols_ref[...]
    column = lax.broadcasted_iota(jnp.int32, (row_count, lanes), 1)
    spread = jnp.zeros((row_count, lanes), jnp.int32)
    for t in range(META_DIGITS):
        spread = jnp.where(column == t * CHUNK + cols[:, 0:1], cols[:, t + 1 : t + 2], spread)
    meta_rows = jnp.dot(to_dest, spread.astype(jnp.bfloat16), preferred_element_type=jnp.float32)
    meta_at = lax.broadcasted_iota(jnp.int32, (slots, devices), 0)
    chunk_of = lax.broadcasted_iota(jnp.int32, (slots, devices), 1)
    meta_picks = (meta_at == chunk_of * CHUNK + CHUNK - 1).astype(jnp.bfloat16)
    meta = jnp.dot(meta_picks, meta_rows.astype(jnp.bfloat16), preferred_element_type=jnp.float32)
    out_ref[...] = rows.astype(jnp.bfloat16)
    out_ref[:, :lanes] = (rows[:, :lanes] + meta).astype(jnp.bfloat16)


def pack(embeddings, slot, dest, rank, digits, slots):
    row_count, feat_width = embeddings.shape
    vmem = pltpu.MemorySpace.VMEM
    unused = jnp.zeros_like(slot)
    index_rows = jnp.stack([slot, dest] + [unused] * 6, axis=0)
    cols = jnp.stack([rank, *digits] + [unused] * (7 - len(digits)), axis=1)
    return pl.pallas_call(
        pack_kernel,
        out_shape=jax.ShapeDtypeStruct((slots, feat_width), jnp.bfloat16),
        in_specs=[
            pl.BlockSpec(memory_space=pl.ANY),
            pl.BlockSpec(memory_space=vmem),
            pl.BlockSpec(memory_space=vmem),
        ],
        out_specs=pl.BlockSpec(memory_space=vmem),
        scratch_shapes=[
            pltpu.VMEM((row_count, feat_width), jnp.float32),
            pltpu.VMEM((row_count, feat_width), jnp.bfloat16),
            pltpu.SemaphoreType.DMA((4,)),
        ],
        compiler_params=pltpu.CompilerParams(vmem_limit_bytes=48 * 1024 * 1024),
    )(embeddings, index_rows, cols)


def on_device(embeddings, cluster, global_index, send_counts):
    row_count, feat_width = embeddings.shape
    blocks = lax.axis_size("blk")
    devices = lax.axis_size("group") * blocks
    slots = devices * CHUNK
    counts = send_counts[0]
    groups = counts.shape[0]
    upto = jnp.arange(groups)[:, None] >= jnp.arange(groups)[None, :]
    cum_ends = jnp.sum(jnp.where(upto, counts[None, :], 0), axis=1)

    position = jnp.arange(row_count, dtype=jnp.int32)
    owner_group = jnp.sum((position[:, None] >= cum_ends[None, :]).astype(jnp.int32), axis=1)
    dest = owner_group * blocks + cluster // BLOCK_WIDTH
    earlier = (dest[:, None] == dest[None, :]) & (position[None, :] < position[:, None])
    rank = jnp.sum(earlier.astype(jnp.int32), axis=1)
    slot = dest * CHUNK + rank

    send = pack(
        embeddings, slot, dest, rank, meta_digits(cluster, global_index), slots
    ).reshape(devices, CHUNK, feat_width)
    slot_ids = jnp.arange(slots, dtype=jnp.int32)
    picks = slot_ids[:, None] == slot[None, :]

    got = lax.all_to_all(send, AXES, 0, 0, tiled=True)
    got_rows = got.reshape(slots, feat_width)
    coded = got[:, CHUNK - 1, : META_DIGITS * CHUNK].astype(jnp.int32)

    def digit(t):
        return coded[:, t * CHUNK : (t + 1) * CHUNK].reshape(slots)

    got_valid = digit(0) > 0
    got_sub = digit(1)
    got_ids = digit(2) * 4096 + digit(3) * 64 + digit(4)

    cosine = lax.dot_general(
        got_rows, got_rows, (((1,), (1,)), ((), ())), preferred_element_type=jnp.float32
    )
    usable = (
        got_valid[None, :]
        & (got_sub[:, None] == got_sub[None, :])
        & (got_ids[None, :] < got_ids[:, None])
    )
    best = jnp.max(jnp.where(usable, cosine, jnp.float32(-1.0)), axis=1)

    wide = jnp.pad(best.reshape(devices, CHUNK), ((0, 0), (0, LANES - CHUNK)))
    returned = lax.all_to_all(wide, AXES, 0, 0, tiled=True)[:, :CHUNK]
    return jnp.sum(jnp.where(picks, returned.reshape(slots, 1), jnp.float32(0.0)), axis=0)


def solution(mesh):
    placed = (
        P(AXES, None),
        P(AXES),
        P(AXES),
        P(AXES, None),
    )
    return jax.shard_map(
        on_device, mesh=mesh, in_specs=placed, out_specs=P(AXES), check_vma=False
    )
```

time: 67 us -> 68.2 us (1.018)
  Pallas kernels: 2 us -> 3.15 us
  matrix products: 4.24 us -> 3.12 us
  other arithmetic: 3.12 us -> 3.87 us
    pallas_call x1, Pallas kernels: 2 us -> 3.15 us  [pack(): pl.pallas_call(pack_kernel, out_shape=jax.ShapeDtypeStruct((slots, feat_w...]
    dot_general x1 -> x0, matrix products: 1.13 us -> none  [on_device(): lax.dot_general(to_dest.astype(jnp.bfloat16), spread.astype(jnp.bfloat16)...]
    select_n x0 -> x1, other arithmetic: none -> 0.7 us  [meta_digits(): global_index % 64]
where the time goes in v7:
time: 68.2 us; the launch traced here: 67.2 us
  blocking collectives  54.4 us (80%)
  other arithmetic  3.87 us (6%)
  Pallas kernels  3.15 us (5%)
  matrix products  3.12 us (5%)
  local copies, waits for them, and re-layouts  2.51 us (4%)
    all_to_all x1, blocking collectives, on_device(): got = lax.all_to_all(send, AXES, 0, 0, tiled=True)  40.9 us
    all_to_all x1, blocking collectives, on_device(): returned = lax.all_to_all(wide, AXES, 0, 0, tiled=True)[:, :CHUNK]  13.5 us
    pallas_call x1, Pallas kernels, pack(): pl.pallas_call(pack_kernel, out_shape=jax.ShapeDtypeStruct((slots, feat_w...  3.15 us
    dot_general x1, matrix products, on_device(): lax.dot_general(got_rows, got_rows, (((1,), (1,)), ((), ())), preferred_e...  3.12 us
    unnamed x2, local copies, waits for them, and re-layouts  1.67 us

profile of v7, /device:TPU:0, one launch (start us, length us, event | category | flops | bytes accessed | tf_op | source)
XLA Modules:
  0.0 67.2 jit_solution(14899280674365726124)
XLA Ops:
  0.0 0.8 %select_reduce_fusion.2 = s32[8]{0:T(128)S(1)} fusion(s32[8]{0:T(128)} %bitcast.18), kind=kLoop, calls=%fused_computation.39 | loop fusion | flops 184 | bytes 64 | tf_op jit(solution)/shard_map/reduce_sum | solution.py:99
  0.8 0.1 convert_reduce_fusion.1
  0.9 0.7 %add_select_fusion.4 = (s32[576]{0:T(1024)S(1)}, s32[576]{0:T(1024)S(1)}) fusion(s32[576]{0:T(1024)} %param.5, s32[576]{0:T(1024)S(1)} %convert_reduce_fusion.1), kind=kLoop, calls=%fused_computation.28 | loop fusion | flops 12096 | bytes 9216 | tf_op jit(solution)/shard_map/jit(remainder)/select_n | solution.py:19
  1.6 0.3 convert_reduce_fusion
  1.9 0.1 pad.8.clone
  1.9 0.1 pad.7.clone
  2.0 0.7 %add_select_fusion = (s32[576]{0:T(1024)S(1)}, s32[576]{0:T(1024)S(1)}, s32[576]{0:T(1024)S(1)}) fusion(s32[576]{0:T(1024)} %param.6), kind=kLoop, calls=%fused_computation.17 | loop fusion | flops 23040 | bytes 9216 | tf_op jit(solution)/shard_map/jit(remainder)/select_n | solution.py:22
  2.8 0.1 copy.18.cols_ref
  3.0 0.1 add_add_fusion.idx_ref
  3.1 0.0 copy-start
  3.1 1.7 %copy-done = f32[576,1024]{1,0:T(8,128)S(1)} copy-done((f32[576,1024]{1,0:T(8,128)S(1)}, f32[576,1024]{1,0:T(8,128)}, u32[]{:S(2)}) %copy-start) | copy-done | bytes 2359320
  4.7 3.1 %shard_map.46 = bf16[1024,1024]{1,0:T(8,128)(2,1)S(1)} custom-call(f32[576,1024]{1,0:T(8,128)S(1)} %copy-done, s32[8,576]{1,0:T(8,128)S(1)} %add_add_fusion.idx_ref, s32[576,8]{1,0:T(8,128)S(1)} %copy.18.cols_ref), custom_call_target="tpu_custom_call" | custom-call | tf_op jit(solution)/shard_map/pallas_call | solution.py:73
  7.9 40.9 %all_to_all.17 = bf16[128,8,1024]{2,1,0:T(8,128)(2,1)S(1)} all-to-all(bf16[128,8,1024]{2,1,0:T(8,128)(2,1)S(1)} %bitcast.13), channel_id=1, replica_groups=mesh['group'=8,'blk'=16] {'group','blk'}, dimensions={0} | all-to-all | bytes 4194304 | tf_op jit(solution)/shard_map/all_to_all | solution.py:114
  48.8 0.1 slice_convert_fusion
  48.9 0.1 fusion.13
  49.1 0.1 gt.15
  49.2 0.1 eq.51
  49.3 0.1 add.58
  49.4 3.1 %select_reduce_fusion = f32[1024]{0:T(1024)S(1)} fusion(bf16[128,8,1024]{2,1,0:T(8,128)(2,1)S(1)} %all_to_all.17, s32[1024]{0:T(1024)S(1)} %add.58, s32[1024]{0:T(1024)S(1)} %eq.51, pred[1024]{0:T(1024)(128)(4,1)S(1)} %gt.15), kind=kOutput, calls=%fused_computation | convolution fusion | flops 2153774080 | bytes 2110464 | tf_op jit(solution)/shard_map/dot_general | solution.py:125
  52.5 0.1 reshape.72
  52.6 13.5 %all_to_all.18 = f32[128,1,128]{2,1,0:T(1,128)S(1)} all-to-all(f32[128,1,128]{2,1,0:T(1,128)S(1)} %bitcast.16), channel_id=1, replica_groups=mesh['group'=8,'blk'=16] {'group','blk'}, dimensions={0} | all-to-all | bytes 131072 | tf_op jit(solution)/shard_map/all_to_all | solution.py:136
  66.1 0.1 broadcast_in_dim.55
  66.2 1.0 %select_reduce_fusion.1 = f32[576]{0:T(1024)} fusion(f32[1024]{0:T(1024)S(1)} %broadcast_in_dim.55, s32[576]{0:T(1024)S(1)} %multiply_add_fusion), kind=kLoop, calls=%fused_computation.1 | loop fusion | flops 1768896 | bytes 8704 | tf_op jit(solution)/shard_map/reduce_sum | solution.py:137
  (15 shorter events, 0.1 us)
Async XLA Ops:
  3.1 1.7 %copy-start = (f32[576,1024]{1,0:T(8,128)S(1)}, f32[576,1024]{1,0:T(8,128)}, u32[]{:S(2)}) copy-start(f32[576,1024]{1,0:T(8,128)} %x_hbm.1) | copy-start | bytes 7077892

commit v8 on v6

--- a/solution.py
+++ b/solution.py
@@ -10,6 +10,7 @@
 CHUNK = 8
 META_DIGITS = 5
 AXES = ("group", "blk")
+LANES = 128
 
 
 def meta_digits(cluster, global_index):
@@ -22,32 +23,40 @@
     )
 
 
-def pack_kernel(x_ref, slot_ref, meta_ref, out_ref):
+def pack_kernel(x_ref, idx_ref, cols_ref, out_ref):
     x = x_ref[...]
     squares = jnp.sum(x * x, axis=1, keepdims=True)
     unit = (x * lax.rsqrt(squares + 1e-06)).astype(jnp.bfloat16)
+    row_count = x_ref.shape[0]
     slots = out_ref.shape[0]
-    lanes = meta_ref.shape[1]
-    slot_at = lax.broadcasted_iota(jnp.int32, (slots, slot_ref.shape[1]), 0)
-    picks = (slot_at == slot_ref[...]).astype(jnp.bfloat16)
+    slot_at = lax.broadcasted_iota(jnp.int32, (slots, row_count), 0)
+    picks = (slot_at == idx_ref[0:1, :]).astype(jnp.bfloat16)
     rows = jnp.dot(picks, unit, preferred_element_type=jnp.float32)
     out_ref[...] = rows.astype(jnp.bfloat16)
-    meta_at = lax.broadcasted_iota(jnp.int32, (slots, meta_ref.shape[0]), 0)
-    chunk_of = lax.broadcasted_iota(jnp.int32, (slots, meta_ref.shape[0]), 1)
-    meta_picks = (meta_at == chunk_of * CHUNK + CHUNK - 1).astype(jnp.bfloat16)
-    meta = jnp.dot(meta_picks, meta_ref[...], preferred_element_type=jnp.float32)
-    out_ref[:, :lanes] = (rows[:, :lanes] + meta).astype(jnp.bfloat16)
+
+    cols = cols_ref[...]
+    column = lax.broadcasted_iota(jnp.int32, (row_count, LANES), 1)
+    spread = jnp.zeros((row_count, LANES), jnp.int32)
+    for t in range(META_DIGITS):
+        spread = jnp.where(column == t * CHUNK + cols[:, 0:1], cols[:, t + 1 : t + 2], spread)
+    meta_picks = (slot_at == idx_ref[1:2, :]).astype(jnp.bfloat16)
+    meta = jnp.dot(meta_picks, spread.astype(jnp.bfloat16), preferred_element_type=jnp.float32)
+    out_ref[:, :LANES] = (rows[:, :LANES] + meta).astype(jnp.bfloat16)
 
 
-def pack(embeddings, slot, meta_rows, slots):
+def pack(embeddings, slot, meta_slot, rank, digits, slots):
+    row_count, feat_width = embeddings.shape
     vmem = pltpu.MemorySpace.VMEM
+    unused = jnp.zeros_like(slot)
+    index_rows = jnp.stack([slot, meta_slot] + [unused] * 6, axis=0)
+    cols = jnp.stack([rank, *digits] + [unused] * (7 - len(digits)), axis=1)
     return pl.pallas_call(
         pack_kernel,
-        out_shape=jax.ShapeDtypeStruct((slots, embeddings.shape[1]), jnp.bfloat16),
+        out_shape=jax.ShapeDtypeStruct((slots, feat_width), jnp.bfloat16),
         in_specs=[pl.BlockSpec(memory_space=vmem)] * 3,
         out_specs=pl.BlockSpec(memory_space=vmem),
         compiler_params=pltpu.CompilerParams(vmem_limit_bytes=48 * 1024 * 1024),
-    )(embeddings, slot.reshape(1, -1), meta_rows)
+    )(embeddings, index_rows, cols)
 
 
 def on_device(embeddings, cluster, global_index, send_counts):
@@ -67,20 +76,9 @@
     rank = jnp.sum(earlier.astype(jnp.int32), axis=1)
     slot = dest * CHUNK + rank
 
-    lanes = 128
-    column = jnp.arange(lanes, dtype=jnp.int32)[None, :]
-    spread = jnp.zeros((row_count, lanes), jnp.int32)
-    for t, digit in enumerate(meta_digits(cluster, global_index)):
-        spread = jnp.where(column == t * CHUNK + rank[:, None], digit[:, None], spread)
-    to_dest = dest[:, None] == jnp.arange(devices, dtype=jnp.int32)[None, :]
-    meta_rows = lax.dot_general(
-        to_dest.astype(jnp.bfloat16),
-        spread.astype(jnp.bfloat16),
-        (((0,), (0,)), ((), ())),
-        preferred_element_type=jnp.float32,
-    ).astype(jnp.bfloat16)
-
-    send = pack(embeddings, slot, meta_rows, slots).reshape(devices, CHUNK, feat_width)
+    send = pack(
+        embeddings, slot, dest * CHUNK + CHUNK - 1, rank, meta_digits(cluster, global_index), slots
+    ).reshape(devices, CHUNK, feat_width)
     slot_ids = jnp.arange(slots, dtype=jnp.int32)
     picks = slot_ids[:, None] == slot[None, :]
 
@@ -105,7 +103,7 @@
     )
     best = jnp.max(jnp.where(usable, cosine, jnp.float32(-1.0)), axis=1)
 
-    wide = jnp.pad(best.reshape(devices, CHUNK), ((0, 0), (0, lanes - CHUNK)))
+    wide = jnp.pad(best.reshape(devices, CHUNK), ((0, 0), (0, LANES - CHUNK)))
     returned = lax.all_to_all(wide, AXES, 0, 0, tiled=True)[:, :CHUNK]
     return jnp.sum(jnp.where(picks, returned.reshape(slots, 1), jnp.float32(0.0)), axis=0)
 

time: 67 us -> 67.4 us (level)
  matrix products: 4.24 us -> 3.12 us
  other arithmetic: 3.12 us -> 3.88 us
    dot_general x1 -> x0, matrix products: 1.13 us -> none  [on_device(): lax.dot_general(to_dest.astype(jnp.bfloat16), spread.astype(jnp.bfloat16)...]
    sub x0 -> x1, other arithmetic: none -> 0.7 us  [on_device(): dest * CHUNK + CHUNK - 1]
where the time goes in v8:
time: 67.4 us; the launch traced here: 66.4 us
  blocking collectives  54.4 us (81%)
  other arithmetic  3.88 us (6%)
  matrix products  3.12 us (5%)
  local copies, waits for them, and re-layouts  2.51 us (4%)
  Pallas kernels  2.33 us (3%)
    all_to_all x1, blocking collectives, on_device(): got = lax.all_to_all(send, AXES, 0, 0, tiled=True)  40.9 us
    all_to_all x1, blocking collectives, on_device(): returned = lax.all_to_all(wide, AXES, 0, 0, tiled=True)[:, :CHUNK]  13.5 us
    dot_general x1, matrix products, on_device(): lax.dot_general(got_rows, got_rows, (((1,), (1,)), ((), ())), preferred_e...  3.12 us
    pallas_call x1, Pallas kernels, pack(): pl.pallas_call(pack_kernel, out_shape=jax.ShapeDtypeStruct((slots, feat_w...  2.33 us
    unnamed x2, local copies, waits for them, and re-layouts  1.67 us

profile of v8, /device:TPU:0, one launch (start us, length us, event | category | flops | bytes accessed | tf_op | source)
XLA Modules:
  0.0 66.4 jit_solution(11298603855641021332)
XLA Ops:
  0.0 0.8 %select_reduce_fusion.2 = s32[8]{0:T(128)S(1)} fusion(s32[8]{0:T(128)} %bitcast.18), kind=kLoop, calls=%fused_computation.38 | loop fusion | flops 184 | bytes 64 | tf_op jit(solution)/shard_map/reduce_sum | solution.py:70
  0.8 0.1 convert_reduce_fusion.1
  0.9 0.7 %multiply_add_fusion = (s32[576]{0:T(1024)S(1)}, s32[576]{0:T(1024)S(1)}, s32[576]{0:T(1024)S(1)}) fusion(s32[576]{0:T(1024)} %param.5, s32[576]{0:T(1024)S(1)} %convert_reduce_fusion.1), kind=kLoop, calls=%fused_computation.42 | loop fusion | flops 13248 | bytes 11520 | tf_op jit(solution)/shard_map/sub | solution.py:80
  1.6 0.3 convert_reduce_fusion
  1.9 0.1 pad.8.clone
  1.9 0.1 pad.7.clone
  2.0 0.7 %add_select_fusion = (s32[576]{0:T(1024)S(1)}, s32[576]{0:T(1024)S(1)}, s32[576]{0:T(1024)S(1)}) fusion(s32[576]{0:T(1024)} %param.6), kind=kLoop, calls=%fused_computation.17 | loop fusion | flops 23040 | bytes 9216 | tf_op jit(solution)/shard_map/jit(remainder)/select_n | solution.py:22
  2.8 0.1 copy.18.cols_ref
  3.0 0.1 add_add_fusion.idx_ref
  3.1 0.0 copy-start
  3.1 1.7 %copy-done = f32[576,1024]{1,0:T(8,128)S(1)} copy-done((f32[576,1024]{1,0:T(8,128)S(1)}, f32[576,1024]{1,0:T(8,128)}, u32[]{:S(2)}) %copy-start) | copy-done | bytes 2359320
  4.7 2.3 %shard_map.46 = bf16[1024,1024]{1,0:T(8,128)(2,1)S(1)} custom-call(f32[576,1024]{1,0:T(8,128)S(1)} %copy-done, s32[8,576]{1,0:T(8,128)S(1)} %add_add_fusion.idx_ref, s32[576,8]{1,0:T(8,128)S(1)} %copy.18.cols_ref), custom_call_target="tpu_custom_call" | custom-call | tf_op jit(solution)/shard_map/pallas_call | solution.py:53
  7.1 40.9 %all_to_all.17 = bf16[128,8,1024]{2,1,0:T(8,128)(2,1)S(1)} all-to-all(bf16[128,8,1024]{2,1,0:T(8,128)(2,1)S(1)} %bitcast.13), channel_id=1, replica_groups=mesh['group'=8,'blk'=16] {'group','blk'}, dimensions={0} | all-to-all | bytes 4194304 | tf_op jit(solution)/shard_map/all_to_all | solution.py:85
  48.0 0.1 slice_convert_fusion
  48.1 0.1 fusion.14
  48.3 0.1 gt.15
  48.4 0.1 eq.51
  48.5 0.1 add.62
  48.6 3.1 %select_reduce_fusion = f32[1024]{0:T(1024)S(1)} fusion(bf16[128,8,1024]{2,1,0:T(8,128)(2,1)S(1)} %all_to_all.17, s32[1024]{0:T(1024)S(1)} %add.62, s32[1024]{0:T(1024)S(1)} %eq.51, pred[1024]{0:T(1024)(128)(4,1)S(1)} %gt.15), kind=kOutput, calls=%fused_computation | convolution fusion | flops 2153774080 | bytes 2110464 | tf_op jit(solution)/shard_map/dot_general | solution.py:96
  51.7 0.1 reshape.72
  51.8 13.5 %all_to_all.18 = f32[128,1,128]{2,1,0:T(1,128)S(1)} all-to-all(f32[128,1,128]{2,1,0:T(1,128)S(1)} %bitcast.16), channel_id=1, replica_groups=mesh['group'=8,'blk'=16] {'group','blk'}, dimensions={0} | all-to-all | bytes 131072 | tf_op jit(solution)/shard_map/all_to_all | solution.py:107
  65.3 0.1 broadcast_in_dim.52
  65.4 1.0 %select_reduce_fusion.1 = f32[576]{0:T(1024)} fusion(f32[1024]{0:T(1024)S(1)} %broadcast_in_dim.52, s32[576]{0:T(1024)S(1)} %multiply_add_fusion.1), kind=kLoop, calls=%fused_computation.1 | loop fusion | flops 1768896 | bytes 8704 | tf_op jit(solution)/shard_map/reduce_sum | solution.py:108
  (15 shorter events, 0.1 us)
Async XLA Ops:
  3.1 1.7 %copy-start = (f32[576,1024]{1,0:T(8,128)S(1)}, f32[576,1024]{1,0:T(8,128)}, u32[]{:S(2)}) copy-start(f32[576,1024]{1,0:T(8,128)} %x_ref.1) | copy-start | bytes 7077892

commit v9 on v8

v9 whole, which is shorter than its diff:
```python
import functools

import jax
import jax.numpy as jnp
from jax import lax
from jax.experimental import pallas as pl
from jax.experimental.pallas import tpu as pltpu
from jax.sharding import PartitionSpec as P

BLOCK_WIDTH = 4
BLOCK_CAP = 7
CHUNK = 8
META_DIGITS = 5
AXES = ("group", "blk")
LANES = 128


def pack_kernel(blocks, counts_ref, cl_row_ref, cl_col_ref, gi_col_ref, x_ref, out_ref, slot_ref):
    row_count = x_ref.shape[0]
    slots = out_ref.shape[0]
    pos_row = lax.broadcasted_iota(jnp.int32, (1, row_count), 1)
    pos_col = lax.broadcasted_iota(jnp.int32, (row_count, 1), 0)
    owner_row = jnp.zeros((1, row_count), jnp.int32)
    owner_col = jnp.zeros((row_count, 1), jnp.int32)
    end = counts_ref[0]
    for g in range(1, counts_ref.shape[0] + 1):
        owner_row = owner_row + (pos_row >= end).astype(jnp.int32)
        owner_col = owner_col + (pos_col >= end).astype(jnp.int32)
        if g < counts_ref.shape[0]:
            end = end + counts_ref[g]
    cl_row = cl_row_ref[...]
    cl_col = cl_col_ref[...]
    dest_row = owner_row * blocks + lax.shift_right_logical(cl_row, 2)
    dest_col = owner_col * blocks + lax.shift_right_logical(cl_col, 2)
    same = dest_col == dest_row
    rank_row = jnp.sum((same & (pos_col < pos_row)).astype(jnp.int32), axis=0, keepdims=True)
    rank_col = jnp.sum((same & (pos_row < pos_col)).astype(jnp.int32), axis=1, keepdims=True)
    slot_row = dest_row * CHUNK + rank_row
    slot_ref[...] = slot_row

    x = x_ref[...]
    squares = jnp.sum(x * x, axis=1, keepdims=True)
    unit = (x * lax.rsqrt(squares + 1e-06)).astype(jnp.bfloat16)
    slot_at = lax.broadcasted_iota(jnp.int32, (slots, row_count), 0)
    picks = (slot_at == slot_row).astype(jnp.bfloat16)
    rows = jnp.dot(picks, unit, preferred_element_type=jnp.float32)
    out_ref[...] = rows.astype(jnp.bfloat16)

    gi_col = gi_col_ref[...]
    digits = (
        jnp.ones_like(cl_col),
        cl_col & (BLOCK_WIDTH - 1),
        lax.shift_right_logical(gi_col, 12),
        lax.shift_right_logical(gi_col, 6) & 63,
        gi_col & 63,
    )
    column = lax.broadcasted_iota(jnp.int32, (row_count, LANES), 1)
    spread = jnp.zeros((row_count, LANES), jnp.int32)
    for t, digit in enumerate(digits):
        spread = jnp.where(column == t * CHUNK + rank_col, digit, spread)
    meta_picks = (slot_at == dest_row * CHUNK + CHUNK - 1).astype(jnp.bfloat16)
    meta = jnp.dot(meta_picks, spread.astype(jnp.bfloat16), preferred_element_type=jnp.float32)
    out_ref[:, :LANES] = (rows[:, :LANES] + meta).astype(jnp.bfloat16)


def pack(embeddings, cluster, global_index, counts, blocks, slots):
    row_count, feat_width = embeddings.shape
    vmem = pltpu.MemorySpace.VMEM
    return pl.pallas_call(
        functools.partial(pack_kernel, blocks),
        out_shape=(
            jax.ShapeDtypeStruct((slots, feat_width), jnp.bfloat16),
            jax.ShapeDtypeStruct((1, row_count), jnp.int32),
        ),
        in_specs=[pl.BlockSpec(memory_space=pltpu.MemorySpace.SMEM)]
        + [pl.BlockSpec(memory_space=vmem)] * 4,
        out_specs=(pl.BlockSpec(memory_space=vmem), pl.BlockSpec(memory_space=vmem)),
        compiler_params=pltpu.CompilerParams(vmem_limit_bytes=48 * 1024 * 1024),
    )(
        counts,
        cluster.reshape(1, row_count),
        cluster.reshape(row_count, 1),
        global_index.reshape(row_count, 1),
        embeddings,
    )


def on_device(embeddings, cluster, global_index, send_counts):
    row_count, feat_width = embeddings.shape
    blocks = lax.axis_size("blk")
    devices = lax.axis_size("group") * blocks
    slots = devices * CHUNK
    send, slot = pack(embeddings, cluster, global_index, send_counts[0], blocks, slots)
    send = send.reshape(devices, CHUNK, feat_width)
    slot_ids = jnp.arange(slots, dtype=jnp.int32)
    picks = slot_ids[:, None] == slot

    got = lax.all_to_all(send, AXES, 0, 0, tiled=True)
    got_rows = got.reshape(slots, feat_width)
    coded = got[:, CHUNK - 1, : META_DIGITS * CHUNK].astype(jnp.int32)

    def digit(t):
        return coded[:, t * CHUNK : (t + 1) * CHUNK].reshape(slots)

    got_valid = digit(0) > 0
    got_sub = digit(1)
    got_ids = digit(2) * 4096 + digit(3) * 64 + digit(4)

    cosine = lax.dot_general(
        got_rows, got_rows, (((1,), (1,)), ((), ())), preferred_element_type=jnp.float32
    )
    usable = (
        got_valid[None, :]
        & (got_sub[:, None] == got_sub[None, :])
        & (got_ids[None, :] < got_ids[:, None])
    )
    best = jnp.max(jnp.where(usable, cosine, jnp.float32(-1.0)), axis=1)

    wide = jnp.pad(best.reshape(devices, CHUNK), ((0, 0), (0, LANES - CHUNK)))
    returned = lax.all_to_all(wide, AXES, 0, 0, tiled=True)[:, :CHUNK]
    return jnp.sum(jnp.where(picks, returned.reshape(slots, 1), jnp.float32(0.0)), axis=0)


def solution(mesh):
    placed = (
        P(AXES, None),
        P(AXES),
        P(AXES),
        P(AXES, None),
    )
    return jax.shard_map(
        on_device, mesh=mesh, in_specs=placed, out_specs=P(AXES), check_vma=False
    )
```

time: 67.4 us -> 69.6 us (1.033)
  blocking collectives: 54.4 us -> 40.9 us
  waiting for transfers between devices: 0 us -> 9.38 us
  starting transfers between devices: 0 us -> 4.61 us
  local copies, waits for them, and re-layouts: 2.51 us -> 5.73 us
  other arithmetic: 3.88 us -> 1.28 us
  Pallas kernels: 2.33 us -> 3.41 us
    all_to_all x1 -> x0, blocking collectives: 13.5 us -> none  [on_device(): returned = lax.all_to_all(wide, AXES, 0, 0, tiled=True)[:, :CHUNK]]
    all_to_all x0 -> x1, waiting for transfers between devices: none -> 9.38 us  [on_device(): returned = lax.all_to_all(wide, AXES, 0, 0, tiled=True)[:, :CHUNK]]
    all_to_all x0 -> x1, starting transfers between devices: none -> 4.61 us  [on_device(): returned = lax.all_to_all(wide, AXES, 0, 0, tiled=True)[:, :CHUNK]]
    reshape x0 -> x3, local copies, waits for them, and re-layouts: none -> 2.32 us  [the longest x1 0.82 us: pack(): cluster.reshape(row_count, 1)]
    reduce_sum x3 -> x0, other arithmetic: 1.13 us -> none  [the longest x1 0.77 us: on_device(): cum_ends = jnp.sum(jnp.where(upto, counts[None, :], 0), axis=1)]
    pallas_call x1, Pallas kernels: 2.33 us -> 3.41 us  [pack(): pl.pallas_call(functools.partial(pack_kernel, blocks), out_shape=(jax.Sha...]
    select_n x1 -> x0, other arithmetic: 0.71 us -> none  [meta_digits(): global_index % 64]
    sub x1 -> x0, other arithmetic: 0.7 us -> none  [on_device(): dest * CHUNK + CHUNK - 1]
  transfers between devices with their start and end apart: 0 -> 1, of which waited for: 0 -> 1; matrix products, arithmetic and copies ran while one was open for 0% -> 0% of each run, Pallas kernels for 0% -> 0%
where the time goes in v9:
time: 69.6 us; the launch traced here: 68.5 us
  blocking collectives  40.9 us (59%)
  waiting for transfers between devices  9.38 us (13%)
  local copies, waits for them, and re-layouts  5.73 us (8%)
  starting transfers between devices  4.61 us (7%)
  Pallas kernels  3.41 us (5%)
  matrix products  3.13 us (4%)
  other arithmetic  1.28 us (2%)
    all_to_all x1, blocking collectives, on_device(): got = lax.all_to_all(send, AXES, 0, 0, tiled=True)  40.9 us
    all_to_all x1, waiting for transfers between devices, on_device(): returned = lax.all_to_all(wide, AXES, 0, 0, tiled=True)[:, :CHUNK]  9.38 us
    all_to_all x1, starting transfers between devices, on_device(): returned = lax.all_to_all(wide, AXES, 0, 0, tiled=True)[:, :CHUNK]  4.61 us
    pallas_call x1, Pallas kernels, pack(): pl.pallas_call(functools.partial(pack_kernel, blocks), out_shape=(jax.Sha...  3.41 us
    dot_general x1, matrix products, on_device(): lax.dot_general(got_rows, got_rows, (((1,), (1,)), ((), ())), preferred_e...  3.13 us
    unnamed x4, local copies, waits for them, and re-layouts  2.32 us
  transfers between devices with their start and end apart: 1, of which 1 were waited for; matrix products, arithmetic and copies ran while one was open for 0% of the time, Pallas kernels for 0%

profile of v9, /device:TPU:0, one launch (start us, length us, event | category | flops | bytes accessed | tf_op | source)
XLA Modules:
  0.0 68.5 jit_solution(17624324639173187851)
XLA Ops:
  0.0 0.8 %reshape.82.cl_col_ref = s32[576,1]{1,0:T(8,128)S(1)} reshape(s32[576]{0:T(1024)} %param.5) | data formatting | bytes 4608 | tf_op jit(solution)/shard_map/reshape | solution.py:82
  0.8 0.7 %reshape.75.cl_row_ref = s32[1,576]{1,0:T(1,128)S(1)} reshape(s32[576]{0:T(1024)} %param.5) | data formatting | bytes 4608 | tf_op jit(solution)/shard_map/reshape | solution.py:81
  1.5 0.8 %reshape.83.gi_col_ref = s32[576,1]{1,0:T(8,128)S(1)} reshape(s32[576]{0:T(1024)} %param.6) | data formatting | bytes 4608 | tf_op jit(solution)/shard_map/reshape | solution.py:83
  2.3 0.0 copy-start
  2.4 1.7 %copy-done = f32[576,1024]{1,0:T(8,128)S(1)} copy-done((f32[576,1024]{1,0:T(8,128)S(1)}, f32[576,1024]{1,0:T(8,128)}, u32[]{:S(2)}) %copy-start) | copy-done | bytes 2359320
  4.0 0.0 copy-start.1
  4.0 0.7 copy-done.1
  4.7 3.4 %shard_map.46 = (bf16[1024,1024]{1,0:T(8,128)(2,1)S(1)}, s32[1,576]{1,0:T(1,128)S(1)}) custom-call(s32[8]{0:T(128)S(1)} %bitcast.14, s32[1,576]{1,0:T(1,128)S(1)} %reshape.75.cl_row_ref, s32[576,1]{1,0:T(8,128)S(1)} %reshape.82.cl_col_ref, s32[576,1]{1,0:T(8,128)S(1)} %reshape.83.gi_col_ref, f32[576,1024]{1,0:T(8,128)S(1)} %copy-done), custom_call_target="tpu_custom_call" | custom-call | tf_op jit(solution)/shard_map/pallas_call | solution.py:69
  8.1 40.9 %all_to_all.17 = bf16[128,8,1024]{2,1,0:T(8,128)(2,1)S(1)} all-to-all(bf16[128,8,1024]{2,1,0:T(8,128)(2,1)S(1)} %bitcast.13), channel_id=1, replica_groups=mesh['group'=8,'blk'=16] {'group','blk'}, dimensions={0} | all-to-all | bytes 4194304 | tf_op jit(solution)/shard_map/all_to_all | solution.py:98
  49.0 0.1 slice_convert_fusion
  49.1 0.1 fusion.5
  49.3 0.1 add.30
  49.4 0.1 eq.34
  49.5 0.1 gt.15
  49.6 3.1 %select_reduce_fusion = f32[1024]{0:T(1024)S(1)} fusion(bf16[128,8,1024]{2,1,0:T(8,128)(2,1)S(1)} %all_to_all.17, s32[1024]{0:T(1024)S(1)} %add.30, s32[1024]{0:T(1024)S(1)} %eq.34, pred[1024]{0:T(1024)(128)(4,1)S(1)} %gt.15), kind=kOutput, calls=%fused_computation | convolution fusion | flops 2153774080 | bytes 2110464 | tf_op jit(solution)/shard_map/dot_general | solution.py:109
  52.7 0.1 reshape.80
  52.8 0.6 pad.4
  53.4 4.6 %all-to-all-start.1 = ((f32[128,1,128]{2,1,0:T(1,128)}), f32[128,1,128]{2,1,0:T(1,128)S(1)}, u32[]{:S(2)}, u32[]{:S(2)}) async-start(f32[128,1,128]{2,1,0:T(1,128)} %bitcast.5), calls=%async_computation.1 | async-start | bytes 131072 | tf_op jit(solution)/shard_map/all_to_all | solution.py:120
  58.0 9.4 %all-to-all-done.1 = f32[128,1,128]{2,1,0:T(1,128)S(1)} async-done(((f32[128,1,128]{2,1,0:T(1,128)}), f32[128,1,128]{2,1,0:T(1,128)S(1)}, u32[]{:S(2)}, u32[]{:S(2)}) %all-to-all-start.1) | async-done | bytes 65568 | tf_op jit(solution)/shard_map/all_to_all | solution.py:120
  67.4 0.1 broadcast_in_dim.23
  67.5 1.0 %select_reduce_fusion.1 = f32[576]{0:T(1024)} fusion(f32[1024]{0:T(1024)S(1)} %broadcast_in_dim.23, s32[576]{0:T(1024)S(1)} %reduce), kind=kLoop, calls=%fused_computation.1 | loop fusion | flops 1768896 | bytes 8704 | tf_op jit(solution)/shard_map/reduce_sum | solution.py:121
  (2 shorter events, 0.0 us)
Async XLA Ops:
  2.3 1.7 %copy-start = (f32[576,1024]{1,0:T(8,128)S(1)}, f32[576,1024]{1,0:T(8,128)}, u32[]{:S(2)}) copy-start(f32[576,1024]{1,0:T(8,128)} %x_ref.1) | copy-start | bytes 7077892
  4.0 0.7 copy-start.1
  53.4 14.0 %all-to-all-start.1 = ((f32[128,1,128]{2,1,0:T(1,128)}), f32[128,1,128]{2,1,0:T(1,128)S(1)}, u32[]{:S(2)}, u32[]{:S(2)}) async-start(f32[128,1,128]{2,1,0:T(1,128)} %bitcast.5), calls=%async_computation.1 | async-start | bytes 131072 | tf_op jit(solution)/shard_map/all_to_all | solution.py:120

commit v10 on v9

--- a/solution.py
+++ b/solution.py
@@ -15,7 +15,7 @@
 LANES = 128
 
 
-def pack_kernel(blocks, counts_ref, cl_row_ref, cl_col_ref, gi_col_ref, x_ref, out_ref, slot_ref):
+def pack_kernel(blocks, counts_ref, cl_ref, gi_ref, x_ref, out_ref, slot_ref):
     row_count = x_ref.shape[0]
     slots = out_ref.shape[0]
     pos_row = lax.broadcasted_iota(jnp.int32, (1, row_count), 1)
@@ -28,8 +28,11 @@
         owner_col = owner_col + (pos_col >= end).astype(jnp.int32)
         if g < counts_ref.shape[0]:
             end = end + counts_ref[g]
-    cl_row = cl_row_ref[...]
-    cl_col = cl_col_ref[...]
+    on_diag = pos_col == pos_row
+    cl_row = cl_ref[...].reshape(1, row_count)
+    gi_row = gi_ref[...].reshape(1, row_count)
+    cl_col = jnp.sum(jnp.where(on_diag, cl_row, 0), axis=1, keepdims=True)
+    gi_col = jnp.sum(jnp.where(on_diag, gi_row, 0), axis=1, keepdims=True)
     dest_row = owner_row * blocks + lax.shift_right_logical(cl_row, 2)
     dest_col = owner_col * blocks + lax.shift_right_logical(cl_col, 2)
     same = dest_col == dest_row
@@ -46,7 +49,6 @@
     rows = jnp.dot(picks, unit, preferred_element_type=jnp.float32)
     out_ref[...] = rows.astype(jnp.bfloat16)
 
-    gi_col = gi_col_ref[...]
     digits = (
         jnp.ones_like(cl_col),
         cl_col & (BLOCK_WIDTH - 1),
@@ -73,14 +75,13 @@
             jax.ShapeDtypeStruct((1, row_count), jnp.int32),
         ),
         in_specs=[pl.BlockSpec(memory_space=pltpu.MemorySpace.SMEM)]
-        + [pl.BlockSpec(memory_space=vmem)] * 4,
+        + [pl.BlockSpec(memory_space=vmem)] * 3,
         out_specs=(pl.BlockSpec(memory_space=vmem), pl.BlockSpec(memory_space=vmem)),
         compiler_params=pltpu.CompilerParams(vmem_limit_bytes=48 * 1024 * 1024),
     )(
         counts,
-        cluster.reshape(1, row_count),
-        cluster.reshape(row_count, 1),
-        global_index.reshape(row_count, 1),
+        cluster,
+        global_index,
         embeddings,
     )
 

time: 69.6 us -> 68.9 us (0.990)
  local copies, waits for them, and re-layouts: 5.73 us -> 4.78 us
    reshape x3 -> x0, local copies, waits for them, and re-layouts: 2.32 us -> none  [the longest x1 0.82 us: pack(): cluster.reshape(row_count, 1)]
    unnamed x4 -> x8, local copies, waits for them, and re-layouts: 2.32 us -> 3.69 us
where the time goes in v10:
time: 68.9 us; the launch traced here: 67.8 us
  blocking collectives  40.9 us (59%)
  waiting for transfers between devices  9.38 us (14%)
  local copies, waits for them, and re-layouts  4.78 us (7%)
  starting transfers between devices  4.61 us (7%)
  Pallas kernels  3.71 us (5%)
  matrix products  3.12 us (5%)
  other arithmetic  1.28 us (2%)
    all_to_all x1, blocking collectives, on_device(): got = lax.all_to_all(send, AXES, 0, 0, tiled=True)  40.9 us
    all_to_all x1, waiting for transfers between devices, on_device(): returned = lax.all_to_all(wide, AXES, 0, 0, tiled=True)[:, :CHUNK]  9.38 us
    all_to_all x1, starting transfers between devices, on_device(): returned = lax.all_to_all(wide, AXES, 0, 0, tiled=True)[:, :CHUNK]  4.61 us
    pallas_call x1, Pallas kernels, pack(): pl.pallas_call(functools.partial(pack_kernel, blocks), out_shape=(jax.Sha...  3.71 us
    unnamed x8, local copies, waits for them, and re-layouts  3.69 us
    dot_general x1, matrix products, on_device(): lax.dot_general(got_rows, got_rows, (((1,), (1,)), ((), ())), preferred_e...  3.12 us
  transfers between devices with their start and end apart: 1, of which 1 were waited for; matrix products, arithmetic and copies ran while one was open for 0% of the time, Pallas kernels for 0%

profile of v10, /device:TPU:0, one launch (start us, length us, event | category | flops | bytes accessed | tf_op | source)
XLA Modules:
  0.0 67.8 jit_solution(4348204360889526217)
XLA Ops:
  0.0 0.0 copy-start
  0.0 1.7 %copy-done = f32[576,1024]{1,0:T(8,128)S(1)} copy-done((f32[576,1024]{1,0:T(8,128)S(1)}, f32[576,1024]{1,0:T(8,128)}, u32[]{:S(2)}) %copy-start) | copy-done | bytes 2359320
  1.7 0.0 copy-start.1
  1.7 0.7 %copy-done.1 = s32[576]{0:T(1024)S(1)} copy-done((s32[576]{0:T(1024)S(1)}, s32[576]{0:T(1024)}, u32[]{:S(2)}) %copy-start.1) | copy-done | bytes 2328
  2.4 0.0 copy-start.2
  2.4 0.7 %copy-done.2 = s32[576]{0:T(1024)S(1)} copy-done((s32[576]{0:T(1024)S(1)}, s32[576]{0:T(1024)}, u32[]{:S(2)}) %copy-start.2) | copy-done | bytes 2328
  3.0 0.0 copy-start.3
  3.0 0.7 copy-done.3
  3.7 3.7 %shard_map.46 = (bf16[1024,1024]{1,0:T(8,128)(2,1)S(1)}, s32[1,576]{1,0:T(1,128)S(1)}) custom-call(s32[8]{0:T(128)S(1)} %bitcast.14, s32[576]{0:T(1024)S(1)} %copy-done.1, s32[576]{0:T(1024)S(1)} %copy-done.2, f32[576,1024]{1,0:T(8,128)S(1)} %copy-done), custom_call_target="tpu_custom_call" | custom-call | tf_op jit(solution)/shard_map/pallas_call | solution.py:71
  7.4 40.9 %all_to_all.17 = bf16[128,8,1024]{2,1,0:T(8,128)(2,1)S(1)} all-to-all(bf16[128,8,1024]{2,1,0:T(8,128)(2,1)S(1)} %bitcast.13), channel_id=1, replica_groups=mesh['group'=8,'blk'=16] {'group','blk'}, dimensions={0} | all-to-all | bytes 4194304 | tf_op jit(solution)/shard_map/all_to_all | solution.py:99
  48.3 0.1 slice_convert_fusion
  48.4 0.1 fusion.5
  48.6 0.1 add.30
  48.7 0.1 eq.34
  48.8 0.1 gt.15
  48.9 3.1 %select_reduce_fusion = f32[1024]{0:T(1024)S(1)} fusion(bf16[128,8,1024]{2,1,0:T(8,128)(2,1)S(1)} %all_to_all.17, s32[1024]{0:T(1024)S(1)} %add.30, s32[1024]{0:T(1024)S(1)} %eq.34, pred[1024]{0:T(1024)(128)(4,1)S(1)} %gt.15), kind=kOutput, calls=%fused_computation | convolution fusion | flops 2153774080 | bytes 2110464 | tf_op jit(solution)/shard_map/dot_general | solution.py:110
  52.0 0.1 reshape.68
  52.1 0.6 pad.4
  52.7 4.6 %all-to-all-start.1 = ((f32[128,1,128]{2,1,0:T(1,128)}), f32[128,1,128]{2,1,0:T(1,128)S(1)}, u32[]{:S(2)}, u32[]{:S(2)}) async-start(f32[128,1,128]{2,1,0:T(1,128)} %bitcast.5), calls=%async_computation.1 | async-start | bytes 131072 | tf_op jit(solution)/shard_map/all_to_all | solution.py:121
  57.4 9.4 %all-to-all-done.1 = f32[128,1,128]{2,1,0:T(1,128)S(1)} async-done(((f32[128,1,128]{2,1,0:T(1,128)}), f32[128,1,128]{2,1,0:T(1,128)S(1)}, u32[]{:S(2)}, u32[]{:S(2)}) %all-to-all-start.1) | async-done | bytes 65568 | tf_op jit(solution)/shard_map/all_to_all | solution.py:121
  66.7 0.1 broadcast_in_dim.23
  66.8 1.0 %select_reduce_fusion.1 = f32[576]{0:T(1024)} fusion(f32[1024]{0:T(1024)S(1)} %broadcast_in_dim.23, s32[576]{0:T(1024)S(1)} %reduce), kind=kLoop, calls=%fused_computation.1 | loop fusion | flops 1768896 | bytes 8704 | tf_op jit(solution)/shard_map/reduce_sum | solution.py:122
  (2 shorter events, 0.0 us)
Async XLA Ops:
  0.0 1.7 %copy-start = (f32[576,1024]{1,0:T(8,128)S(1)}, f32[576,1024]{1,0:T(8,128)}, u32[]{:S(2)}) copy-start(f32[576,1024]{1,0:T(8,128)} %x_ref.1) | copy-start | bytes 7077892
  1.7 0.7 %copy-start.1 = (s32[576]{0:T(1024)S(1)}, s32[576]{0:T(1024)}, u32[]{:S(2)}) copy-start(s32[576]{0:T(1024)} %cl_ref.1) | copy-start | bytes 6916
  2.4 0.7 %copy-start.2 = (s32[576]{0:T(1024)S(1)}, s32[576]{0:T(1024)}, u32[]{:S(2)}) copy-start(s32[576]{0:T(1024)} %gi_ref.1) | copy-start | bytes 6916
  3.0 0.7 copy-start.3
  52.7 14.0 %all-to-all-start.1 = ((f32[128,1,128]{2,1,0:T(1,128)}), f32[128,1,128]{2,1,0:T(1,128)S(1)}, u32[]{:S(2)}, u32[]{:S(2)}) async-start(f32[128,1,128]{2,1,0:T(1,128)} %bitcast.5), calls=%async_computation.1 | async-start | bytes 131072 | tf_op jit(solution)/shard_map/all_to_all | solution.py:121

commit v11 on v8

--- a/solution.py
+++ b/solution.py
@@ -64,7 +64,12 @@
     blocks = lax.axis_size("blk")
     devices = lax.axis_size("group") * blocks
     slots = devices * CHUNK
-    counts = send_counts[0]
+    small = lax.optimization_barrier(
+        jnp.concatenate([cluster, global_index, send_counts[0]])
+    )
+    cluster = small[:row_count]
+    global_index = small[row_count : 2 * row_count]
+    counts = small[2 * row_count :]
     groups = counts.shape[0]
     upto = jnp.arange(groups)[:, None] >= jnp.arange(groups)[None, :]
     cum_ends = jnp.sum(jnp.where(upto, counts[None, :], 0), axis=1)

time: 67.4 us -> 66.4 us (0.985)
  other arithmetic: 3.88 us -> 2.08 us
  local copies, waits for them, and re-layouts: 2.51 us -> 3.29 us
    concatenate x0 -> x1, local copies, waits for them, and re-layouts: none -> 0.78 us  [on_device(): jnp.concatenate([cluster, global_index, send_counts[0]])]
    sub x1, other arithmetic: 0.7 us -> 0.01 us  [on_device(): dest * CHUNK + CHUNK - 1]
where the time goes in v11:
time: 66.4 us; the launch traced here: 65.4 us
  blocking collectives  54.4 us (82%)
  local copies, waits for them, and re-layouts  3.29 us (5%)
  matrix products  3.12 us (5%)
  Pallas kernels  2.33 us (4%)
  other arithmetic  2.08 us (3%)
    all_to_all x1, blocking collectives, on_device(): got = lax.all_to_all(send, AXES, 0, 0, tiled=True)  40.9 us
    all_to_all x1, blocking collectives, on_device(): returned = lax.all_to_all(wide, AXES, 0, 0, tiled=True)[:, :CHUNK]  13.5 us
    dot_general x1, matrix products, on_device(): lax.dot_general(got_rows, got_rows, (((1,), (1,)), ((), ())), preferred_e...  3.12 us
    pallas_call x1, Pallas kernels, pack(): pl.pallas_call(pack_kernel, out_shape=jax.ShapeDtypeStruct((slots, feat_w...  2.33 us
    unnamed x2, local copies, waits for them, and re-layouts  1.67 us

profile of v11, /device:TPU:0, one launch (start us, length us, event | category | flops | bytes accessed | tf_op | source)
XLA Modules:
  0.0 65.4 jit_solution(16833807830035076037)
XLA Ops:
  0.0 0.8 %concatenate.3 = s32[1160]{0:T(1024)S(1)} concatenate(s32[576]{0:T(1024)} %param.5, s32[576]{0:T(1024)} %param.6, s32[8]{0:T(128)} %bitcast.18), dimensions={0} | concatenate | bytes 9280 | tf_op jit(solution)/shard_map/concatenate | solution.py:68
  0.8 0.1 add_select_fusion
  0.9 0.1 select_reduce_fusion.2
  1.0 0.1 convert_reduce_fusion.1
  1.1 0.1 add_select_fusion.1
  1.2 0.1 add_select_fusion.4
  1.2 0.3 convert_reduce_fusion
  1.6 0.1 pad.8.clone
  1.6 0.1 pad.7.clone
  1.8 0.1 copy.18.cols_ref
  2.0 0.1 add_add_fusion.idx_ref
  2.1 0.0 copy-start
  2.1 1.7 %copy-done = f32[576,1024]{1,0:T(8,128)S(1)} copy-done((f32[576,1024]{1,0:T(8,128)S(1)}, f32[576,1024]{1,0:T(8,128)}, u32[]{:S(2)}) %copy-start) | copy-done | bytes 2359320
  3.7 2.3 %shard_map.46 = bf16[1024,1024]{1,0:T(8,128)(2,1)S(1)} custom-call(f32[576,1024]{1,0:T(8,128)S(1)} %copy-done, s32[8,576]{1,0:T(8,128)S(1)} %add_add_fusion.idx_ref, s32[576,8]{1,0:T(8,128)S(1)} %copy.18.cols_ref), custom_call_target="tpu_custom_call" | custom-call | tf_op jit(solution)/shard_map/pallas_call | solution.py:53
  6.1 40.9 %all_to_all.17 = bf16[128,8,1024]{2,1,0:T(8,128)(2,1)S(1)} all-to-all(bf16[128,8,1024]{2,1,0:T(8,128)(2,1)S(1)} %bitcast.13), channel_id=1, replica_groups=mesh['group'=8,'blk'=16] {'group','blk'}, dimensions={0} | all-to-all | bytes 4194304 | tf_op jit(solution)/shard_map/all_to_all | solution.py:90
  47.0 0.1 slice_convert_fusion
  47.1 0.1 fusion.15
  47.2 0.1 gt.15
  47.4 0.1 eq.51
  47.4 0.1 add.62
  47.5 3.1 %select_reduce_fusion = f32[1024]{0:T(1024)S(1)} fusion(bf16[128,8,1024]{2,1,0:T(8,128)(2,1)S(1)} %all_to_all.17, s32[1024]{0:T(1024)S(1)} %add.62, s32[1024]{0:T(1024)S(1)} %eq.51, pred[1024]{0:T(1024)(128)(4,1)S(1)} %gt.15), kind=kOutput, calls=%fused_computation | convolution fusion | flops 2153774080 | bytes 2110464 | tf_op jit(solution)/shard_map/dot_general | solution.py:101
  50.7 0.1 reshape.73
  50.8 13.5 %all_to_all.18 = f32[128,1,128]{2,1,0:T(1,128)S(1)} all-to-all(f32[128,1,128]{2,1,0:T(1,128)S(1)} %bitcast.16), channel_id=1, replica_groups=mesh['group'=8,'blk'=16] {'group','blk'}, dimensions={0} | all-to-all | bytes 131072 | tf_op jit(solution)/shard_map/all_to_all | solution.py:112
  64.3 0.1 broadcast_in_dim.50
  64.4 1.0 %select_reduce_fusion.1 = f32[576]{0:T(1024)} fusion(f32[1024]{0:T(1024)S(1)} %broadcast_in_dim.50, s32[576]{0:T(1024)S(1)} %multiply_add_fusion.1), kind=kLoop, calls=%fused_computation.1 | loop fusion | flops 1768896 | bytes 8704 | tf_op jit(solution)/shard_map/reduce_sum | solution.py:113
  (17 shorter events, 0.1 us)
Async XLA Ops:
  2.1 1.7 %copy-start = (f32[576,1024]{1,0:T(8,128)S(1)}, f32[576,1024]{1,0:T(8,128)}, u32[]{:S(2)}) copy-start(f32[576,1024]{1,0:T(8,128)} %x_ref.1) | copy-start | bytes 7077892

commit v12 on v11

--- a/solution.py
+++ b/solution.py
@@ -59,6 +59,35 @@
     )(embeddings, index_rows, cols)
 
 
+def score_kernel(got_ref, key_ref, query_ref, best_ref):
+    got = got_ref[...]
+    cosine = lax.dot_general(
+        got, got, (((1,), (1,)), ((), ())), preferred_element_type=jnp.float32
+    )
+    key = key_ref[...]
+    query = query_ref[...]
+    usable = (
+        (key[:, 0:1] > 0)
+        & (key[:, 1:2] == query[1:2, :])
+        & (key[:, 2:3] < query[2:3, :])
+    )
+    best_ref[...] = jnp.max(jnp.where(usable, cosine, jnp.float32(-1.0)), axis=0, keepdims=True)
+
+
+def score(got_rows, valid, sub, ids):
+    slots = got_rows.shape[0]
+    vmem = pltpu.MemorySpace.VMEM
+    unused = jnp.zeros_like(ids)
+    fields = [valid.astype(jnp.int32), sub, ids] + [unused] * 5
+    return pl.pallas_call(
+        score_kernel,
+        out_shape=jax.ShapeDtypeStruct((1, slots), jnp.float32),
+        in_specs=[pl.BlockSpec(memory_space=vmem)] * 3,
+        out_specs=pl.BlockSpec(memory_space=vmem),
+        compiler_params=pltpu.CompilerParams(vmem_limit_bytes=48 * 1024 * 1024),
+    )(got_rows, jnp.stack(fields, axis=1), jnp.stack(fields, axis=0))
+
+
 def on_device(embeddings, cluster, global_index, send_counts):
     row_count, feat_width = embeddings.shape
     blocks = lax.axis_size("blk")
@@ -98,15 +127,7 @@
     got_sub = digit(1)
     got_ids = digit(2) * 4096 + digit(3) * 64 + digit(4)
 
-    cosine = lax.dot_general(
-        got_rows, got_rows, (((1,), (1,)), ((), ())), preferred_element_type=jnp.float32
-    )
-    usable = (
-        got_valid[None, :]
-        & (got_sub[:, None] == got_sub[None, :])
-        & (got_ids[None, :] < got_ids[:, None])
-    )
-    best = jnp.max(jnp.where(usable, cosine, jnp.float32(-1.0)), axis=1)
+    best = score(got_rows, got_valid, got_sub, got_ids)
 
     wide = jnp.pad(best.reshape(devices, CHUNK), ((0, 0), (0, LANES - CHUNK)))
     returned = lax.all_to_all(wide, AXES, 0, 0, tiled=True)[:, :CHUNK]

time: 66.4 us -> 67.7 us (1.020)
  matrix products: 3.12 us -> 0 us
  Pallas kernels: 2.33 us -> 5 us
  local copies, waits for them, and re-layouts: 3.29 us -> 4.4 us
    dot_general x1 -> x0, matrix products: 3.12 us -> none  [on_device(): lax.dot_general(got_rows, got_rows, (((1,), (1,)), ((), ())), preferred_e...]
    pallas_call x0 -> x1, Pallas kernels: none -> 2.67 us  [score(): pl.pallas_call(score_kernel, out_shape=jax.ShapeDtypeStruct((1, slots), j...]
where the time goes in v12:
time: 67.7 us; the launch traced here: 66.8 us
  blocking collectives  54.4 us (80%)
  Pallas kernels  5 us (7%)
  local copies, waits for them, and re-layouts  4.4 us (6%)
  other arithmetic  2.73 us (4%)
    all_to_all x1, blocking collectives, on_device(): got = lax.all_to_all(send, AXES, 0, 0, tiled=True)  40.9 us
    all_to_all x1, blocking collectives, on_device(): returned = lax.all_to_all(wide, AXES, 0, 0, tiled=True)[:, :CHUNK]  13.5 us
    pallas_call x1, Pallas kernels, score(): pl.pallas_call(score_kernel, out_shape=jax.ShapeDtypeStruct((1, slots), j...  2.67 us
    pallas_call x1, Pallas kernels, pack(): pl.pallas_call(pack_kernel, out_shape=jax.ShapeDtypeStruct((slots, feat_w...  2.33 us
    unnamed x2, local copies, waits for them, and re-layouts  1.67 us

profile of v12, /device:TPU:0, one launch (start us, length us, event | category | flops | bytes accessed | tf_op | source)
XLA Modules:
  0.0 66.8 jit_solution(16340642953403402955)
XLA Ops:
  0.0 0.8 %concatenate.3 = s32[1160]{0:T(1024)S(1)} concatenate(s32[576]{0:T(1024)} %param.5, s32[576]{0:T(1024)} %param.6, s32[8]{0:T(128)} %bitcast.15), dimensions={0} | concatenate | bytes 9280 | tf_op jit(solution)/shard_map/concatenate | solution.py:97
  0.8 0.1 add_select_fusion
  0.9 0.1 add_select_fusion.1
  1.0 0.1 add_select_fusion.4
  1.0 0.1 select_reduce_fusion.1
  1.1 0.1 convert_reduce_fusion.1
  1.3 0.3 convert_reduce_fusion
  1.6 0.1 pad.7.clone
  1.7 0.1 pad.8.clone
  1.8 0.1 copy.20.cols_ref
  2.0 0.1 add_add_fusion.idx_ref
  2.1 0.0 copy-start
  2.1 1.7 %copy-done = f32[576,1024]{1,0:T(8,128)S(1)} copy-done((f32[576,1024]{1,0:T(8,128)S(1)}, f32[576,1024]{1,0:T(8,128)}, u32[]{:S(2)}) %copy-start) | copy-done | bytes 2359320
  3.7 2.3 %shard_map.46 = bf16[1024,1024]{1,0:T(8,128)(2,1)S(1)} custom-call(f32[576,1024]{1,0:T(8,128)S(1)} %copy-done, s32[8,576]{1,0:T(8,128)S(1)} %add_add_fusion.idx_ref, s32[576,8]{1,0:T(8,128)S(1)} %copy.20.cols_ref), custom_call_target="tpu_custom_call" | custom-call | tf_op jit(solution)/shard_map/pallas_call | solution.py:53
  6.1 40.9 %all_to_all.17 = bf16[128,8,1024]{2,1,0:T(8,128)(2,1)S(1)} all-to-all(bf16[128,8,1024]{2,1,0:T(8,128)(2,1)S(1)} %bitcast.10), channel_id=1, replica_groups=mesh['group'=8,'blk'=16] {'group','blk'}, dimensions={0} | all-to-all | bytes 4194304 | tf_op jit(solution)/shard_map/all_to_all | solution.py:119
  47.0 0.1 slice_convert_fusion
  47.1 0.1 slice_add_fusion
  47.2 0.1 add.79
  47.3 0.1 add.78
  47.4 0.1 stack_reshape.7
  47.5 0.1 stack_reshape.6
  47.6 0.1 reshape.141
  47.7 0.1 reshape.140
  47.9 0.2 copy.21.key_ref
  48.2 2.7 %shard_map.47 = f32[1,1024]{1,0:T(1,128)S(1)} custom-call(bf16[1024,1024]{1,0:T(8,128)(2,1)S(1)} %bitcast.9, s32[1024,8]{1,0:T(8,128)S(1)} %copy.21.key_ref, s32[8,1024]{1,0:T(8,128)S(1)} %stack.64.query_ref), custom_call_target="tpu_custom_call" | custom-call | tf_op jit(solution)/shard_map/pallas_call | solution.py:82
  50.9 0.5 broadcast.121
  51.4 0.7 reduce.3
  52.0 0.1 reshape.138
  52.1 13.5 %all_to_all.18 = f32[128,1,128]{2,1,0:T(1,128)S(1)} all-to-all(f32[128,1,128]{2,1,0:T(1,128)S(1)} %bitcast.13), channel_id=1, replica_groups=mesh['group'=8,'blk'=16] {'group','blk'}, dimensions={0} | all-to-all | bytes 131072 | tf_op jit(solution)/shard_map/all_to_all | solution.py:133
  65.7 0.1 broadcast_in_dim.42
  65.8 1.0 %select_reduce_fusion = f32[576]{0:T(1024)} fusion(f32[1024]{0:T(1024)S(1)} %broadcast_in_dim.42, s32[576]{0:T(1024)S(1)} %multiply_add_fusion.1), kind=kLoop, calls=%fused_computation | loop fusion | flops 1768896 | bytes 8704 | tf_op jit(solution)/shard_map/reduce_sum | solution.py:134
  (23 shorter events, 0.2 us)
Async XLA Ops:
  2.1 1.7 %copy-start = (f32[576,1024]{1,0:T(8,128)S(1)}, f32[576,1024]{1,0:T(8,128)}, u32[]{:S(2)}) copy-start(f32[576,1024]{1,0:T(8,128)} %x_ref.1) | copy-start | bytes 7077892

commit v13 on v11

--- a/solution.py
+++ b/solution.py
@@ -11,6 +11,7 @@
 META_DIGITS = 5
 AXES = ("group", "blk")
 LANES = 128
+VMEM_LIMIT = 60 * 1024 * 1024
 
 
 def meta_digits(cluster, global_index):
@@ -23,10 +24,24 @@
     )
 
 
-def pack_kernel(x_ref, idx_ref, cols_ref, out_ref):
-    x = x_ref[...]
-    squares = jnp.sum(x * x, axis=1, keepdims=True)
-    unit = (x * lax.rsqrt(squares + 1e-06)).astype(jnp.bfloat16)
+def pack_kernel(x_hbm, idx_ref, cols_ref, out_ref, x_buf, unit_buf, sems):
+    pieces = sems.shape[0]
+    piece = x_buf.shape[0] // pieces
+    copies = [
+        pltpu.make_async_copy(
+            x_hbm.at[pl.ds(j * piece, piece)], x_buf.at[pl.ds(j * piece, piece)], sems.at[j]
+        )
+        for j in range(pieces)
+    ]
+    for copy in copies:
+        copy.start()
+    for j, copy in enumerate(copies):
+        copy.wait()
+        x = x_buf[pl.ds(j * piece, piece), :]
+        squares = jnp.sum(x * x, axis=1, keepdims=True)
+        unit_buf[pl.ds(j * piece, piece), :] = (x * lax.rsqrt(squares + 1e-06)).astype(jnp.bfloat16)
+    unit = unit_buf[...]
+    x_ref = x_buf
     row_count = x_ref.shape[0]
     slots = out_ref.shape[0]
     slot_at = lax.broadcasted_iota(jnp.int32, (slots, row_count), 0)
@@ -53,9 +68,14 @@
     return pl.pallas_call(
         pack_kernel,
         out_shape=jax.ShapeDtypeStruct((slots, feat_width), jnp.bfloat16),
-        in_specs=[pl.BlockSpec(memory_space=vmem)] * 3,
+        in_specs=[pl.BlockSpec(memory_space=pl.ANY)] + [pl.BlockSpec(memory_space=vmem)] * 2,
         out_specs=pl.BlockSpec(memory_space=vmem),
-        compiler_params=pltpu.CompilerParams(vmem_limit_bytes=48 * 1024 * 1024),
+        scratch_shapes=[
+            pltpu.VMEM((row_count, feat_width), jnp.float32),
+            pltpu.VMEM((row_count, feat_width), jnp.bfloat16),
+            pltpu.SemaphoreType.DMA((4,)),
+        ],
+        compiler_params=pltpu.CompilerParams(vmem_limit_bytes=VMEM_LIMIT),
     )(embeddings, index_rows, cols)
 
 

time: 66.4 us -> 70.2 us (1.057)
  Pallas kernels: 2.33 us -> 6.24 us
  local copies, waits for them, and re-layouts: 3.29 us -> 2.37 us
    pallas_call x1, Pallas kernels: 2.33 us -> 6.24 us  [pack(): pl.pallas_call(pack_kernel, out_shape=jax.ShapeDtypeStruct((slots, feat_w...]
    unnamed x2 -> x0, local copies, waits for them, and re-layouts: 1.67 us -> none
    another operation x9, local copies, waits for them, and re-layouts: 0.21 us -> 0.96 us  [pack(): cols = jnp.stack([rank, *digits] + [unused] * (7 - len(digits)), axis=1)]
where the time goes in v13:
time: 70.2 us; the launch traced here: 69.2 us
  blocking collectives  54.6 us (78%)
  Pallas kernels  6.24 us (9%)
  matrix products  3.11 us (4%)
  other arithmetic  2.67 us (4%)
  local copies, waits for them, and re-layouts  2.37 us (3%)
    all_to_all x1, blocking collectives, on_device(): got = lax.all_to_all(send, AXES, 0, 0, tiled=True)  41.1 us
    all_to_all x1, blocking collectives, on_device(): returned = lax.all_to_all(wide, AXES, 0, 0, tiled=True)[:, :CHUNK]  13.5 us
    pallas_call x1, Pallas kernels, pack(): pl.pallas_call(pack_kernel, out_shape=jax.ShapeDtypeStruct((slots, feat_w...  6.24 us
    dot_general x1, matrix products, on_device(): lax.dot_general(got_rows, got_rows, (((1,), (1,)), ((), ())), preferred_e...  3.11 us

profile of v13, /device:TPU:0, one launch (start us, length us, event | category | flops | bytes accessed | tf_op | source)
XLA Modules:
  0.0 69.2 jit_solution(5693776264755381722)
XLA Ops:
  0.0 0.8 %concatenate.3 = s32[1160]{0:T(1024)S(1)} concatenate(s32[576]{0:T(1024)} %param.5, s32[576]{0:T(1024)} %param.6, s32[8]{0:T(128)} %bitcast.18), dimensions={0} | concatenate | bytes 9280 | tf_op jit(solution)/shard_map/concatenate | solution.py:88
  0.8 0.1 add_select_fusion
  0.9 0.1 select_reduce_fusion.2
  1.0 0.1 convert_reduce_fusion.1
  1.1 0.1 add_select_fusion.1
  1.2 0.1 add_select_fusion.4
  1.2 0.3 convert_reduce_fusion
  1.6 0.1 pad.8.clone
  1.6 0.1 pad.7.clone
  1.8 0.9 %copy.18.cols_ref = s32[576,8]{1,0:T(8,128)} copy(s32[576,8]{0,1:T(8,128)S(1)} %stack.44) | data formatting | bytes 36864 | tf_op jit(solution)/shard_map/stack | solution.py:67
  2.7 0.7 add_add_fusion.idx_ref
  3.4 6.2 %shard_map.46 = bf16[1024,1024]{1,0:T(8,128)(2,1)} custom-call(f32[576,1024]{1,0:T(8,128)} %x_hbm.1, s32[8,576]{1,0:T(8,128)} %add_add_fusion.idx_ref, s32[576,8]{1,0:T(8,128)} %copy.18.cols_ref), custom_call_target="tpu_custom_call" | custom-call | tf_op jit(solution)/shard_map/pallas_call | solution.py:68
  9.6 41.1 %all_to_all.17 = bf16[128,8,1024]{2,1,0:T(8,128)(2,1)S(1)} all-to-all(bf16[128,8,1024]{2,1,0:T(8,128)(2,1)} %bitcast.13), channel_id=1, replica_groups=mesh['group'=8,'blk'=16] {'group','blk'}, dimensions={0} | all-to-all | bytes 4194304 | tf_op jit(solution)/shard_map/all_to_all | solution.py:110
  50.8 0.1 slice_convert_fusion
  50.9 0.1 fusion.15
  51.0 0.1 gt.15
  51.1 0.1 eq.51
  51.2 0.1 add.62
  51.3 3.1 %select_reduce_fusion = f32[1024]{0:T(1024)S(1)} fusion(bf16[128,8,1024]{2,1,0:T(8,128)(2,1)S(1)} %all_to_all.17, s32[1024]{0:T(1024)S(1)} %add.62, s32[1024]{0:T(1024)S(1)} %eq.51, pred[1024]{0:T(1024)(128)(4,1)S(1)} %gt.15), kind=kOutput, calls=%fused_computation | convolution fusion | flops 2153774080 | bytes 2110464 | tf_op jit(solution)/shard_map/dot_general | solution.py:121
  54.4 0.1 reshape.73
  54.6 13.5 %all_to_all.18 = f32[128,1,128]{2,1,0:T(1,128)S(1)} all-to-all(f32[128,1,128]{2,1,0:T(1,128)S(1)} %bitcast.16), channel_id=1, replica_groups=mesh['group'=8,'blk'=16] {'group','blk'}, dimensions={0} | all-to-all | bytes 131072 | tf_op jit(solution)/shard_map/all_to_all | solution.py:132
  68.1 0.1 broadcast_in_dim.50
  68.2 1.0 %select_reduce_fusion.1 = f32[576]{0:T(1024)} fusion(f32[1024]{0:T(1024)S(1)} %broadcast_in_dim.50, s32[576]{0:T(1024)S(1)} %multiply_add_fusion.1), kind=kLoop, calls=%fused_computation.1 | loop fusion | flops 1768896 | bytes 8704 | tf_op jit(solution)/shard_map/reduce_sum | solution.py:133
  (17 shorter events, 0.1 us)

commit v14 on v13

--- a/solution.py
+++ b/solution.py
@@ -11,7 +11,7 @@
 META_DIGITS = 5
 AXES = ("group", "blk")
 LANES = 128
-VMEM_LIMIT = 60 * 1024 * 1024
+VMEM_LIMIT = 50 * 1024 * 1024
 
 
 def meta_digits(cluster, global_index):

time: 70.2 us -> 66.3 us (0.944)
  Pallas kernels: 6.24 us -> 3.92 us
  local copies, waits for them, and re-layouts: 2.37 us -> 1.62 us
    pallas_call x1, Pallas kernels: 6.24 us -> 3.92 us  [pack(): pl.pallas_call(pack_kernel, out_shape=jax.ShapeDtypeStruct((slots, feat_w...]
    another operation x9, local copies, waits for them, and re-layouts: 0.96 us -> 0.21 us  [pack(): cols = jnp.stack([rank, *digits] + [unused] * (7 - len(digits)), axis=1)]
where the time goes in v14:
time: 66.3 us; the launch traced here: 65.3 us
  blocking collectives  54.4 us (82%)
  Pallas kernels  3.92 us (6%)
  matrix products  3.12 us (5%)
  other arithmetic  2.08 us (3%)
  local copies, waits for them, and re-layouts  1.62 us (2%)
    all_to_all x1, blocking collectives, on_device(): got = lax.all_to_all(send, AXES, 0, 0, tiled=True)  40.9 us
    all_to_all x1, blocking collectives, on_device(): returned = lax.all_to_all(wide, AXES, 0, 0, tiled=True)[:, :CHUNK]  13.5 us
    pallas_call x1, Pallas kernels, pack(): pl.pallas_call(pack_kernel, out_shape=jax.ShapeDtypeStruct((slots, feat_w...  3.92 us
    dot_general x1, matrix products, on_device(): lax.dot_general(got_rows, got_rows, (((1,), (1,)), ((), ())), preferred_e...  3.12 us

profile of v14, /device:TPU:0, one launch (start us, length us, event | category | flops | bytes accessed | tf_op | source)
XLA Modules:
  0.0 65.3 jit_solution(14488717965418406142)
XLA Ops:
  0.0 0.8 %concatenate.3 = s32[1160]{0:T(1024)S(1)} concatenate(s32[576]{0:T(1024)} %param.5, s32[576]{0:T(1024)} %param.6, s32[8]{0:T(128)} %bitcast.18), dimensions={0} | concatenate | bytes 9280 | tf_op jit(solution)/shard_map/concatenate | solution.py:88
  0.8 0.1 add_select_fusion
  0.9 0.1 select_reduce_fusion.2
  1.0 0.1 convert_reduce_fusion.1
  1.1 0.1 add_select_fusion.1
  1.2 0.1 add_select_fusion.4
  1.2 0.3 convert_reduce_fusion
  1.6 0.1 pad.8.clone
  1.6 0.1 pad.7.clone
  1.8 0.1 copy.18.cols_ref
  2.0 0.1 add_add_fusion.idx_ref
  2.1 3.9 %shard_map.46 = bf16[1024,1024]{1,0:T(8,128)(2,1)S(1)} custom-call(f32[576,1024]{1,0:T(8,128)} %x_hbm.1, s32[8,576]{1,0:T(8,128)S(1)} %add_add_fusion.idx_ref, s32[576,8]{1,0:T(8,128)S(1)} %copy.18.cols_ref), custom_call_target="tpu_custom_call" | custom-call | tf_op jit(solution)/shard_map/pallas_call | solution.py:68
  6.0 40.9 %all_to_all.17 = bf16[128,8,1024]{2,1,0:T(8,128)(2,1)S(1)} all-to-all(bf16[128,8,1024]{2,1,0:T(8,128)(2,1)S(1)} %bitcast.13), channel_id=1, replica_groups=mesh['group'=8,'blk'=16] {'group','blk'}, dimensions={0} | all-to-all | bytes 4194304 | tf_op jit(solution)/shard_map/all_to_all | solution.py:110
  46.9 0.1 slice_convert_fusion
  47.0 0.1 fusion.15
  47.2 0.1 gt.15
  47.3 0.1 eq.51
  47.4 0.1 add.62
  47.5 3.1 %select_reduce_fusion = f32[1024]{0:T(1024)S(1)} fusion(bf16[128,8,1024]{2,1,0:T(8,128)(2,1)S(1)} %all_to_all.17, s32[1024]{0:T(1024)S(1)} %add.62, s32[1024]{0:T(1024)S(1)} %eq.51, pred[1024]{0:T(1024)(128)(4,1)S(1)} %gt.15), kind=kOutput, calls=%fused_computation | convolution fusion | flops 2153774080 | bytes 2110464 | tf_op jit(solution)/shard_map/dot_general | solution.py:121
  50.6 0.1 reshape.73
  50.7 13.5 %all_to_all.18 = f32[128,1,128]{2,1,0:T(1,128)S(1)} all-to-all(f32[128,1,128]{2,1,0:T(1,128)S(1)} %bitcast.16), channel_id=1, replica_groups=mesh['group'=8,'blk'=16] {'group','blk'}, dimensions={0} | all-to-all | bytes 131072 | tf_op jit(solution)/shard_map/all_to_all | solution.py:132
  64.2 0.1 broadcast_in_dim.50
  64.3 1.0 %select_reduce_fusion.1 = f32[576]{0:T(1024)} fusion(f32[1024]{0:T(1024)S(1)} %broadcast_in_dim.50, s32[576]{0:T(1024)S(1)} %multiply_add_fusion.1), kind=kLoop, calls=%fused_computation.1 | loop fusion | flops 1768896 | bytes 8704 | tf_op jit(solution)/shard_map/reduce_sum | solution.py:133
  (17 shorter events, 0.1 us)

commit v15 on v14

--- a/solution.py
+++ b/solution.py
@@ -24,38 +24,40 @@
     )
 
 
-def pack_kernel(x_hbm, idx_ref, cols_ref, out_ref, x_buf, unit_buf, sems):
-    pieces = sems.shape[0]
-    piece = x_buf.shape[0] // pieces
+def pack_kernel(x_hbm, idx_ref, cols_ref, out_ref, x_buf, sems):
+    row_count = x_buf.shape[0]
+    slots = out_ref.shape[0]
+    starts = list(range(0, row_count - LANES, LANES))
+    ends = starts[1:] + [row_count]
     copies = [
         pltpu.make_async_copy(
-            x_hbm.at[pl.ds(j * piece, piece)], x_buf.at[pl.ds(j * piece, piece)], sems.at[j]
+            x_hbm.at[pl.ds(lo, hi - lo)], x_buf.at[pl.ds(lo, hi - lo)], sems.at[j]
         )
-        for j in range(pieces)
+        for j, (lo, hi) in enumerate(zip(starts, ends))
     ]
     for copy in copies:
         copy.start()
-    for j, copy in enumerate(copies):
-        copy.wait()
-        x = x_buf[pl.ds(j * piece, piece), :]
-        squares = jnp.sum(x * x, axis=1, keepdims=True)
-        unit_buf[pl.ds(j * piece, piece), :] = (x * lax.rsqrt(squares + 1e-06)).astype(jnp.bfloat16)
-    unit = unit_buf[...]
-    x_ref = x_buf
-    row_count = x_ref.shape[0]
-    slots = out_ref.shape[0]
-    slot_at = lax.broadcasted_iota(jnp.int32, (slots, row_count), 0)
-    picks = (slot_at == idx_ref[0:1, :]).astype(jnp.bfloat16)
-    rows = jnp.dot(picks, unit, preferred_element_type=jnp.float32)
-    out_ref[...] = rows.astype(jnp.bfloat16)
 
     cols = cols_ref[...]
     column = lax.broadcasted_iota(jnp.int32, (row_count, LANES), 1)
     spread = jnp.zeros((row_count, LANES), jnp.int32)
     for t in range(META_DIGITS):
         spread = jnp.where(column == t * CHUNK + cols[:, 0:1], cols[:, t + 1 : t + 2], spread)
-    meta_picks = (slot_at == idx_ref[1:2, :]).astype(jnp.bfloat16)
+    meta_at = lax.broadcasted_iota(jnp.int32, (slots, row_count), 0)
+    meta_picks = (meta_at == idx_ref[1:2, :]).astype(jnp.bfloat16)
     meta = jnp.dot(meta_picks, spread.astype(jnp.bfloat16), preferred_element_type=jnp.float32)
+
+    rows = None
+    for (lo, hi), copy in zip(zip(starts, ends), copies):
+        copy.wait()
+        x = x_buf[pl.ds(lo, hi - lo), :]
+        squares = jnp.sum(x * x, axis=1, keepdims=True)
+        unit = (x * lax.rsqrt(squares + 1e-06)).astype(jnp.bfloat16)
+        slot_at = lax.broadcasted_iota(jnp.int32, (slots, hi - lo), 0)
+        picks = (slot_at == idx_ref[0:1, lo:hi]).astype(jnp.bfloat16)
+        part = jnp.dot(picks, unit, preferred_element_type=jnp.float32)
+        rows = part if rows is None else rows + part
+    out_ref[...] = rows.astype(jnp.bfloat16)
     out_ref[:, :LANES] = (rows[:, :LANES] + meta).astype(jnp.bfloat16)
 
 
@@ -72,8 +74,7 @@
         out_specs=pl.BlockSpec(memory_space=vmem),
         scratch_shapes=[
             pltpu.VMEM((row_count, feat_width), jnp.float32),
-            pltpu.VMEM((row_count, feat_width), jnp.bfloat16),
-            pltpu.SemaphoreType.DMA((4,)),
+            pltpu.SemaphoreType.DMA((row_count // LANES,)),
         ],
         compiler_params=pltpu.CompilerParams(vmem_limit_bytes=VMEM_LIMIT),
     )(embeddings, index_rows, cols)

time: 66.3 us -> 68.2 us (1.029)
  Pallas kernels: 3.92 us -> 5.89 us
    pallas_call x1, Pallas kernels: 3.92 us -> 5.89 us  [pack(): pl.pallas_call(pack_kernel, out_shape=jax.ShapeDtypeStruct((slots, feat_w...]
where the time goes in v15:
time: 68.2 us; the launch traced here: 67.3 us
  blocking collectives  54.4 us (80%)
  Pallas kernels  5.89 us (9%)
  matrix products  3.12 us (5%)
  other arithmetic  2.08 us (3%)
  local copies, waits for them, and re-layouts  1.62 us (2%)
    all_to_all x1, blocking collectives, on_device(): got = lax.all_to_all(send, AXES, 0, 0, tiled=True)  40.9 us
    all_to_all x1, blocking collectives, on_device(): returned = lax.all_to_all(wide, AXES, 0, 0, tiled=True)[:, :CHUNK]  13.5 us
    pallas_call x1, Pallas kernels, pack(): pl.pallas_call(pack_kernel, out_shape=jax.ShapeDtypeStruct((slots, feat_w...  5.89 us
    dot_general x1, matrix products, on_device(): lax.dot_general(got_rows, got_rows, (((1,), (1,)), ((), ())), preferred_e...  3.12 us

profile of v15, /device:TPU:0, one launch (start us, length us, event | category | flops | bytes accessed | tf_op | source)
XLA Modules:
  0.0 67.3 jit_solution(16298164926670228568)
XLA Ops:
  0.0 0.8 %concatenate.3 = s32[1160]{0:T(1024)S(1)} concatenate(s32[576]{0:T(1024)} %param.5, s32[576]{0:T(1024)} %param.6, s32[8]{0:T(128)} %bitcast.18), dimensions={0} | concatenate | bytes 9280 | tf_op jit(solution)/shard_map/concatenate | solution.py:89
  0.8 0.1 add_select_fusion
  0.9 0.1 select_reduce_fusion.2
  1.0 0.1 convert_reduce_fusion.1
  1.1 0.1 add_select_fusion.1
  1.2 0.1 add_select_fusion.4
  1.2 0.3 convert_reduce_fusion
  1.6 0.1 pad.8.clone
  1.6 0.1 pad.7.clone
  1.8 0.1 copy.18.cols_ref
  2.0 0.1 add_add_fusion.idx_ref
  2.1 5.9 %shard_map.46 = bf16[1024,1024]{1,0:T(8,128)(2,1)S(1)} custom-call(f32[576,1024]{1,0:T(8,128)} %x_hbm.1, s32[8,576]{1,0:T(8,128)S(1)} %add_add_fusion.idx_ref, s32[576,8]{1,0:T(8,128)S(1)} %copy.18.cols_ref), custom_call_target="tpu_custom_call" | custom-call | tf_op jit(solution)/shard_map/pallas_call | solution.py:70
  8.0 40.9 %all_to_all.17 = bf16[128,8,1024]{2,1,0:T(8,128)(2,1)S(1)} all-to-all(bf16[128,8,1024]{2,1,0:T(8,128)(2,1)S(1)} %bitcast.13), channel_id=1, replica_groups=mesh['group'=8,'blk'=16] {'group','blk'}, dimensions={0} | all-to-all | bytes 4194304 | tf_op jit(solution)/shard_map/all_to_all | solution.py:111
  48.9 0.1 slice_convert_fusion
  49.0 0.1 fusion.15
  49.1 0.1 gt.15
  49.2 0.1 eq.51
  49.3 0.1 add.62
  49.4 3.1 %select_reduce_fusion = f32[1024]{0:T(1024)S(1)} fusion(bf16[128,8,1024]{2,1,0:T(8,128)(2,1)S(1)} %all_to_all.17, s32[1024]{0:T(1024)S(1)} %add.62, s32[1024]{0:T(1024)S(1)} %eq.51, pred[1024]{0:T(1024)(128)(4,1)S(1)} %gt.15), kind=kOutput, calls=%fused_computation | convolution fusion | flops 2153774080 | bytes 2110464 | tf_op jit(solution)/shard_map/dot_general | solution.py:122
  52.6 0.1 reshape.73
  52.7 13.5 %all_to_all.18 = f32[128,1,128]{2,1,0:T(1,128)S(1)} all-to-all(f32[128,1,128]{2,1,0:T(1,128)S(1)} %bitcast.16), channel_id=1, replica_groups=mesh['group'=8,'blk'=16] {'group','blk'}, dimensions={0} | all-to-all | bytes 131072 | tf_op jit(solution)/shard_map/all_to_all | solution.py:133
  66.2 0.1 broadcast_in_dim.50
  66.3 1.0 %select_reduce_fusion.1 = f32[576]{0:T(1024)} fusion(f32[1024]{0:T(1024)S(1)} %broadcast_in_dim.50, s32[576]{0:T(1024)S(1)} %multiply_add_fusion.1), kind=kLoop, calls=%fused_computation.1 | loop fusion | flops 1768896 | bytes 8704 | tf_op jit(solution)/shard_map/reduce_sum | solution.py:134
  (17 shorter events, 0.1 us)

commit v16 on v10

--- a/solution.py
+++ b/solution.py
@@ -13,41 +13,42 @@
 META_DIGITS = 5
 AXES = ("group", "blk")
 LANES = 128
+VMEM_LIMIT = 50 * 1024 * 1024
 
 
-def pack_kernel(blocks, counts_ref, cl_ref, gi_ref, x_ref, out_ref, slot_ref):
-    row_count = x_ref.shape[0]
+def pack_kernel(blocks, x_hbm, small_ref, out_ref, slot_ref, x_buf, unit_buf, sems):
+    pieces = sems.shape[0]
+    row_count = x_buf.shape[0]
+    piece = row_count // pieces
     slots = out_ref.shape[0]
+    copies = [
+        pltpu.make_async_copy(
+            x_hbm.at[pl.ds(j * piece, piece)], x_buf.at[pl.ds(j * piece, piece)], sems.at[j]
+        )
+        for j in range(pieces)
+    ]
+    for copy in copies:
+        copy.start()
+
     pos_row = lax.broadcasted_iota(jnp.int32, (1, row_count), 1)
     pos_col = lax.broadcasted_iota(jnp.int32, (row_count, 1), 0)
+    cl_row = small_ref[0:1, :]
+    gi_row = small_ref[1:2, :]
+    counts_row = small_ref[2:3, :]
     owner_row = jnp.zeros((1, row_count), jnp.int32)
-    owner_col = jnp.zeros((row_count, 1), jnp.int32)
-    end = counts_ref[0]
-    for g in range(1, counts_ref.shape[0] + 1):
+    for g in range(blocks.groups):
+        end = jnp.sum(jnp.where(pos_row <= g, counts_row, 0), axis=1, keepdims=True)
         owner_row = owner_row + (pos_row >= end).astype(jnp.int32)
-        owner_col = owner_col + (pos_col >= end).astype(jnp.int32)
-        if g < counts_ref.shape[0]:
-            end = end + counts_ref[g]
+    dest_row = owner_row * blocks.blocks + lax.shift_right_logical(cl_row, 2)
     on_diag = pos_col == pos_row
-    cl_row = cl_ref[...].reshape(1, row_count)
-    gi_row = gi_ref[...].reshape(1, row_count)
+    dest_col = jnp.sum(jnp.where(on_diag, dest_row, 0), axis=1, keepdims=True)
     cl_col = jnp.sum(jnp.where(on_diag, cl_row, 0), axis=1, keepdims=True)
     gi_col = jnp.sum(jnp.where(on_diag, gi_row, 0), axis=1, keepdims=True)
-    dest_row = owner_row * blocks + lax.shift_right_logical(cl_row, 2)
-    dest_col = owner_col * blocks + lax.shift_right_logical(cl_col, 2)
     same = dest_col == dest_row
     rank_row = jnp.sum((same & (pos_col < pos_row)).astype(jnp.int32), axis=0, keepdims=True)
     rank_col = jnp.sum((same & (pos_row < pos_col)).astype(jnp.int32), axis=1, keepdims=True)
     slot_row = dest_row * CHUNK + rank_row
     slot_ref[...] = slot_row
-
-    x = x_ref[...]
-    squares = jnp.sum(x * x, axis=1, keepdims=True)
-    unit = (x * lax.rsqrt(squares + 1e-06)).astype(jnp.bfloat16)
-    slot_at = lax.broadcasted_iota(jnp.int32, (slots, row_count), 0)
-    picks = (slot_at == slot_row).astype(jnp.bfloat16)
-    rows = jnp.dot(picks, unit, preferred_element_type=jnp.float32)
-    out_ref[...] = rows.astype(jnp.bfloat16)
 
     digits = (
         jnp.ones_like(cl_col),
@@ -60,30 +61,54 @@
     spread = jnp.zeros((row_count, LANES), jnp.int32)
     for t, digit in enumerate(digits):
         spread = jnp.where(column == t * CHUNK + rank_col, digit, spread)
+    slot_at = lax.broadcasted_iota(jnp.int32, (slots, row_count), 0)
     meta_picks = (slot_at == dest_row * CHUNK + CHUNK - 1).astype(jnp.bfloat16)
     meta = jnp.dot(meta_picks, spread.astype(jnp.bfloat16), preferred_element_type=jnp.float32)
+    picks = (slot_at == slot_row).astype(jnp.bfloat16)
+
+    for j, copy in enumerate(copies):
+        copy.wait()
+        x = x_buf[pl.ds(j * piece, piece), :]
+        squares = jnp.sum(x * x, axis=1, keepdims=True)
+        unit_buf[pl.ds(j * piece, piece), :] = (x * lax.rsqrt(squares + 1e-06)).astype(jnp.bfloat16)
+    rows = jnp.dot(picks, unit_buf[...], preferred_element_type=jnp.float32)
+    out_ref[...] = rows.astype(jnp.bfloat16)
     out_ref[:, :LANES] = (rows[:, :LANES] + meta).astype(jnp.bfloat16)
 
 
-def pack(embeddings, cluster, global_index, counts, blocks, slots):
+class MeshSizes:
+    def __init__(self, groups, blocks):
+        self.groups = groups
+        self.blocks = blocks
+
+
+def pack(embeddings, cluster, global_index, counts, sizes, slots):
     row_count, feat_width = embeddings.shape
     vmem = pltpu.MemorySpace.VMEM
+    joined = lax.optimization_barrier(jnp.concatenate([cluster, global_index, counts]))
+    small = jnp.stack(
+        [
+            joined[:row_count],
+            joined[row_count : 2 * row_count],
+            jnp.pad(joined[2 * row_count :], (0, row_count - counts.shape[0])),
+        ],
+        axis=0,
+    )
     return pl.pallas_call(
-        functools.partial(pack_kernel, blocks),
+        functools.partial(pack_kernel, sizes),
         out_shape=(
             jax.ShapeDtypeStruct((slots, feat_width), jnp.bfloat16),
             jax.ShapeDtypeStruct((1, row_count), jnp.int32),
         ),
-        in_specs=[pl.BlockSpec(memory_space=pltpu.MemorySpace.SMEM)]
-        + [pl.BlockSpec(memory_space=vmem)] * 3,
+        in_specs=[pl.BlockSpec(memory_space=pl.ANY), pl.BlockSpec(memory_space=vmem)],
         out_specs=(pl.BlockSpec(memory_space=vmem), pl.BlockSpec(memory_space=vmem)),
-        compiler_params=pltpu.CompilerParams(vmem_limit_bytes=48 * 1024 * 1024),
-    )(
-        counts,
-        cluster,
-        global_index,
-        embeddings,
-    )
+        scratch_shapes=[
+            pltpu.VMEM((row_count, feat_width), jnp.float32),
+            pltpu.VMEM((row_count, feat_width), jnp.bfloat16),
+            pltpu.SemaphoreType.DMA((4,)),
+        ],
+        compiler_params=pltpu.CompilerParams(vmem_limit_bytes=VMEM_LIMIT),
+    )(embeddings, small)
 
 
 def on_device(embeddings, cluster, global_index, send_counts):
@@ -91,7 +116,8 @@
     blocks = lax.axis_size("blk")
     devices = lax.axis_size("group") * blocks
     slots = devices * CHUNK
-    send, slot = pack(embeddings, cluster, global_index, send_counts[0], blocks, slots)
+    sizes = MeshSizes(lax.axis_size("group"), blocks)
+    send, slot = pack(embeddings, cluster, global_index, send_counts[0], sizes, slots)
     send = send.reshape(devices, CHUNK, feat_width)
     slot_ids = jnp.arange(slots, dtype=jnp.int32)
     picks = slot_ids[:, None] == slot

time: 68.9 us -> 67.2 us (0.975)
  local copies, waits for them, and re-layouts: 4.78 us -> 1.95 us
  Pallas kernels: 3.71 us -> 4.87 us
    unnamed x8 -> x0, local copies, waits for them, and re-layouts: 3.69 us -> none
    pallas_call x1, Pallas kernels: 3.71 us -> 4.87 us  [pack(): pl.pallas_call(functools.partial(pack_kernel, sizes), out_shape=(jax.Shap...]
    concatenate x0 -> x1, local copies, waits for them, and re-layouts: none -> 0.78 us  [pack(): jnp.concatenate([cluster, global_index, counts])]
where the time goes in v16:
time: 67.2 us; the launch traced here: 66.2 us
  blocking collectives  40.9 us (61%)
  waiting for transfers between devices  9.38 us (14%)
  Pallas kernels  4.87 us (7%)
  starting transfers between devices  4.61 us (7%)
  matrix products  3.12 us (5%)
  local copies, waits for them, and re-layouts  1.95 us (3%)
  other arithmetic  1.29 us (2%)
    all_to_all x1, blocking collectives, on_device(): got = lax.all_to_all(send, AXES, 0, 0, tiled=True)  40.9 us
    all_to_all x1, waiting for transfers between devices, on_device(): returned = lax.all_to_all(wide, AXES, 0, 0, tiled=True)[:, :CHUNK]  9.38 us
    pallas_call x1, Pallas kernels, pack(): pl.pallas_call(functools.partial(pack_kernel, sizes), out_shape=(jax.Shap...  4.87 us
    all_to_all x1, starting transfers between devices, on_device(): returned = lax.all_to_all(wide, AXES, 0, 0, tiled=True)[:, :CHUNK]  4.61 us
    dot_general x1, matrix products, on_device(): lax.dot_general(got_rows, got_rows, (((1,), (1,)), ((), ())), preferred_e...  3.12 us
  transfers between devices with their start and end apart: 1, of which 1 were waited for; matrix products, arithmetic and copies ran while one was open for 0% of the time, Pallas kernels for 0%

profile of v16, /device:TPU:0, one launch (start us, length us, event | category | flops | bytes accessed | tf_op | source)
XLA Modules:
  0.0 66.2 jit_solution(4694340706121081700)
XLA Ops:
  0.0 0.8 %concatenate.3 = s32[1160]{0:T(1024)S(1)} concatenate(s32[576]{0:T(1024)} %param.5, s32[576]{0:T(1024)} %param.6, s32[8]{0:T(128)} %bitcast.17), dimensions={0} | concatenate | bytes 9280 | tf_op jit(solution)/shard_map/concatenate | solution.py:88
  0.8 0.1 fusion.6
  0.9 4.9 %shard_map.46 = (bf16[1024,1024]{1,0:T(8,128)(2,1)S(1)}, s32[1,576]{1,0:T(1,128)S(1)}) custom-call(f32[576,1024]{1,0:T(8,128)} %x_hbm.1, s32[3,576]{1,0:T(4,128)S(1)} %pad_add_fusion.small_ref), custom_call_target="tpu_custom_call" | custom-call | tf_op jit(solution)/shard_map/pallas_call | solution.py:97
  5.8 40.9 %all_to_all.17 = bf16[128,8,1024]{2,1,0:T(8,128)(2,1)S(1)} all-to-all(bf16[128,8,1024]{2,1,0:T(8,128)(2,1)S(1)} %bitcast.13), channel_id=1, replica_groups=mesh['group'=8,'blk'=16] {'group','blk'}, dimensions={0} | all-to-all | bytes 4194304 | tf_op jit(solution)/shard_map/all_to_all | solution.py:125
  46.7 0.1 slice_convert_fusion
  46.8 0.1 fusion.5
  47.0 0.1 add.32
  47.1 0.1 eq.34
  47.2 0.1 gt.15
  47.3 3.1 %select_reduce_fusion = f32[1024]{0:T(1024)S(1)} fusion(bf16[128,8,1024]{2,1,0:T(8,128)(2,1)S(1)} %all_to_all.17, s32[1024]{0:T(1024)S(1)} %add.32, s32[1024]{0:T(1024)S(1)} %eq.34, pred[1024]{0:T(1024)(128)(4,1)S(1)} %gt.15), kind=kOutput, calls=%fused_computation | convolution fusion | flops 2153774080 | bytes 2110464 | tf_op jit(solution)/shard_map/dot_general | solution.py:136
  50.4 0.1 reshape.68
  50.5 0.6 pad.9
  51.1 4.6 %all-to-all-start.1 = ((f32[128,1,128]{2,1,0:T(1,128)}), f32[128,1,128]{2,1,0:T(1,128)S(1)}, u32[]{:S(2)}, u32[]{:S(2)}) async-start(f32[128,1,128]{2,1,0:T(1,128)} %bitcast.5), calls=%async_computation.1 | async-start | bytes 131072 | tf_op jit(solution)/shard_map/all_to_all | solution.py:147
  55.7 9.4 %all-to-all-done.1 = f32[128,1,128]{2,1,0:T(1,128)S(1)} async-done(((f32[128,1,128]{2,1,0:T(1,128)}), f32[128,1,128]{2,1,0:T(1,128)S(1)}, u32[]{:S(2)}, u32[]{:S(2)}) %all-to-all-start.1) | async-done | bytes 65568 | tf_op jit(solution)/shard_map/all_to_all | solution.py:147
  65.1 0.1 broadcast_in_dim.23
  65.2 1.0 %select_reduce_fusion.1 = f32[576]{0:T(1024)} fusion(f32[1024]{0:T(1024)S(1)} %broadcast_in_dim.23, s32[576]{0:T(1024)S(1)} %reduce), kind=kLoop, calls=%fused_computation.1 | loop fusion | flops 1768896 | bytes 8704 | tf_op jit(solution)/shard_map/reduce_sum | solution.py:148
  (8 shorter events, 0.1 us)
Async XLA Ops:
  51.1 14.0 %all-to-all-start.1 = ((f32[128,1,128]{2,1,0:T(1,128)}), f32[128,1,128]{2,1,0:T(1,128)S(1)}, u32[]{:S(2)}, u32[]{:S(2)}) async-start(f32[128,1,128]{2,1,0:T(1,128)} %bitcast.5), calls=%async_computation.1 | async-start | bytes 131072 | tf_op jit(solution)/shard_map/all_to_all | solution.py:147

commit v17 on v16

--- a/solution.py
+++ b/solution.py
@@ -40,30 +40,35 @@
         end = jnp.sum(jnp.where(pos_row <= g, counts_row, 0), axis=1, keepdims=True)
         owner_row = owner_row + (pos_row >= end).astype(jnp.int32)
     dest_row = owner_row * blocks.blocks + lax.shift_right_logical(cl_row, 2)
-    on_diag = pos_col == pos_row
-    dest_col = jnp.sum(jnp.where(on_diag, dest_row, 0), axis=1, keepdims=True)
-    cl_col = jnp.sum(jnp.where(on_diag, cl_row, 0), axis=1, keepdims=True)
-    gi_col = jnp.sum(jnp.where(on_diag, gi_row, 0), axis=1, keepdims=True)
-    same = dest_col == dest_row
-    rank_row = jnp.sum((same & (pos_col < pos_row)).astype(jnp.int32), axis=0, keepdims=True)
-    rank_col = jnp.sum((same & (pos_row < pos_col)).astype(jnp.int32), axis=1, keepdims=True)
+    devices = slots // CHUNK
+    dest_hot = lax.broadcasted_iota(jnp.int32, (devices, row_count), 0) == dest_row
+    before = pos_col < pos_row
+    counted = jnp.dot(
+        dest_hot.astype(jnp.bfloat16), before.astype(jnp.bfloat16), preferred_element_type=jnp.float32
+    )
+    rank_row = jnp.sum(jnp.where(dest_hot, counted, 0.0), axis=0, keepdims=True).astype(jnp.int32)
     slot_row = dest_row * CHUNK + rank_row
     slot_ref[...] = slot_row
 
     digits = (
-        jnp.ones_like(cl_col),
-        cl_col & (BLOCK_WIDTH - 1),
-        lax.shift_right_logical(gi_col, 12),
-        lax.shift_right_logical(gi_col, 6) & 63,
-        gi_col & 63,
+        jnp.ones_like(cl_row),
+        cl_row & (BLOCK_WIDTH - 1),
+        lax.shift_right_logical(gi_row, 12),
+        lax.shift_right_logical(gi_row, 6) & 63,
+        gi_row & 63,
     )
-    column = lax.broadcasted_iota(jnp.int32, (row_count, LANES), 1)
-    spread = jnp.zeros((row_count, LANES), jnp.int32)
+    column = lax.broadcasted_iota(jnp.int32, (LANES, row_count), 0)
+    spread = jnp.zeros((LANES, row_count), jnp.int32)
     for t, digit in enumerate(digits):
-        spread = jnp.where(column == t * CHUNK + rank_col, digit, spread)
+        spread = jnp.where(column == t * CHUNK + rank_row, digit, spread)
     slot_at = lax.broadcasted_iota(jnp.int32, (slots, row_count), 0)
     meta_picks = (slot_at == dest_row * CHUNK + CHUNK - 1).astype(jnp.bfloat16)
-    meta = jnp.dot(meta_picks, spread.astype(jnp.bfloat16), preferred_element_type=jnp.float32)
+    meta = lax.dot_general(
+        meta_picks,
+        spread.astype(jnp.bfloat16),
+        (((1,), (1,)), ((), ())),
+        preferred_element_type=jnp.float32,
+    )
     picks = (slot_at == slot_row).astype(jnp.bfloat16)
 
     for j, copy in enumerate(copies):

time: 67.2 us -> 66.5 us (0.990)
  no operation moved by 1% of the time
where the time goes in v17:
time: 66.5 us; the launch traced here: 65.5 us
  blocking collectives  40.9 us (62%)
  waiting for transfers between devices  9.38 us (14%)
  starting transfers between devices  4.61 us (7%)
  Pallas kernels  4.2 us (6%)
  matrix products  3.12 us (5%)
  local copies, waits for them, and re-layouts  1.95 us (3%)
  other arithmetic  1.29 us (2%)
    all_to_all x1, blocking collectives, on_device(): got = lax.all_to_all(send, AXES, 0, 0, tiled=True)  40.9 us
    all_to_all x1, waiting for transfers between devices, on_device(): returned = lax.all_to_all(wide, AXES, 0, 0, tiled=True)[:, :CHUNK]  9.38 us
    all_to_all x1, starting transfers between devices, on_device(): returned = lax.all_to_all(wide, AXES, 0, 0, tiled=True)[:, :CHUNK]  4.61 us
    pallas_call x1, Pallas kernels, pack(): pl.pallas_call(functools.partial(pack_kernel, sizes), out_shape=(jax.Shap...  4.2 us
    dot_general x1, matrix products, on_device(): lax.dot_general(got_rows, got_rows, (((1,), (1,)), ((), ())), preferred_e...  3.12 us
  transfers between devices with their start and end apart: 1, of which 1 were waited for; matrix products, arithmetic and copies ran while one was open for 0% of the time, Pallas kernels for 0%

profile of v17, /device:TPU:0, one launch (start us, length us, event | category | flops | bytes accessed | tf_op | source)
XLA Modules:
  0.0 65.5 jit_solution(719641588260632239)
XLA Ops:
  0.0 0.8 %concatenate.3 = s32[1160]{0:T(1024)S(1)} concatenate(s32[576]{0:T(1024)} %param.5, s32[576]{0:T(1024)} %param.6, s32[8]{0:T(128)} %bitcast.17), dimensions={0} | concatenate | bytes 9280 | tf_op jit(solution)/shard_map/concatenate | solution.py:93
  0.8 0.1 fusion.6
  0.9 4.2 %shard_map.46 = (bf16[1024,1024]{1,0:T(8,128)(2,1)S(1)}, s32[1,576]{1,0:T(1,128)S(1)}) custom-call(f32[576,1024]{1,0:T(8,128)} %x_hbm.1, s32[3,576]{1,0:T(4,128)S(1)} %pad_add_fusion.small_ref), custom_call_target="tpu_custom_call" | custom-call | tf_op jit(solution)/shard_map/pallas_call | solution.py:102
  5.1 40.9 %all_to_all.17 = bf16[128,8,1024]{2,1,0:T(8,128)(2,1)S(1)} all-to-all(bf16[128,8,1024]{2,1,0:T(8,128)(2,1)S(1)} %bitcast.13), channel_id=1, replica_groups=mesh['group'=8,'blk'=16] {'group','blk'}, dimensions={0} | all-to-all | bytes 4194304 | tf_op jit(solution)/shard_map/all_to_all | solution.py:130
  46.0 0.1 slice_convert_fusion
  46.1 0.1 fusion.5
  46.3 0.1 add.32
  46.4 0.1 eq.34
  46.5 0.1 gt.15
  46.6 3.1 %select_reduce_fusion = f32[1024]{0:T(1024)S(1)} fusion(bf16[128,8,1024]{2,1,0:T(8,128)(2,1)S(1)} %all_to_all.17, s32[1024]{0:T(1024)S(1)} %add.32, s32[1024]{0:T(1024)S(1)} %eq.34, pred[1024]{0:T(1024)(128)(4,1)S(1)} %gt.15), kind=kOutput, calls=%fused_computation | convolution fusion | flops 2153774080 | bytes 2110464 | tf_op jit(solution)/shard_map/dot_general | solution.py:141
  49.7 0.1 reshape.68
  49.8 0.6 pad.9
  50.4 4.6 %all-to-all-start.1 = ((f32[128,1,128]{2,1,0:T(1,128)}), f32[128,1,128]{2,1,0:T(1,128)S(1)}, u32[]{:S(2)}, u32[]{:S(2)}) async-start(f32[128,1,128]{2,1,0:T(1,128)} %bitcast.5), calls=%async_computation.1 | async-start | bytes 131072 | tf_op jit(solution)/shard_map/all_to_all | solution.py:152
  55.1 9.4 %all-to-all-done.1 = f32[128,1,128]{2,1,0:T(1,128)S(1)} async-done(((f32[128,1,128]{2,1,0:T(1,128)}), f32[128,1,128]{2,1,0:T(1,128)S(1)}, u32[]{:S(2)}, u32[]{:S(2)}) %all-to-all-start.1) | async-done | bytes 65568 | tf_op jit(solution)/shard_map/all_to_all | solution.py:152
  64.5 0.1 broadcast_in_dim.23
  64.5 1.0 %select_reduce_fusion.1 = f32[576]{0:T(1024)} fusion(f32[1024]{0:T(1024)S(1)} %broadcast_in_dim.23, s32[576]{0:T(1024)S(1)} %reduce), kind=kLoop, calls=%fused_computation.1 | loop fusion | flops 1768896 | bytes 8704 | tf_op jit(solution)/shard_map/reduce_sum | solution.py:153
  (8 shorter events, 0.1 us)
Async XLA Ops:
  50.4 14.0 %all-to-all-start.1 = ((f32[128,1,128]{2,1,0:T(1,128)}), f32[128,1,128]{2,1,0:T(1,128)S(1)}, u32[]{:S(2)}, u32[]{:S(2)}) async-start(f32[128,1,128]{2,1,0:T(1,128)} %bitcast.5), calls=%async_computation.1 | async-start | bytes 131072 | tf_op jit(solution)/shard_map/all_to_all | solution.py:152

commit v18 on v11

--- a/solution.py
+++ b/solution.py
@@ -102,11 +102,11 @@
         got_rows, got_rows, (((1,), (1,)), ((), ())), preferred_element_type=jnp.float32
     )
     usable = (
-        got_valid[None, :]
+        got_valid[:, None]
         & (got_sub[:, None] == got_sub[None, :])
-        & (got_ids[None, :] < got_ids[:, None])
+        & (got_ids[:, None] < got_ids[None, :])
     )
-    best = jnp.max(jnp.where(usable, cosine, jnp.float32(-1.0)), axis=1)
+    best = jnp.max(jnp.where(usable, cosine, jnp.float32(-1.0)), axis=0)
 
     wide = jnp.pad(best.reshape(devices, CHUNK), ((0, 0), (0, LANES - CHUNK)))
     returned = lax.all_to_all(wide, AXES, 0, 0, tiled=True)[:, :CHUNK]

time: 66.4 us -> 66.6 us (level)
  no operation moved by 1% of the time
where the time goes in v18:
time: 66.6 us; the launch traced here: 65.6 us
  blocking collectives  54.4 us (82%)
  matrix products  3.32 us (5%)
  local copies, waits for them, and re-layouts  3.29 us (5%)
  Pallas kernels  2.33 us (3%)
  other arithmetic  2.08 us (3%)
    all_to_all x1, blocking collectives, on_device(): got = lax.all_to_all(send, AXES, 0, 0, tiled=True)  40.9 us
    all_to_all x1, blocking collectives, on_device(): returned = lax.all_to_all(wide, AXES, 0, 0, tiled=True)[:, :CHUNK]  13.5 us
    dot_general x1, matrix products, on_device(): lax.dot_general(got_rows, got_rows, (((1,), (1,)), ((), ())), preferred_e...  3.32 us
    pallas_call x1, Pallas kernels, pack(): pl.pallas_call(pack_kernel, out_shape=jax.ShapeDtypeStruct((slots, feat_w...  2.33 us
    unnamed x2, local copies, waits for them, and re-layouts  1.67 us

profile of v18, /device:TPU:0, one launch (start us, length us, event | category | flops | bytes accessed | tf_op | source)
XLA Modules:
  0.0 65.6 jit_solution(11580077719646641671)
XLA Ops:
  0.0 0.8 %concatenate.3 = s32[1160]{0:T(1024)S(1)} concatenate(s32[576]{0:T(1024)} %param.5, s32[576]{0:T(1024)} %param.6, s32[8]{0:T(128)} %bitcast.18), dimensions={0} | concatenate | bytes 9280 | tf_op jit(solution)/shard_map/concatenate | solution.py:68
  0.8 0.1 add_select_fusion
  0.9 0.1 select_reduce_fusion.2
  1.0 0.1 convert_reduce_fusion.1
  1.1 0.1 add_select_fusion.1
  1.2 0.1 add_select_fusion.4
  1.2 0.3 convert_reduce_fusion
  1.6 0.1 pad.8.clone
  1.6 0.1 pad.7.clone
  1.8 0.1 copy.18.cols_ref
  2.0 0.1 add_add_fusion.idx_ref
  2.1 0.0 copy-start
  2.1 1.7 %copy-done = f32[576,1024]{1,0:T(8,128)S(1)} copy-done((f32[576,1024]{1,0:T(8,128)S(1)}, f32[576,1024]{1,0:T(8,128)}, u32[]{:S(2)}) %copy-start) | copy-done | bytes 2359320
  3.7 2.3 %shard_map.46 = bf16[1024,1024]{1,0:T(8,128)(2,1)S(1)} custom-call(f32[576,1024]{1,0:T(8,128)S(1)} %copy-done, s32[8,576]{1,0:T(8,128)S(1)} %add_add_fusion.idx_ref, s32[576,8]{1,0:T(8,128)S(1)} %copy.18.cols_ref), custom_call_target="tpu_custom_call" | custom-call | tf_op jit(solution)/shard_map/pallas_call | solution.py:53
  6.1 40.9 %all_to_all.17 = bf16[128,8,1024]{2,1,0:T(8,128)(2,1)S(1)} all-to-all(bf16[128,8,1024]{2,1,0:T(8,128)(2,1)S(1)} %bitcast.13), channel_id=1, replica_groups=mesh['group'=8,'blk'=16] {'group','blk'}, dimensions={0} | all-to-all | bytes 4194304 | tf_op jit(solution)/shard_map/all_to_all | solution.py:90
  47.0 0.1 slice_convert_fusion
  47.1 0.1 fusion.15
  47.2 0.1 gt.15
  47.4 0.1 eq.51
  47.4 0.1 add.62
  47.5 3.3 %select_reduce_fusion = f32[1024]{0:T(1024)S(1)} fusion(bf16[128,8,1024]{2,1,0:T(8,128)(2,1)S(1)} %all_to_all.17, s32[1024]{0:T(1024)S(1)} %add.62, s32[1024]{0:T(1024)S(1)} %eq.51, pred[1024]{0:T(1024)(128)(4,1)S(1)} %gt.15), kind=kOutput, calls=%fused_computation | convolution fusion | flops 2153774080 | bytes 2110464 | tf_op jit(solution)/shard_map/dot_general | solution.py:101
  50.9 0.1 reshape.73
  51.0 13.5 %all_to_all.18 = f32[128,1,128]{2,1,0:T(1,128)S(1)} all-to-all(f32[128,1,128]{2,1,0:T(1,128)S(1)} %bitcast.16), channel_id=1, replica_groups=mesh['group'=8,'blk'=16] {'group','blk'}, dimensions={0} | all-to-all | bytes 131072 | tf_op jit(solution)/shard_map/all_to_all | solution.py:112
  64.5 0.1 broadcast_in_dim.50
  64.6 1.0 %select_reduce_fusion.1 = f32[576]{0:T(1024)} fusion(f32[1024]{0:T(1024)S(1)} %broadcast_in_dim.50, s32[576]{0:T(1024)S(1)} %multiply_add_fusion.1), kind=kLoop, calls=%fused_computation.1 | loop fusion | flops 1768896 | bytes 8704 | tf_op jit(solution)/shard_map/reduce_sum | solution.py:113
  (17 shorter events, 0.1 us)
Async XLA Ops:
  2.1 1.7 %copy-start = (f32[576,1024]{1,0:T(8,128)S(1)}, f32[576,1024]{1,0:T(8,128)}, u32[]{:S(2)}) copy-start(f32[576,1024]{1,0:T(8,128)} %x_ref.1) | copy-start | bytes 7077892

commit v19 on v11

--- a/solution.py
+++ b/solution.py
@@ -110,7 +110,12 @@
 
     wide = jnp.pad(best.reshape(devices, CHUNK), ((0, 0), (0, LANES - CHUNK)))
     returned = lax.all_to_all(wide, AXES, 0, 0, tiled=True)[:, :CHUNK]
-    return jnp.sum(jnp.where(picks, returned.reshape(slots, 1), jnp.float32(0.0)), axis=0)
+    return jnp.dot(
+        returned.reshape(1, slots),
+        picks.astype(jnp.float32),
+        precision=lax.Precision.HIGHEST,
+        preferred_element_type=jnp.float32,
+    ).reshape(row_count)
 
 
 def solution(mesh):

time: 66.4 us -> 66.9 us (level)
  matrix products: 3.12 us -> 4.61 us
  other arithmetic: 2.08 us -> 1.07 us
    dot_general x0 -> x1, matrix products: none -> 1.5 us  [on_device(): jnp.dot(returned.reshape(1, slots), picks.astype(jnp.float32), precision=...]
    reduce_sum x1 -> x0, other arithmetic: 1 us -> none  [on_device(): jnp.sum(jnp.where(picks, returned.reshape(slots, 1), jnp.float32(0.0)), a...]
where the time goes in v19:
time: 66.9 us; the launch traced here: 65.9 us
  blocking collectives  54.4 us (81%)
  matrix products  4.61 us (7%)
  local copies, waits for them, and re-layouts  3.3 us (5%)
  Pallas kernels  2.33 us (3%)
  other arithmetic  1.07 us (2%)
    all_to_all x1, blocking collectives, on_device(): got = lax.all_to_all(send, AXES, 0, 0, tiled=True)  40.9 us
    all_to_all x1, blocking collectives, on_device(): returned = lax.all_to_all(wide, AXES, 0, 0, tiled=True)[:, :CHUNK]  13.5 us
    dot_general x1, matrix products, on_device(): lax.dot_general(got_rows, got_rows, (((1,), (1,)), ((), ())), preferred_e...  3.12 us
    pallas_call x1, Pallas kernels, pack(): pl.pallas_call(pack_kernel, out_shape=jax.ShapeDtypeStruct((slots, feat_w...  2.33 us
    unnamed x2, local copies, waits for them, and re-layouts  1.67 us
    dot_general x1, matrix products, on_device(): jnp.dot(returned.reshape(1, slots), picks.astype(jnp.float32), precision=...  1.5 us

profile of v19, /device:TPU:0, one launch (start us, length us, event | category | flops | bytes accessed | tf_op | source)
XLA Modules:
  0.0 65.9 jit_solution(18410328573851414333)
XLA Ops:
  0.0 0.8 %concatenate.3 = s32[1160]{0:T(1024)S(1)} concatenate(s32[576]{0:T(1024)} %param.5, s32[576]{0:T(1024)} %param.6, s32[8]{0:T(128)} %bitcast.19), dimensions={0} | concatenate | bytes 9280 | tf_op jit(solution)/shard_map/concatenate | solution.py:68
  0.8 0.1 add_select_fusion
  0.9 0.1 select_reduce_fusion.1
  1.0 0.1 convert_reduce_fusion.1
  1.1 0.1 add_select_fusion.1
  1.2 0.1 add_select_fusion.4
  1.2 0.3 convert_reduce_fusion
  1.6 0.1 pad.8.clone
  1.6 0.1 pad.7.clone
  1.8 0.1 copy.18.cols_ref
  2.0 0.1 add_add_fusion.idx_ref
  2.1 0.0 copy-start
  2.1 1.7 %copy-done = f32[576,1024]{1,0:T(8,128)S(1)} copy-done((f32[576,1024]{1,0:T(8,128)S(1)}, f32[576,1024]{1,0:T(8,128)}, u32[]{:S(2)}) %copy-start) | copy-done | bytes 2359320
  3.7 2.3 %shard_map.46 = bf16[1024,1024]{1,0:T(8,128)(2,1)S(1)} custom-call(f32[576,1024]{1,0:T(8,128)S(1)} %copy-done, s32[8,576]{1,0:T(8,128)S(1)} %add_add_fusion.idx_ref, s32[576,8]{1,0:T(8,128)S(1)} %copy.18.cols_ref), custom_call_target="tpu_custom_call" | custom-call | tf_op jit(solution)/shard_map/pallas_call | solution.py:53
  6.1 40.9 %all_to_all.17 = bf16[128,8,1024]{2,1,0:T(8,128)(2,1)S(1)} all-to-all(bf16[128,8,1024]{2,1,0:T(8,128)(2,1)S(1)} %bitcast.14), channel_id=1, replica_groups=mesh['group'=8,'blk'=16] {'group','blk'}, dimensions={0} | all-to-all | bytes 4194304 | tf_op jit(solution)/shard_map/all_to_all | solution.py:90
  47.0 0.1 slice_convert_fusion
  47.1 0.1 fusion.18
  47.2 0.1 gt.15
  47.4 0.1 eq.48
  47.4 0.1 add.62
  47.5 3.1 %select_reduce_fusion = f32[1024]{0:T(1024)S(1)} fusion(bf16[128,8,1024]{2,1,0:T(8,128)(2,1)S(1)} %all_to_all.17, s32[1024]{0:T(1024)S(1)} %add.62, s32[1024]{0:T(1024)S(1)} %eq.48, pred[1024]{0:T(1024)(128)(4,1)S(1)} %gt.15), kind=kOutput, calls=%fused_computation | convolution fusion | flops 2153774080 | bytes 2110464 | tf_op jit(solution)/shard_map/dot_general | solution.py:101
  50.7 0.1 reshape.79
  50.8 13.5 %all_to_all.18 = f32[128,1,128]{2,1,0:T(1,128)S(1)} all-to-all(f32[128,1,128]{2,1,0:T(1,128)S(1)} %bitcast.17), channel_id=1, replica_groups=mesh['group'=8,'blk'=16] {'group','blk'}, dimensions={0} | all-to-all | bytes 131072 | tf_op jit(solution)/shard_map/all_to_all | solution.py:112
  64.3 0.1 reshape.82
  64.4 1.5 %fusion.7 = f32[576]{0:T(1024)} fusion(f32[1024,1]{0,1:T(1,128)S(1)} %reshape.82, s32[576]{0:T(1024)S(1)} %multiply_add_fusion.1), kind=kOutput, calls=%fused_computation.9 | convolution fusion | flops 7667712 | bytes 8704 | tf_op jit(solution)/shard_map/dot_general | solution.py:113
  (17 shorter events, 0.1 us)
Async XLA Ops:
  2.1 1.7 %copy-start = (f32[576,1024]{1,0:T(8,128)S(1)}, f32[576,1024]{1,0:T(8,128)}, u32[]{:S(2)}) copy-start(f32[576,1024]{1,0:T(8,128)} %x_ref.1) | copy-start | bytes 7077892

commit v20 on v11

--- a/solution.py
+++ b/solution.py
@@ -85,7 +85,7 @@
         embeddings, slot, dest * CHUNK + CHUNK - 1, rank, meta_digits(cluster, global_index), slots
     ).reshape(devices, CHUNK, feat_width)
     slot_ids = jnp.arange(slots, dtype=jnp.int32)
-    picks = slot_ids[:, None] == slot[None, :]
+    picks = slot[:, None] == slot_ids[None, :]
 
     got = lax.all_to_all(send, AXES, 0, 0, tiled=True)
     got_rows = got.reshape(slots, feat_width)
@@ -110,7 +110,7 @@
 
     wide = jnp.pad(best.reshape(devices, CHUNK), ((0, 0), (0, LANES - CHUNK)))
     returned = lax.all_to_all(wide, AXES, 0, 0, tiled=True)[:, :CHUNK]
-    return jnp.sum(jnp.where(picks, returned.reshape(slots, 1), jnp.float32(0.0)), axis=0)
+    return jnp.sum(jnp.where(picks, returned.reshape(1, slots), jnp.float32(0.0)), axis=1)
 
 
 def solution(mesh):

time: 66.4 us -> 66.4 us (level)
  no operation moved by 1% of the time
where the time goes in v20:
time: 66.4 us; the launch traced here: 65.4 us
  blocking collectives  54.4 us (82%)
  local copies, waits for them, and re-layouts  3.29 us (5%)
  matrix products  3.12 us (5%)
  Pallas kernels  2.33 us (4%)
  other arithmetic  2.08 us (3%)
    all_to_all x1, blocking collectives, on_device(): got = lax.all_to_all(send, AXES, 0, 0, tiled=True)  40.9 us
    all_to_all x1, blocking collectives, on_device(): returned = lax.all_to_all(wide, AXES, 0, 0, tiled=True)[:, :CHUNK]  13.5 us
    dot_general x1, matrix products, on_device(): lax.dot_general(got_rows, got_rows, (((1,), (1,)), ((), ())), preferred_e...  3.12 us
    pallas_call x1, Pallas kernels, pack(): pl.pallas_call(pack_kernel, out_shape=jax.ShapeDtypeStruct((slots, feat_w...  2.33 us
    unnamed x2, local copies, waits for them, and re-layouts  1.67 us

profile of v20, /device:TPU:0, one launch (start us, length us, event | category | flops | bytes accessed | tf_op | source)
XLA Modules:
  0.0 65.4 jit_solution(15406208153578224096)
XLA Ops:
  0.0 0.8 %concatenate.3 = s32[1160]{0:T(1024)S(1)} concatenate(s32[576]{0:T(1024)} %param.5, s32[576]{0:T(1024)} %param.6, s32[8]{0:T(128)} %bitcast.18), dimensions={0} | concatenate | bytes 9280 | tf_op jit(solution)/shard_map/concatenate | solution.py:68
  0.8 0.1 add_select_fusion
  0.9 0.1 select_reduce_fusion.2
  1.0 0.1 convert_reduce_fusion.1
  1.1 0.1 add_select_fusion.1
  1.2 0.1 add_select_fusion.4
  1.2 0.3 convert_reduce_fusion
  1.6 0.1 pad.8.clone
  1.6 0.1 pad.7.clone
  1.8 0.1 copy.18.cols_ref
  2.0 0.1 add_add_fusion.idx_ref
  2.1 0.0 copy-start
  2.1 1.7 %copy-done = f32[576,1024]{1,0:T(8,128)S(1)} copy-done((f32[576,1024]{1,0:T(8,128)S(1)}, f32[576,1024]{1,0:T(8,128)}, u32[]{:S(2)}) %copy-start) | copy-done | bytes 2359320
  3.7 2.3 %shard_map.46 = bf16[1024,1024]{1,0:T(8,128)(2,1)S(1)} custom-call(f32[576,1024]{1,0:T(8,128)S(1)} %copy-done, s32[8,576]{1,0:T(8,128)S(1)} %add_add_fusion.idx_ref, s32[576,8]{1,0:T(8,128)S(1)} %copy.18.cols_ref), custom_call_target="tpu_custom_call" | custom-call | tf_op jit(solution)/shard_map/pallas_call | solution.py:53
  6.1 40.9 %all_to_all.17 = bf16[128,8,1024]{2,1,0:T(8,128)(2,1)S(1)} all-to-all(bf16[128,8,1024]{2,1,0:T(8,128)(2,1)S(1)} %bitcast.13), channel_id=1, replica_groups=mesh['group'=8,'blk'=16] {'group','blk'}, dimensions={0} | all-to-all | bytes 4194304 | tf_op jit(solution)/shard_map/all_to_all | solution.py:90
  47.0 0.1 slice_convert_fusion
  47.1 0.1 fusion.15
  47.2 0.1 gt.15
  47.4 0.1 eq.51
  47.4 0.1 add.62
  47.5 3.1 %select_reduce_fusion = f32[1024]{0:T(1024)S(1)} fusion(bf16[128,8,1024]{2,1,0:T(8,128)(2,1)S(1)} %all_to_all.17, s32[1024]{0:T(1024)S(1)} %add.62, s32[1024]{0:T(1024)S(1)} %eq.51, pred[1024]{0:T(1024)(128)(4,1)S(1)} %gt.15), kind=kOutput, calls=%fused_computation | convolution fusion | flops 2153774080 | bytes 2110464 | tf_op jit(solution)/shard_map/dot_general | solution.py:101
  50.7 0.1 reshape.73
  50.8 13.5 %all_to_all.18 = f32[128,1,128]{2,1,0:T(1,128)S(1)} all-to-all(f32[128,1,128]{2,1,0:T(1,128)S(1)} %bitcast.16), channel_id=1, replica_groups=mesh['group'=8,'blk'=16] {'group','blk'}, dimensions={0} | all-to-all | bytes 131072 | tf_op jit(solution)/shard_map/all_to_all | solution.py:112
  64.3 0.1 broadcast_in_dim.47
  64.4 1.0 %select_reduce_fusion.1 = f32[576]{0:T(1024)} fusion(f32[1024]{0:T(1024)S(1)} %broadcast_in_dim.47, s32[576]{0:T(1024)S(1)} %multiply_add_fusion.1), kind=kLoop, calls=%fused_computation.1 | loop fusion | flops 1768896 | bytes 8704 | tf_op jit(solution)/shard_map/reduce_sum | solution.py:113
  (17 shorter events, 0.1 us)
Async XLA Ops:
  2.1 1.7 %copy-start = (f32[576,1024]{1,0:T(8,128)S(1)}, f32[576,1024]{1,0:T(8,128)}, u32[]{:S(2)}) copy-start(f32[576,1024]{1,0:T(8,128)} %x_ref.1) | copy-start | bytes 7077892

commit v21 on v11

--- a/solution.py
+++ b/solution.py
@@ -92,11 +92,14 @@
     coded = got[:, CHUNK - 1, : META_DIGITS * CHUNK].astype(jnp.int32)
 
     def digit(t):
-        return coded[:, t * CHUNK : (t + 1) * CHUNK].reshape(slots)
+        return coded[:, t * CHUNK : (t + 1) * CHUNK]
 
-    got_valid = digit(0) > 0
-    got_sub = digit(1)
-    got_ids = digit(2) * 4096 + digit(3) * 64 + digit(4)
+    packed = (
+        (digit(2) * 4096 + digit(3) * 64 + digit(4)) * 8 + digit(1) * 2 + digit(0)
+    ).reshape(slots)
+    got_valid = (packed & 1) > 0
+    got_sub = (packed >> 1) & 3
+    got_ids = packed >> 3
 
     cosine = lax.dot_general(
         got_rows, got_rows, (((1,), (1,)), ((), ())), preferred_element_type=jnp.float32

time: 66.4 us -> 66.6 us (level)
    unnamed x2 -> x3, local copies, waits for them, and re-layouts: 1.67 us -> 1.75 us
where the time goes in v21:
time: 66.6 us; the launch traced here: 65.6 us
  blocking collectives  54.4 us (82%)
  local copies, waits for them, and re-layouts  3.77 us (6%)
  matrix products  3.1 us (5%)
  Pallas kernels  2.33 us (3%)
  other arithmetic  1.85 us (3%)
    all_to_all x1, blocking collectives, on_device(): got = lax.all_to_all(send, AXES, 0, 0, tiled=True)  40.9 us
    all_to_all x1, blocking collectives, on_device(): returned = lax.all_to_all(wide, AXES, 0, 0, tiled=True)[:, :CHUNK]  13.5 us
    dot_general x1, matrix products, on_device(): lax.dot_general(got_rows, got_rows, (((1,), (1,)), ((), ())), preferred_e...  3.1 us
    pallas_call x1, Pallas kernels, pack(): pl.pallas_call(pack_kernel, out_shape=jax.ShapeDtypeStruct((slots, feat_w...  2.33 us
    unnamed x3, local copies, waits for them, and re-layouts  1.75 us

profile of v21, /device:TPU:0, one launch (start us, length us, event | category | flops | bytes accessed | tf_op | source)
XLA Modules:
  0.0 65.6 jit_solution(11598010107867965451)
XLA Ops:
  0.0 0.8 %concatenate.3 = s32[1160]{0:T(1024)S(1)} concatenate(s32[576]{0:T(1024)} %param.5, s32[576]{0:T(1024)} %param.6, s32[8]{0:T(128)} %bitcast.18), dimensions={0} | concatenate | bytes 9280 | tf_op jit(solution)/shard_map/concatenate | solution.py:68
  0.8 0.1 add_select_fusion
  0.9 0.1 select_reduce_fusion.2
  1.0 0.1 convert_reduce_fusion.1
  1.1 0.1 add_select_fusion.1
  1.2 0.1 add_select_fusion.4
  1.2 0.3 convert_reduce_fusion
  1.6 0.1 pad.8.clone
  1.6 0.1 pad.7.clone
  1.8 0.1 copy.27.cols_ref
  2.0 0.1 add_add_fusion.idx_ref
  2.1 0.0 copy-start
  2.1 1.7 %copy-done = f32[576,1024]{1,0:T(8,128)S(1)} copy-done((f32[576,1024]{1,0:T(8,128)S(1)}, f32[576,1024]{1,0:T(8,128)}, u32[]{:S(2)}) %copy-start) | copy-done | bytes 2359320
  3.7 2.3 %shard_map.46 = bf16[1024,1024]{1,0:T(8,128)(2,1)S(1)} custom-call(f32[576,1024]{1,0:T(8,128)S(1)} %copy-done, s32[8,576]{1,0:T(8,128)S(1)} %add_add_fusion.idx_ref, s32[576,8]{1,0:T(8,128)S(1)} %copy.27.cols_ref), custom_call_target="tpu_custom_call" | custom-call | tf_op jit(solution)/shard_map/pallas_call | solution.py:53
  6.1 40.9 %all_to_all.17 = bf16[128,8,1024]{2,1,0:T(8,128)(2,1)S(1)} all-to-all(bf16[128,8,1024]{2,1,0:T(8,128)(2,1)S(1)} %bitcast.15), channel_id=1, replica_groups=mesh['group'=8,'blk'=16] {'group','blk'}, dimensions={0} | all-to-all | bytes 4194304 | tf_op jit(solution)/shard_map/all_to_all | solution.py:90
  47.0 0.1 slice.43
  47.0 0.1 copy.33
  47.2 0.1 copy.29
  47.3 0.1 gt.15
  47.4 0.1 copy.30
  47.5 0.1 and.72
  47.6 0.1 copy.31
  47.7 0.1 shift_right_arithmetic.28
  47.8 3.1 %select_reduce_fusion = f32[1024]{0:T(1024)S(1)} fusion(bf16[128,8,1024]{2,1,0:T(8,128)(2,1)S(1)} %all_to_all.17, s32[1024]{0:T(1024)S(1)} %shift_right_arithmetic.28, s32[1024]{0:T(1024)S(1)} %and.72, pred[1024]{0:T(1024)(128)(4,1)S(1)} %gt.15), kind=kOutput, calls=%fused_computation | convolution fusion | flops 2153774080 | bytes 2110464 | tf_op jit(solution)/shard_map/dot_general | solution.py:104
  50.9 0.1 reshape.61
  51.0 13.5 %all_to_all.18 = f32[128,1,128]{2,1,0:T(1,128)S(1)} all-to-all(f32[128,1,128]{2,1,0:T(1,128)S(1)} %bitcast.16), channel_id=1, replica_groups=mesh['group'=8,'blk'=16] {'group','blk'}, dimensions={0} | all-to-all | bytes 131072 | tf_op jit(solution)/shard_map/all_to_all | solution.py:115
  64.6 0.1 broadcast_in_dim.52
  64.6 1.0 %select_reduce_fusion.1 = f32[576]{0:T(1024)} fusion(f32[1024]{0:T(1024)S(1)} %broadcast_in_dim.52, s32[576]{0:T(1024)S(1)} %multiply_add_fusion.1), kind=kLoop, calls=%fused_computation.1 | loop fusion | flops 1768896 | bytes 8704 | tf_op jit(solution)/shard_map/reduce_sum | solution.py:116
  (19 shorter events, 0.1 us)
Async XLA Ops:
  2.1 1.7 %copy-start = (f32[576,1024]{1,0:T(8,128)S(1)}, f32[576,1024]{1,0:T(8,128)}, u32[]{:S(2)}) copy-start(f32[576,1024]{1,0:T(8,128)} %x_ref.1) | copy-start | bytes 7077892

commit v22 on v14

--- a/solution.py
+++ b/solution.py
@@ -35,27 +35,26 @@
     ]
     for copy in copies:
         copy.start()
-    for j, copy in enumerate(copies):
-        copy.wait()
-        x = x_buf[pl.ds(j * piece, piece), :]
-        squares = jnp.sum(x * x, axis=1, keepdims=True)
-        unit_buf[pl.ds(j * piece, piece), :] = (x * lax.rsqrt(squares + 1e-06)).astype(jnp.bfloat16)
-    unit = unit_buf[...]
-    x_ref = x_buf
-    row_count = x_ref.shape[0]
+    row_count = x_buf.shape[0]
     slots = out_ref.shape[0]
-    slot_at = lax.broadcasted_iota(jnp.int32, (slots, row_count), 0)
-    picks = (slot_at == idx_ref[0:1, :]).astype(jnp.bfloat16)
-    rows = jnp.dot(picks, unit, preferred_element_type=jnp.float32)
-    out_ref[...] = rows.astype(jnp.bfloat16)
 
     cols = cols_ref[...]
     column = lax.broadcasted_iota(jnp.int32, (row_count, LANES), 1)
     spread = jnp.zeros((row_count, LANES), jnp.int32)
     for t in range(META_DIGITS):
         spread = jnp.where(column == t * CHUNK + cols[:, 0:1], cols[:, t + 1 : t + 2], spread)
+    slot_at = lax.broadcasted_iota(jnp.int32, (slots, row_count), 0)
     meta_picks = (slot_at == idx_ref[1:2, :]).astype(jnp.bfloat16)
     meta = jnp.dot(meta_picks, spread.astype(jnp.bfloat16), preferred_element_type=jnp.float32)
+    picks = (slot_at == idx_ref[0:1, :]).astype(jnp.bfloat16)
+
+    for j, copy in enumerate(copies):
+        copy.wait()
+        x = x_buf[pl.ds(j * piece, piece), :]
+        squares = jnp.sum(x * x, axis=1, keepdims=True)
+        unit_buf[pl.ds(j * piece, piece), :] = (x * lax.rsqrt(squares + 1e-06)).astype(jnp.bfloat16)
+    rows = jnp.dot(picks, unit_buf[...], preferred_element_type=jnp.float32)
+    out_ref[...] = rows.astype(jnp.bfloat16)
     out_ref[:, :LANES] = (rows[:, :LANES] + meta).astype(jnp.bfloat16)
 
 

time: 66.3 us -> 67 us (1.011)
  Pallas kernels: 3.92 us -> 4.68 us
    pallas_call x1, Pallas kernels: 3.92 us -> 4.68 us  [pack(): pl.pallas_call(pack_kernel, out_shape=jax.ShapeDtypeStruct((slots, feat_w...]
where the time goes in v22:
time: 67 us; the launch traced here: 66.1 us
  blocking collectives  54.4 us (81%)
  Pallas kernels  4.68 us (7%)
  matrix products  3.12 us (5%)
  other arithmetic  2.08 us (3%)
  local copies, waits for them, and re-layouts  1.62 us (2%)
    all_to_all x1, blocking collectives, on_device(): got = lax.all_to_all(send, AXES, 0, 0, tiled=True)  40.9 us
    all_to_all x1, blocking collectives, on_device(): returned = lax.all_to_all(wide, AXES, 0, 0, tiled=True)[:, :CHUNK]  13.5 us
    pallas_call x1, Pallas kernels, pack(): pl.pallas_call(pack_kernel, out_shape=jax.ShapeDtypeStruct((slots, feat_w...  4.68 us
    dot_general x1, matrix products, on_device(): lax.dot_general(got_rows, got_rows, (((1,), (1,)), ((), ())), preferred_e...  3.12 us

profile of v22, /device:TPU:0, one launch (start us, length us, event | category | flops | bytes accessed | tf_op | source)
XLA Modules:
  0.0 66.1 jit_solution(4401629974115276631)
XLA Ops:
  0.0 0.8 %concatenate.3 = s32[1160]{0:T(1024)S(1)} concatenate(s32[576]{0:T(1024)} %param.5, s32[576]{0:T(1024)} %param.6, s32[8]{0:T(128)} %bitcast.18), dimensions={0} | concatenate | bytes 9280 | tf_op jit(solution)/shard_map/concatenate | solution.py:87
  0.8 0.1 add_select_fusion
  0.9 0.1 select_reduce_fusion.2
  1.0 0.1 convert_reduce_fusion.1
  1.1 0.1 add_select_fusion.1
  1.2 0.1 add_select_fusion.4
  1.2 0.3 convert_reduce_fusion
  1.6 0.1 pad.8.clone
  1.6 0.1 pad.7.clone
  1.8 0.1 copy.18.cols_ref
  2.0 0.1 add_add_fusion.idx_ref
  2.1 4.7 %shard_map.46 = bf16[1024,1024]{1,0:T(8,128)(2,1)S(1)} custom-call(f32[576,1024]{1,0:T(8,128)} %x_hbm.1, s32[8,576]{1,0:T(8,128)S(1)} %add_add_fusion.idx_ref, s32[576,8]{1,0:T(8,128)S(1)} %copy.18.cols_ref), custom_call_target="tpu_custom_call" | custom-call | tf_op jit(solution)/shard_map/pallas_call | solution.py:67
  6.7 40.9 %all_to_all.17 = bf16[128,8,1024]{2,1,0:T(8,128)(2,1)S(1)} all-to-all(bf16[128,8,1024]{2,1,0:T(8,128)(2,1)S(1)} %bitcast.13), channel_id=1, replica_groups=mesh['group'=8,'blk'=16] {'group','blk'}, dimensions={0} | all-to-all | bytes 4194304 | tf_op jit(solution)/shard_map/all_to_all | solution.py:109
  47.7 0.1 slice_convert_fusion
  47.8 0.1 fusion.15
  47.9 0.1 gt.15
  48.0 0.1 eq.51
  48.1 0.1 add.62
  48.2 3.1 %select_reduce_fusion = f32[1024]{0:T(1024)S(1)} fusion(bf16[128,8,1024]{2,1,0:T(8,128)(2,1)S(1)} %all_to_all.17, s32[1024]{0:T(1024)S(1)} %add.62, s32[1024]{0:T(1024)S(1)} %eq.51, pred[1024]{0:T(1024)(128)(4,1)S(1)} %gt.15), kind=kOutput, calls=%fused_computation | convolution fusion | flops 2153774080 | bytes 2110464 | tf_op jit(solution)/shard_map/dot_general | solution.py:120
  51.3 0.1 reshape.73
  51.4 13.5 %all_to_all.18 = f32[128,1,128]{2,1,0:T(1,128)S(1)} all-to-all(f32[128,1,128]{2,1,0:T(1,128)S(1)} %bitcast.16), channel_id=1, replica_groups=mesh['group'=8,'blk'=16] {'group','blk'}, dimensions={0} | all-to-all | bytes 131072 | tf_op jit(solution)/shard_map/all_to_all | solution.py:131
  65.0 0.1 broadcast_in_dim.50
  65.1 1.0 %select_reduce_fusion.1 = f32[576]{0:T(1024)} fusion(f32[1024]{0:T(1024)S(1)} %broadcast_in_dim.50, s32[576]{0:T(1024)S(1)} %multiply_add_fusion.1), kind=kLoop, calls=%fused_computation.1 | loop fusion | flops 1768896 | bytes 8704 | tf_op jit(solution)/shard_map/reduce_sum | solution.py:132
  (17 shorter events, 0.1 us)

commit v23 on v11

--- a/solution.py
+++ b/solution.py
@@ -32,7 +32,7 @@
     slot_at = lax.broadcasted_iota(jnp.int32, (slots, row_count), 0)
     picks = (slot_at == idx_ref[0:1, :]).astype(jnp.bfloat16)
     rows = jnp.dot(picks, unit, preferred_element_type=jnp.float32)
-    out_ref[...] = rows.astype(jnp.bfloat16)
+    out_ref[:, LANES:] = rows[:, LANES:].astype(jnp.bfloat16)
 
     cols = cols_ref[...]
     column = lax.broadcasted_iota(jnp.int32, (row_count, LANES), 1)

time: 66.4 us -> 66.4 us (level)
  no operation moved by 1% of the time
where the time goes in v23:
time: 66.4 us; the launch traced here: 65.4 us
  blocking collectives  54.4 us (82%)
  local copies, waits for them, and re-layouts  3.29 us (5%)
  matrix products  3.11 us (5%)
  Pallas kernels  2.32 us (3%)
  other arithmetic  2.08 us (3%)
    all_to_all x1, blocking collectives, on_device(): got = lax.all_to_all(send, AXES, 0, 0, tiled=True)  40.9 us
    all_to_all x1, blocking collectives, on_device(): returned = lax.all_to_all(wide, AXES, 0, 0, tiled=True)[:, :CHUNK]  13.5 us
    dot_general x1, matrix products, on_device(): lax.dot_general(got_rows, got_rows, (((1,), (1,)), ((), ())), preferred_e...  3.11 us
    pallas_call x1, Pallas kernels, pack(): pl.pallas_call(pack_kernel, out_shape=jax.ShapeDtypeStruct((slots, feat_w...  2.32 us
    unnamed x2, local copies, waits for them, and re-layouts  1.67 us

profile of v23, /device:TPU:0, one launch (start us, length us, event | category | flops | bytes accessed | tf_op | source)
XLA Modules:
  0.0 65.4 jit_solution(5861566216426148982)
XLA Ops:
  0.0 0.8 %concatenate.3 = s32[1160]{0:T(1024)S(1)} concatenate(s32[576]{0:T(1024)} %param.5, s32[576]{0:T(1024)} %param.6, s32[8]{0:T(128)} %bitcast.18), dimensions={0} | concatenate | bytes 9280 | tf_op jit(solution)/shard_map/concatenate | solution.py:68
  0.8 0.1 add_select_fusion
  0.9 0.1 select_reduce_fusion.2
  1.0 0.1 convert_reduce_fusion.1
  1.1 0.1 add_select_fusion.1
  1.2 0.1 add_select_fusion.4
  1.2 0.3 convert_reduce_fusion
  1.6 0.1 pad.8.clone
  1.6 0.1 pad.7.clone
  1.8 0.1 copy.18.cols_ref
  2.0 0.1 add_add_fusion.idx_ref
  2.1 0.0 copy-start
  2.1 1.7 %copy-done = f32[576,1024]{1,0:T(8,128)S(1)} copy-done((f32[576,1024]{1,0:T(8,128)S(1)}, f32[576,1024]{1,0:T(8,128)}, u32[]{:S(2)}) %copy-start) | copy-done | bytes 2359320
  3.7 2.3 %shard_map.46 = bf16[1024,1024]{1,0:T(8,128)(2,1)S(1)} custom-call(f32[576,1024]{1,0:T(8,128)S(1)} %copy-done, s32[8,576]{1,0:T(8,128)S(1)} %add_add_fusion.idx_ref, s32[576,8]{1,0:T(8,128)S(1)} %copy.18.cols_ref), custom_call_target="tpu_custom_call" | custom-call | tf_op jit(solution)/shard_map/pallas_call | solution.py:53
  6.1 40.9 %all_to_all.17 = bf16[128,8,1024]{2,1,0:T(8,128)(2,1)S(1)} all-to-all(bf16[128,8,1024]{2,1,0:T(8,128)(2,1)S(1)} %bitcast.13), channel_id=1, replica_groups=mesh['group'=8,'blk'=16] {'group','blk'}, dimensions={0} | all-to-all | bytes 4194304 | tf_op jit(solution)/shard_map/all_to_all | solution.py:90
  47.0 0.1 slice_convert_fusion
  47.1 0.1 fusion.15
  47.2 0.1 gt.15
  47.3 0.1 eq.51
  47.4 0.1 add.62
  47.5 3.1 %select_reduce_fusion = f32[1024]{0:T(1024)S(1)} fusion(bf16[128,8,1024]{2,1,0:T(8,128)(2,1)S(1)} %all_to_all.17, s32[1024]{0:T(1024)S(1)} %add.62, s32[1024]{0:T(1024)S(1)} %eq.51, pred[1024]{0:T(1024)(128)(4,1)S(1)} %gt.15), kind=kOutput, calls=%fused_computation | convolution fusion | flops 2153774080 | bytes 2110464 | tf_op jit(solution)/shard_map/dot_general | solution.py:101
  50.7 0.1 reshape.73
  50.8 13.5 %all_to_all.18 = f32[128,1,128]{2,1,0:T(1,128)S(1)} all-to-all(f32[128,1,128]{2,1,0:T(1,128)S(1)} %bitcast.16), channel_id=1, replica_groups=mesh['group'=8,'blk'=16] {'group','blk'}, dimensions={0} | all-to-all | bytes 131072 | tf_op jit(solution)/shard_map/all_to_all | solution.py:112
  64.3 0.1 broadcast_in_dim.50
  64.4 1.0 %select_reduce_fusion.1 = f32[576]{0:T(1024)} fusion(f32[1024]{0:T(1024)S(1)} %broadcast_in_dim.50, s32[576]{0:T(1024)S(1)} %multiply_add_fusion.1), kind=kLoop, calls=%fused_computation.1 | loop fusion | flops 1768896 | bytes 8704 | tf_op jit(solution)/shard_map/reduce_sum | solution.py:113
  (17 shorter events, 0.1 us)
Async XLA Ops:
  2.1 1.7 %copy-start = (f32[576,1024]{1,0:T(8,128)S(1)}, f32[576,1024]{1,0:T(8,128)}, u32[]{:S(2)}) copy-start(f32[576,1024]{1,0:T(8,128)} %x_ref.1) | copy-start | bytes 7077892

commit v24 on v11

--- a/solution.py
+++ b/solution.py
@@ -101,11 +101,9 @@
     cosine = lax.dot_general(
         got_rows, got_rows, (((1,), (1,)), ((), ())), preferred_element_type=jnp.float32
     )
-    usable = (
-        got_valid[None, :]
-        & (got_sub[:, None] == got_sub[None, :])
-        & (got_ids[None, :] < got_ids[:, None])
-    )
+    key = jnp.where(got_valid, got_sub * 131072 + got_ids, 1 << 30)
+    gap = key[:, None] - key[None, :]
+    usable = (gap > 0) & (gap <= got_ids[:, None])
     best = jnp.max(jnp.where(usable, cosine, jnp.float32(-1.0)), axis=1)
 
     wide = jnp.pad(best.reshape(devices, CHUNK), ((0, 0), (0, LANES - CHUNK)))

time: 66.4 us -> 65.9 us (level)
  no operation moved by 1% of the time
where the time goes in v24:
time: 65.9 us; the launch traced here: 64.9 us
  blocking collectives  54.4 us (83%)
  local copies, waits for them, and re-layouts  3.29 us (5%)
  matrix products  2.61 us (4%)
  Pallas kernels  2.33 us (4%)
  other arithmetic  2.08 us (3%)
    all_to_all x1, blocking collectives, on_device(): got = lax.all_to_all(send, AXES, 0, 0, tiled=True)  40.9 us
    all_to_all x1, blocking collectives, on_device(): returned = lax.all_to_all(wide, AXES, 0, 0, tiled=True)[:, :CHUNK]  13.5 us
    dot_general x1, matrix products, on_device(): lax.dot_general(got_rows, got_rows, (((1,), (1,)), ((), ())), preferred_e...  2.61 us
    pallas_call x1, Pallas kernels, pack(): pl.pallas_call(pack_kernel, out_shape=jax.ShapeDtypeStruct((slots, feat_w...  2.33 us
    unnamed x2, local copies, waits for them, and re-layouts  1.67 us

profile of v24, /device:TPU:0, one launch (start us, length us, event | category | flops | bytes accessed | tf_op | source)
XLA Modules:
  0.0 64.9 jit_solution(14967098556772454528)
XLA Ops:
  0.0 0.8 %concatenate.3 = s32[1160]{0:T(1024)S(1)} concatenate(s32[576]{0:T(1024)} %param.5, s32[576]{0:T(1024)} %param.6, s32[8]{0:T(128)} %bitcast.18), dimensions={0} | concatenate | bytes 9280 | tf_op jit(solution)/shard_map/concatenate | solution.py:68
  0.8 0.1 add_select_fusion
  0.9 0.1 select_reduce_fusion.2
  1.0 0.1 convert_reduce_fusion.1
  1.1 0.1 add_select_fusion.1
  1.2 0.1 add_select_fusion.4
  1.2 0.3 convert_reduce_fusion
  1.6 0.1 pad.8.clone
  1.6 0.1 pad.7.clone
  1.8 0.1 copy.18.cols_ref
  2.0 0.1 add_add_fusion.idx_ref
  2.1 0.0 copy-start
  2.1 1.7 %copy-done = f32[576,1024]{1,0:T(8,128)S(1)} copy-done((f32[576,1024]{1,0:T(8,128)S(1)}, f32[576,1024]{1,0:T(8,128)}, u32[]{:S(2)}) %copy-start) | copy-done | bytes 2359320
  3.7 2.3 %shard_map.46 = bf16[1024,1024]{1,0:T(8,128)(2,1)S(1)} custom-call(f32[576,1024]{1,0:T(8,128)S(1)} %copy-done, s32[8,576]{1,0:T(8,128)S(1)} %add_add_fusion.idx_ref, s32[576,8]{1,0:T(8,128)S(1)} %copy.18.cols_ref), custom_call_target="tpu_custom_call" | custom-call | tf_op jit(solution)/shard_map/pallas_call | solution.py:53
  6.1 40.9 %all_to_all.17 = bf16[128,8,1024]{2,1,0:T(8,128)(2,1)S(1)} all-to-all(bf16[128,8,1024]{2,1,0:T(8,128)(2,1)S(1)} %bitcast.13), channel_id=1, replica_groups=mesh['group'=8,'blk'=16] {'group','blk'}, dimensions={0} | all-to-all | bytes 4194304 | tf_op jit(solution)/shard_map/all_to_all | solution.py:90
  47.0 0.1 slice_convert_fusion
  47.1 0.1 slice_multiply_fusion.2
  47.3 0.1 gt.25
  47.4 0.1 mul.68
  47.4 0.1 add.79
  47.6 2.6 %select_reduce_fusion = f32[1024]{0:T(1024)S(1)} fusion(bf16[128,8,1024]{2,1,0:T(8,128)(2,1)S(1)} %all_to_all.17, s32[1024]{0:T(1024)S(1)} %add.79, s32[1024]{0:T(1024)S(1)} %add_select_fusion.6), kind=kOutput, calls=%fused_computation.2 | convolution fusion | flops 2153774080 | bytes 2109440 | tf_op jit(solution)/shard_map/dot_general | solution.py:101
  50.2 0.1 reshape.102
  50.3 13.5 %all_to_all.18 = f32[128,1,128]{2,1,0:T(1,128)S(1)} all-to-all(f32[128,1,128]{2,1,0:T(1,128)S(1)} %bitcast.16), channel_id=1, replica_groups=mesh['group'=8,'blk'=16] {'group','blk'}, dimensions={0} | all-to-all | bytes 131072 | tf_op jit(solution)/shard_map/all_to_all | solution.py:110
  63.8 0.1 broadcast_in_dim.55
  63.9 1.0 %select_reduce_fusion.1 = f32[576]{0:T(1024)} fusion(f32[1024]{0:T(1024)S(1)} %broadcast_in_dim.55, s32[576]{0:T(1024)S(1)} %multiply_add_fusion.1), kind=kLoop, calls=%fused_computation.4 | loop fusion | flops 1768896 | bytes 8704 | tf_op jit(solution)/shard_map/reduce_sum | solution.py:111
  (18 shorter events, 0.1 us)
Async XLA Ops:
  2.1 1.7 %copy-start = (f32[576,1024]{1,0:T(8,128)S(1)}, f32[576,1024]{1,0:T(8,128)}, u32[]{:S(2)}) copy-start(f32[576,1024]{1,0:T(8,128)} %x_ref.1) | copy-start | bytes 7077892

commit v25 on v24

--- a/solution.py
+++ b/solution.py
@@ -103,7 +103,7 @@
     )
     key = jnp.where(got_valid, got_sub * 131072 + got_ids, 1 << 30)
     gap = key[:, None] - key[None, :]
-    usable = (gap > 0) & (gap <= got_ids[:, None])
+    usable = (gap > 0) & (gap <= (key & 131071)[:, None])
     best = jnp.max(jnp.where(usable, cosine, jnp.float32(-1.0)), axis=1)
 
     wide = jnp.pad(best.reshape(devices, CHUNK), ((0, 0), (0, LANES - CHUNK)))

time: 65.9 us -> 65.7 us (level)
  no operation moved by 1% of the time
where the time goes in v25:
time: 65.7 us; the launch traced here: 64.7 us
  blocking collectives  54.4 us (83%)
  local copies, waits for them, and re-layouts  3.1 us (5%)
  matrix products  2.62 us (4%)
  Pallas kernels  2.33 us (4%)
  other arithmetic  2.07 us (3%)
    all_to_all x1, blocking collectives, on_device(): got = lax.all_to_all(send, AXES, 0, 0, tiled=True)  40.9 us
    all_to_all x1, blocking collectives, on_device(): returned = lax.all_to_all(wide, AXES, 0, 0, tiled=True)[:, :CHUNK]  13.5 us
    dot_general x1, matrix products, on_device(): lax.dot_general(got_rows, got_rows, (((1,), (1,)), ((), ())), preferred_e...  2.62 us
    pallas_call x1, Pallas kernels, pack(): pl.pallas_call(pack_kernel, out_shape=jax.ShapeDtypeStruct((slots, feat_w...  2.33 us
    unnamed x2, local copies, waits for them, and re-layouts  1.67 us

profile of v25, /device:TPU:0, one launch (start us, length us, event | category | flops | bytes accessed | tf_op | source)
XLA Modules:
  0.0 64.7 jit_solution(6770021802710230844)
XLA Ops:
  0.0 0.8 %concatenate.3 = s32[1160]{0:T(1024)S(1)} concatenate(s32[576]{0:T(1024)} %param.5, s32[576]{0:T(1024)} %param.6, s32[8]{0:T(128)} %bitcast.17), dimensions={0} | concatenate | bytes 9280 | tf_op jit(solution)/shard_map/concatenate | solution.py:68
  0.8 0.1 add_select_fusion
  0.9 0.1 select_reduce_fusion.2
  1.0 0.1 convert_reduce_fusion.1
  1.1 0.1 add_select_fusion.1
  1.2 0.1 add_select_fusion.4
  1.2 0.3 convert_reduce_fusion
  1.6 0.1 pad.8.clone
  1.6 0.1 pad.7.clone
  1.8 0.1 copy.18.cols_ref
  2.0 0.1 add_add_fusion.idx_ref
  2.1 0.0 copy-start
  2.1 1.7 %copy-done = f32[576,1024]{1,0:T(8,128)S(1)} copy-done((f32[576,1024]{1,0:T(8,128)S(1)}, f32[576,1024]{1,0:T(8,128)}, u32[]{:S(2)}) %copy-start) | copy-done | bytes 2359320
  3.7 2.3 %shard_map.46 = bf16[1024,1024]{1,0:T(8,128)(2,1)S(1)} custom-call(f32[576,1024]{1,0:T(8,128)S(1)} %copy-done, s32[8,576]{1,0:T(8,128)S(1)} %add_add_fusion.idx_ref, s32[576,8]{1,0:T(8,128)S(1)} %copy.18.cols_ref), custom_call_target="tpu_custom_call" | custom-call | tf_op jit(solution)/shard_map/pallas_call | solution.py:53
  6.1 40.9 %all_to_all.17 = bf16[128,8,1024]{2,1,0:T(8,128)(2,1)S(1)} all-to-all(bf16[128,8,1024]{2,1,0:T(8,128)(2,1)S(1)} %bitcast.13), channel_id=1, replica_groups=mesh['group'=8,'blk'=16] {'group','blk'}, dimensions={0} | all-to-all | bytes 4194304 | tf_op jit(solution)/shard_map/all_to_all | solution.py:90
  47.0 0.1 slice_convert_fusion
  47.1 0.1 fusion.7
  47.2 0.1 reshape.113
  47.3 2.6 %select_reduce_fusion = f32[1024]{0:T(1024)S(1)} fusion(bf16[128,8,1024]{2,1,0:T(8,128)(2,1)S(1)} %all_to_all.17, s32[1024]{0:T(1024)S(1)} %broadcast_and_fusion, s32[1024]{0:T(1024)S(1)} %reshape.113), kind=kOutput, calls=%fused_computation.2 | convolution fusion | flops 2153774080 | bytes 2109440 | tf_op jit(solution)/shard_map/dot_general | solution.py:101
  50.0 0.1 reshape.110
  50.1 13.5 %all_to_all.18 = f32[128,1,128]{2,1,0:T(1,128)S(1)} all-to-all(f32[128,1,128]{2,1,0:T(1,128)S(1)} %bitcast.15), channel_id=1, replica_groups=mesh['group'=8,'blk'=16] {'group','blk'}, dimensions={0} | all-to-all | bytes 131072 | tf_op jit(solution)/shard_map/all_to_all | solution.py:110
  63.6 0.1 broadcast_in_dim.55
  63.7 1.0 %select_reduce_fusion.1 = f32[576]{0:T(1024)} fusion(f32[1024]{0:T(1024)S(1)} %broadcast_in_dim.55, s32[576]{0:T(1024)S(1)} %multiply_add_fusion.1), kind=kLoop, calls=%fused_computation.4 | loop fusion | flops 1768896 | bytes 8704 | tf_op jit(solution)/shard_map/reduce_sum | solution.py:111
  (17 shorter events, 0.1 us)
Async XLA Ops:
  2.1 1.7 %copy-start = (f32[576,1024]{1,0:T(8,128)S(1)}, f32[576,1024]{1,0:T(8,128)}, u32[]{:S(2)}) copy-start(f32[576,1024]{1,0:T(8,128)} %x_ref.1) | copy-start | bytes 7077892
